TPU v7x, 512 devices: a whole 4x4x16 slice. The times are simulated.
512 devices in a mesh: req: 128 (over x, z, core), head: 4 (over y).
Axes of the slice: x: 4, y: 4, z: 16, core: 2. Of those that a mesh axis runs over, the one named last changes fastest.
Arguments:
- queries: bfloat16 [128, 16, 2048], P('req', None, 'head'), may hold values from -6 to 6
- forget_logits: bfloat16 [128, 16, 2048], P('req', None, 'head'), may hold values from -8 to 8
- values: bfloat16 [128, 16, 2048], P('req', None, 'head'), may hold values from -6 to 6
- gate_input: bfloat16 [128, 16, 2048], P('req', None, 'head'), may hold values from -6 to 6
- init_states: float32 [128, 16, 128, 128], P('req', 'head'), may hold values from -4 to 4
- norm_gain: float32 [128], replicated, may hold values from 0.1 to 1.9
- out_weight: bfloat16 [2048, 2048], P('head'), may hold values from -0.125 to 0.125
- dealing: int32 [128], P('req'), may hold values from 0 to 127, as said below
- accepted: int32 [128], P('req'), may hold values from 0 to 16, as said below
Outputs:
- verified: bfloat16 [128, 16, 2048], P('req', None, 'head')
- new_states: float32 [128, 16, 128, 128], P('req', 'head')
Inputs may be any that keep to these rules, and one draw needn't show every extreme that they name: `dealing`: each request appears in exactly one dealt slot. `accepted`: some request accepts all 16 draft tokens and some accepts none.
All inputs are finite; a program needn't handle non-finite values.
Results may differ from a plain program's by a relative error of at most 0.0049.
Values may be sent and summed in bfloat16 or wider, within the bound.
No kernel may reach another device: no remote copies, remote signals or barrier semaphores. Data moves between devices by JAX's collectives and lax.ppermute only.
A program may use at most 64 MiB of HBM per device.

v0:
```python
import jax
import jax.numpy as jnp
from jax import lax
from jax.sharding import PartitionSpec as P

lower_bound = 0.8
norm_eps = 1e-05


def route_gathered(token_tuple, deal_all, worker, local_count):
    mine = worker * local_count + jnp.arange(local_count, dtype=jnp.int32)
    shard_rows = (
        lax.all_gather(token_tuple[0], "req", axis=0, tiled=True),
        lax.all_gather(token_tuple[1], "req", axis=0, tiled=True),
        lax.all_gather(token_tuple[2], "req", axis=0, tiled=True),
        lax.all_gather(token_tuple[3], "req", axis=0, tiled=True),
    )
    match = (deal_all[None, :] == mine[:, None]).astype(jnp.bfloat16)
    totals = tuple(
        (
            jnp.einsum("rk,kte->rte", match, rows, preferred_element_type=jnp.float32)
            for rows in shard_rows
        )
    )
    return tuple((acc.astype(jnp.bfloat16) for acc in totals))


def per_device(
    queries,
    forget_logits,
    values,
    gate_input,
    init_states,
    norm_gain,
    out_weight,
    dealing,
    accepted,
):
    local_count = queries.shape[0]
    draft_len = queries.shape[1]
    head_local = init_states.shape[1]
    head_size = init_states.shape[3]
    deal_all = lax.all_gather(dealing, "req", axis=0, tiled=True)
    worker = lax.axis_index("req")
    token_tuple = (queries, forget_logits, values, gate_input)
    tokens_q, tokens_f, tokens_v, tokens_g = route_gathered(
        token_tuple, deal_all, worker, local_count
    )

    def heads_of(tensor):
        return jnp.moveaxis(
            tensor.astype(jnp.float32).reshape(local_count, draft_len, head_local, head_size), 1, 0
        )

    query_seq = heads_of(tokens_q)
    forget_seq = lower_bound + (1.0 - lower_bound) * jax.nn.sigmoid(heads_of(tokens_f))
    value_seq = heads_of(tokens_v)
    numbers = jnp.arange(1, draft_len + 1, dtype=jnp.int32)

    def advance(state_pair, inputs):
        current, chosen = state_pair
        query_now, forget_now, value_now, number = inputs
        current = (
            forget_now[..., None] * current
            + (1.0 - forget_now)[..., None] * value_now[..., None, :]
        )
        chosen = jnp.where((accepted == number)[:, None, None, None], current, chosen)
        output = jnp.einsum("rhk,rhkv->rhv", query_now, current, precision=lax.Precision.HIGHEST)
        return ((current, chosen), output)

    (last_state, new_states), outputs = lax.scan(
        advance, (init_states, init_states), (query_seq, forget_seq, value_seq, numbers)
    )
    outputs = jnp.moveaxis(outputs, 0, 1)
    meansq = jnp.mean(outputs * outputs, axis=-1, keepdims=True)
    gate_heads = tokens_g.astype(jnp.float32).reshape(local_count, draft_len, head_local, head_size)
    mixed_rows = (
        outputs * lax.rsqrt(meansq + norm_eps) * norm_gain * jax.nn.silu(gate_heads)
    ).astype(jnp.bfloat16)
    mixed_rows = mixed_rows.reshape(local_count * draft_len, head_local * head_size)
    partial_out = jnp.dot(mixed_rows, out_weight, preferred_element_type=jnp.float32)
    summed = lax.psum_scatter(partial_out, "head", scatter_dimension=1, tiled=True)
    verified = summed.astype(jnp.bfloat16).reshape(local_count, draft_len, summed.shape[1])
    return (verified, new_states)


def solution(mesh):
    placed = (
        P("req", None, "head"),
        P("req", None, "head"),
        P("req", None, "head"),
        P("req", None, "head"),
        P("req", "head", None, None),
        P(),
        P("head", None),
        P("req"),
        P("req"),
    )
    return jax.shard_map(
        per_device,
        mesh=mesh,
        in_specs=placed,
        out_specs=(P("req", None, "head"), P("req", "head", None, None)),
        check_vma=False,
    )
```

profile of v0, /device:TPU:6, one launch (start us, length us, event | category | flops | bytes accessed | tf_op | source)
XLA Modules:
  0.0 614.5 jit_solution(16999576388277183235)
XLA Ops:
  7.2 1.1 copy.69
  8.4 0.7 all-gather.9.cloned.1.call-update
  9.1 0.7 all-gather.5.cloned.1.call-update
  9.9 0.5 all-gather.11.cloned.1.call-update
  11.1 1.3 dynamic-slice
  12.4 0.8 dynamic-update-slice
  13.2 32.1 %all-reduce = s32[128]{0:T(128)S(1)} all-reduce(s32[128]{0:T(128)S(1)} %dynamic-update-slice), channel_id=1, replica_groups=mesh['req'=128,'head'=4] {'req'}, use_global_device_ids=true, to_apply=%add | all-reduce | flops 128 | bytes 1024
  45.3 0.7 broadcast_bitcast_fusion
  45.9 109.4 %all-gather.7.cloned.1.call-done = bf16[128,16,512]{2,1,0:T(8,128)(2,1)} async-done(((bf16[1,16,512]{2,1,0:T(8,128)(2,1)}), bf16[128,16,512]{2,1,0:T(8,128)(2,1)}) %all-gather.7.cloned.1.call-update) | async-done | bytes 2097168 | tf_op jit(solution)/shard_map/all_gather | solution.py:15
  155.3 3.9 fusion.6
  159.2 136.3 %all-gather.9.cloned.1.call-done = bf16[128,16,512]{2,1,0:T(8,128)(2,1)} async-done(((bf16[1,16,512]{2,1,0:T(8,128)(2,1)}), bf16[128,16,512]{2,1,0:T(8,128)(2,1)}) %all-gather.9.cloned.1.call-update) | async-done | bytes 2097168 | tf_op jit(solution)/shard_map/all_gather | solution.py:13
  295.5 3.9 fusion.4
  299.4 136.3 %all-gather.5.cloned.1.call-done = bf16[128,16,512]{2,1,0:T(8,128)(2,1)} async-done(((bf16[1,16,512]{2,1,0:T(8,128)(2,1)}), bf16[128,16,512]{2,1,0:T(8,128)(2,1)}) %all-gather.5.cloned.1.call-update) | async-done | bytes 2097168 | tf_op jit(solution)/shard_map/all_gather | solution.py:14
  435.7 3.9 fusion.8
  439.7 40.8 %while.14 = (s32[]{:T(128)}, f32[1,4,128,128]{3,2,1,0:T(8,128)S(1)}, f32[1,4,128,128]{3,2,1,0:T(8,128)S(1)}, f32[16,1,4,128]{3,2,1,0:T(4,128)S(1)}, f32[16,1,4,1...) while((s32[]{:T(128)}, ...), condition=%wide.region_1.2_spmd, body=%wide.region_0.1_spmd.sunk | while | flops 1049091 | bytes 1339531 | solution.py:71
  439.7 0.6 dynamic_slice.23
  441.9 0.3 fusion.34
  442.2 0.6 dynamic_slice.23
  444.5 0.3 fusion.34
  444.8 0.6 dynamic_slice.23
  447.0 0.3 fusion.34
  447.3 0.6 dynamic_slice.23
  449.5 0.3 fusion.34
  449.9 0.6 dynamic_slice.23
  452.4 0.6 dynamic_slice.23
  454.6 0.3 fusion.34
  455.0 0.6 dynamic_slice.23
  457.2 0.3 fusion.34
  457.5 0.6 dynamic_slice.23
  459.7 0.3 fusion.34
  460.1 0.6 dynamic_slice.23
  462.3 0.3 fusion.34
  462.6 0.6 dynamic_slice.23
  465.2 0.6 dynamic_slice.23
  467.4 0.3 fusion.34
  467.7 0.6 dynamic_slice.23
  470.3 0.6 dynamic_slice.23
  472.5 0.3 fusion.34
  472.8 0.6 dynamic_slice.23
  475.0 0.3 fusion.34
  475.4 0.6 dynamic_slice.23
  477.6 0.3 fusion.34
  477.9 0.6 dynamic_slice.23
  480.6 95.3 %all-gather.11.cloned.1.call-done = bf16[128,16,512]{2,1,0:T(8,128)(2,1)} async-done(((bf16[1,16,512]{2,1,0:T(8,128)(2,1)}), bf16[128,16,512]{2,1,0:T(8,128)(2,1)}) %all-gather.11.cloned.1.call-update) | async-done | bytes 2097168 | tf_op jit(solution)/shard_map/all_gather | solution.py:16
  575.9 3.9 fusion.2
  579.8 1.0 fusion.16
  580.9 25.8 %reduce-scatter.2.cloned.1.call-done = f32[16,512]{1,0:T(8,128)} async-done(((f32[16,2048]{1,0:T(8,128)}), f32[16,512]{1,0:T(8,128)}) %reduce-scatter.2.cloned.1.call-update) | async-done | bytes 32784 | tf_op jit(solution)/shard_map/reduce_scatter | solution.py:82
  606.7 1.4 convert_bitcast_fusion
  (108 shorter events, 6.8 us)
Async XLA Ops:
  7.2 572.7 %copy-start = (bf16[512,2048]{1,0:T(8,128)(2,1)S(1)}, bf16[512,2048]{1,0:T(8,128)(2,1)}, u32[]{:S(2)}) copy-start(bf16[512,2048]{1,0:T(8,128)(2,1)} %param.17) | copy-start | bytes 6291460
  7.2 148.1 %all-gather.7.cloned.1.call-start = ((), (), s32[]{:S(2)}) async-start(), calls=%async_computation.2 | async-start | bytes 2113536 | tf_op jit(solution)/shard_map/all_gather | solution.py:15
  8.3 287.2 %all-gather.9.cloned.1.call-start = ((), (), s32[]{:S(2)}) async-start(), calls=%async_computation.3 | async-start | bytes 2113536 | tf_op jit(solution)/shard_map/all_gather | solution.py:13
  9.1 426.6 %all-gather.5.cloned.1.call-start = ((), (), s32[]{:S(2)}) async-start(), calls=%async_computation.1 | async-start | bytes 2113536 | tf_op jit(solution)/shard_map/all_gather | solution.py:14
  9.8 566.0 %all-gather.11.cloned.1.call-start = ((), (), s32[]{:S(2)}) async-start(), calls=%async_computation.4 | async-start | bytes 2113536 | tf_op jit(solution)/shard_map/all_gather | solution.py:16
  10.4 596.2 %reduce-scatter.2.cloned.1.call-start = ((), (), s32[]{:S(2)}) async-start(), calls=%async_computation.5 | async-start | bytes 163840 | tf_op jit(solution)/shard_map/reduce_scatter | solution.py:82
  480.4 100.4 %copy-start.1 = (f32[1,4,128,128]{3,2,1,0:T(8,128)}, f32[1,4,128,128]{3,2,1,0:T(8,128)S(1)}, u32[]{:S(2)}) copy-start(f32[1,4,128,128]{3,2,1,0:T(8,128)S(1)} %get-tuple-element.49) | copy-start | bytes 786436
Sparse Core Ops, SparseCore 0:
  11.1 144.1 all-gather.6
  158.5 137.0 all-gather.8
  298.7 137.0 all-gather.4
  438.7 137.0 all-gather.10
  581.0 25.5 reduce-scatter.1
where the time goes:
time: 615 us
  waiting for transfers between devices  505 us (82%)
  blocking collectives  32.1 us (5%)
  matrix products  21.6 us (4%)
  loops' own time  21.3 us (3%)
  between operations  14.5 us (2%)
  local copies, waits for them, and re-layouts  13.8 us (2%)
    all_gather x1, waiting for transfers between devices, route_gathered(): lax.all_gather(token_tuple[1], 'req', axis=0, tiled=True)  136 us
    all_gather x1, waiting for transfers between devices, route_gathered(): lax.all_gather(token_tuple[0], 'req', axis=0, tiled=True)  136 us
    all_gather x1, waiting for transfers between devices, route_gathered(): lax.all_gather(token_tuple[2], 'req', axis=0, tiled=True)  109 us
    all_gather x1, waiting for transfers between devices, route_gathered(): lax.all_gather(token_tuple[3], 'req', axis=0, tiled=True)  95.3 us
    unnamed x1, blocking collectives  32.1 us
    reduce_scatter x1, waiting for transfers between devices, per_device(): lax.psum_scatter(partial_out, 'head', scatter_dimension=1, tiled=True)  25.8 us
    another operation x1, loops' own time, per_device(): lax.scan(advance, (init_states, init_states), (query_seq, forget_seq, val...  21.3 us
    dot_general x4, matrix products, route_gathered(): jnp.einsum('rk,kte->rte', match, rows, preferred_element_type=jnp.float32)  15.5 us
  transfers between devices with their start and end apart: 5, of which 5 were waited for; matrix products, arithmetic and copies ran while one was open for 6% of the time, Pallas kernels for 0%

commit v1 on v0

v1 whole, which is shorter than its diff:
```python
import jax
import jax.numpy as jnp
from jax import lax
from jax.sharding import Mesh, PartitionSpec as P

lower_bound = 0.8
norm_eps = 1e-05

ROW = ("x", "c")
REQ = ("x", "z", "c")


def route_two_stage(token_tuple, dealing):
    rows = jnp.concatenate([t[0] for t in token_tuple], axis=0)
    width = rows.shape[1]
    dest_row = jnp.broadcast_to(dealing.astype(jnp.bfloat16).reshape(1, 1), (1, width))
    payload = jnp.concatenate([rows, dest_row], axis=0)
    gathered = lax.all_gather(payload, ROW, axis=0, tiled=False)
    dest = gathered[:, -1, 0].astype(jnp.int32)
    body = gathered[:, :-1, :]
    zn = lax.axis_size("z")
    my_x = lax.axis_index("x")
    my_c = lax.axis_index("c")
    cn = lax.axis_size("c")
    target = (my_x * zn + jnp.arange(zn, dtype=jnp.int32)) * cn + my_c
    match = (target[:, None] == dest[None, :]).astype(jnp.bfloat16)
    send = jnp.einsum("zk,kre->zre", match, body, preferred_element_type=jnp.float32).astype(jnp.bfloat16)
    got = lax.all_to_all(send, "z", 0, 0, tiled=False)
    mine = jnp.sum(got.astype(jnp.float32), axis=0).astype(jnp.bfloat16)
    n = len(token_tuple)
    per = mine.shape[0] // n
    return tuple(mine[i * per:(i + 1) * per][None] for i in range(n))


def per_device(
    queries,
    forget_logits,
    values,
    gate_input,
    init_states,
    norm_gain,
    out_weight,
    dealing,
    accepted,
):
    local_count = queries.shape[0]
    draft_len = queries.shape[1]
    head_local = init_states.shape[1]
    head_size = init_states.shape[3]
    token_tuple = (queries, forget_logits, values, gate_input)
    tokens_q, tokens_f, tokens_v, tokens_g = route_two_stage(token_tuple, dealing)

    def heads_of(tensor):
        return jnp.moveaxis(
            tensor.astype(jnp.float32).reshape(local_count, draft_len, head_local, head_size), 1, 0
        )

    query_seq = heads_of(tokens_q)
    forget_seq = lower_bound + (1.0 - lower_bound) * jax.nn.sigmoid(heads_of(tokens_f))
    value_seq = heads_of(tokens_v)
    numbers = jnp.arange(1, draft_len + 1, dtype=jnp.int32)

    def advance(state_pair, inputs):
        current, chosen = state_pair
        query_now, forget_now, value_now, number = inputs
        current = (
            forget_now[..., None] * current
            + (1.0 - forget_now)[..., None] * value_now[..., None, :]
        )
        chosen = jnp.where((accepted == number)[:, None, None, None], current, chosen)
        output = jnp.einsum("rhk,rhkv->rhv", query_now, current, precision=lax.Precision.HIGHEST)
        return ((current, chosen), output)

    (last_state, new_states), outputs = lax.scan(
        advance, (init_states, init_states), (query_seq, forget_seq, value_seq, numbers)
    )
    outputs = jnp.moveaxis(outputs, 0, 1)
    meansq = jnp.mean(outputs * outputs, axis=-1, keepdims=True)
    gate_heads = tokens_g.astype(jnp.float32).reshape(local_count, draft_len, head_local, head_size)
    mixed_rows = (
        outputs * lax.rsqrt(meansq + norm_eps) * norm_gain * jax.nn.silu(gate_heads)
    ).astype(jnp.bfloat16)
    mixed_rows = mixed_rows.reshape(local_count * draft_len, head_local * head_size)
    partial_out = jnp.dot(mixed_rows, out_weight, preferred_element_type=jnp.float32)
    hn = lax.axis_size("head")
    rows = partial_out.shape[0]
    split = partial_out.reshape(rows, hn, partial_out.shape[1] // hn)
    swapped = lax.all_to_all(split, "head", 1, 1, tiled=True)
    summed = jnp.sum(swapped, axis=1)
    verified = summed.astype(jnp.bfloat16).reshape(local_count, draft_len, summed.shape[1])
    return (verified, new_states)


def solution(mesh):
    xs, zs, cs = 4, mesh.shape["req"] // 8, 2
    sub = Mesh(mesh.devices.reshape(xs, zs, cs, mesh.shape["head"]), ("x", "z", "c", "head"))
    placed = (
        P(REQ, None, "head"),
        P(REQ, None, "head"),
        P(REQ, None, "head"),
        P(REQ, None, "head"),
        P(REQ, "head", None, None),
        P(),
        P("head", None),
        P(REQ),
        P(REQ),
    )
    return jax.shard_map(
        per_device,
        mesh=sub,
        in_specs=placed,
        out_specs=(P(REQ, None, "head"), P(REQ, "head", None, None)),
        check_vma=False,
    )
```

time: 615 us -> 142 us (0.23)
  waiting for transfers between devices: 505 us -> 47.6 us
  matrix products: 21.6 us -> 6.28 us
  between operations: 14.5 us -> 1.43 us
  starting transfers between devices: 0.19 us -> 12.4 us
    all_gather x4 -> x0, waiting for transfers between devices: 477 us -> none  [the longest x1 136 us: route_gathered(): lax.all_gather(token_tuple[1], 'req', axis=0, tiled=True)]
    all_to_all x0 -> x1, waiting for transfers between devices: none -> 47.6 us  [route_two_stage(): got = lax.all_to_all(send, 'z', 0, 0, tiled=False)]
    unnamed x1 -> x0, blocking collectives: 32.1 us -> none
    reduce_scatter x1 -> x0, waiting for transfers between devices: 25.8 us -> none  [per_device(): lax.psum_scatter(partial_out, 'head', scatter_dimension=1, tiled=True)]
    all_gather x0 -> x1, blocking collectives: none -> 16 us  [route_two_stage(): gathered = lax.all_gather(payload, ROW, axis=0, tiled=False)]
    dot_general x4 -> x1, matrix products: 15.5 us -> 0.57 us  [route_two_stage(): jnp.einsum('zk,kre->zre', match, body, preferred_element_type=jnp.float32)]
    all_to_all x0 -> x1, starting transfers between devices: none -> 12.4 us  [route_two_stage(): got = lax.all_to_all(send, 'z', 0, 0, tiled=False)]
    all_to_all x0 -> x1, blocking collectives: none -> 10.2 us  [per_device(): swapped = lax.all_to_all(split, 'head', 1, 1, tiled=True)]
  transfers between devices with their start and end apart: 5 -> 1, of which waited for: 5 -> 1; matrix products, arithmetic and copies ran while one was open for 6% -> 2% of each run, Pallas kernels for 0% -> 0%
where the time goes in v1:
time: 142 us; the launch traced here: 141 us
  waiting for transfers between devices  47.6 us (34%)
  blocking collectives  26.3 us (19%)
  loops' own time  21.3 us (15%)
  local copies, waits for them, and re-layouts  18.4 us (13%)
  starting transfers between devices  12.4 us (9%)
  other arithmetic  7 us (5%)
  matrix products  6.28 us (4%)
  between operations  1.43 us (1%)
    all_to_all x1, waiting for transfers between devices, route_two_stage(): got = lax.all_to_all(send, 'z', 0, 0, tiled=False)  47.6 us
    another operation x1, loops' own time, per_device(): lax.scan(advance, (init_states, init_states), (query_seq, forget_seq, val...  21.3 us
    all_gather x1, blocking collectives, route_two_stage(): gathered = lax.all_gather(payload, ROW, axis=0, tiled=False)  16 us
    all_to_all x1, starting transfers between devices, route_two_stage(): got = lax.all_to_all(send, 'z', 0, 0, tiled=False)  12.4 us
    all_to_all x1, blocking collectives, per_device(): swapped = lax.all_to_all(split, 'head', 1, 1, tiled=True)  10.2 us
    dynamic_slice x32, local copies, waits for them, and re-layouts, per_device(): lax.scan(advance, (init_states, init_states), (query_seq, forget_seq, val...  9.58 us
    dot_general x16, matrix products, advance(): jnp.einsum('rhk,rhkv->rhv', query_now, current, precision=lax.Precision.H...  5.06 us
    select_n x16, other arithmetic, advance(): jnp.where((accepted == number)[:, None, None, None], current, chosen)  4.48 us
  transfers between devices with their start and end apart: 1, of which 1 were waited for; matrix products, arithmetic and copies ran while one was open for 2% of the time, Pallas kernels for 0%

profile of v1, /device:TPU:6, one launch (start us, length us, event | category | flops | bytes accessed | tf_op | source)
XLA Modules:
  0.0 140.6 jit_solution(2282585019202053629)
XLA Ops:
  0.6 1.0 copy.43
  1.6 0.7 bitcast_dynamic-update-slice_fusion.3
  3.0 0.7 bitcast_dynamic-update-slice_fusion.2
  3.7 0.7 bitcast_dynamic-update-slice_fusion.1
  4.4 0.7 bitcast_dynamic-update-slice_fusion
  5.1 16.0 %all-gather.1 = bf16[8,65,512]{2,1,0:T(8,128)(2,1)S(1)} all-gather(bf16[1,65,512]{2,1,0:T(8,128)(2,1)S(1)} %bitcast.55), channel_id=2, replica_groups=mesh['x'=4,'z'=16,'c'=2,'head'=4] {'x','c'}, dimensions={0}, use_global_device_ids=true | all-gather | bytes 599040 | tf_op jit(solution)/shard_map/all_gather | solution.py:18
  21.5 0.6 convolution_convert_fusion
  22.1 1.6 %copy.15 = bf16[16,64,512]{2,1,0:T(8,128)(2,1)} copy(bf16[16,64,512]{2,0,1:T(8,128)(2,1)S(1)} %convolution_convert_fusion) | data formatting | bytes 2097152 | tf_op jit(solution)/shard_map/convert_element_type | solution.py:27
  23.7 12.4 %all-to-all-start = ((bf16[16,64,512]{2,1,0:T(8,128)(2,1)}), bf16[16,64,512]{2,1,0:T(8,128)(2,1)}, u32[]{:S(2)}, u32[]{:S(2)}) async-start(bf16[16,64,512]{2,1,0:T(8,128)(2,1)} %copy.15), calls=%async_computation | async-start | bytes 2097152 | tf_op jit(solution)/shard_map/all_to_all | solution.py:28
  36.1 2.9 %copy.19 = bf16[2048,512]{1,0:T(8,128)(2,1)S(1)} copy(bf16[2048,512]{0,1:T(8,128)(2,1)} %bitcast.52) | data formatting | bytes 4194304 | tf_op jit(solution)/shard_map/dot_general | solution.py:84
  39.0 47.6 %all-to-all-done = bf16[16,64,512]{2,1,0:T(8,128)(2,1)} async-done(((bf16[16,64,512]{2,1,0:T(8,128)(2,1)}), bf16[16,64,512]{2,1,0:T(8,128)(2,1)}, u32[]{:S(2)}, u32[]{:S(2)}) %all-to-all-start) | async-done | bytes 1048608 | tf_op jit(solution)/shard_map/all_to_all | solution.py:28
  86.6 1.4 reduce_sum.30
  88.1 40.8 %while.14 = (s32[]{:T(128)}, f32[1,4,128,128]{3,2,1,0:T(8,128)S(1)}, f32[1,4,128,128]{3,2,1,0:T(8,128)S(1)}, f32[16,1,4,128]{3,2,1,0:T(4,128)S(1)}, f32[16,1,4,1...) while((s32[]{:T(128)}, ...), condition=%wide.region_2.3_spmd, body=%wide.region_1.2_spmd.sunk | while | flops 1049091 | bytes 1339531 | solution.py:74
  88.1 0.6 dynamic_slice.23
  90.3 0.3 fusion.19
  90.6 0.6 dynamic_slice.23
  92.9 0.3 fusion.19
  93.2 0.6 dynamic_slice.23
  95.4 0.3 fusion.19
  95.7 0.6 dynamic_slice.23
  97.9 0.3 fusion.19
  98.3 0.6 dynamic_slice.23
  100.5 0.3 fusion.19
  100.8 0.6 dynamic_slice.23
  103.0 0.3 fusion.19
  103.4 0.6 dynamic_slice.23
  105.6 0.3 fusion.19
  105.9 0.6 dynamic_slice.23
  108.1 0.3 fusion.19
  108.5 0.6 dynamic_slice.23
  110.7 0.3 fusion.19
  111.0 0.6 dynamic_slice.23
  113.2 0.3 fusion.19
  113.6 0.6 dynamic_slice.23
  115.8 0.3 fusion.19
  116.1 0.6 dynamic_slice.23
  118.3 0.3 fusion.19
  118.7 0.6 dynamic_slice.23
  120.9 0.3 fusion.19
  121.2 0.6 dynamic_slice.23
  123.4 0.3 fusion.19
  123.8 0.6 dynamic_slice.23
  126.0 0.3 fusion.19
  126.3 0.6 dynamic_slice.23
  128.5 0.3 fusion.19
  129.1 0.6 fusion.10
  129.8 10.2 %all_to_all.10 = f32[16,4,512]{2,0,1:T(8,128)S(1)} all-to-all(f32[16,4,512]{2,0,1:T(8,128)S(1)} %fusion.10), channel_id=1, replica_groups=mesh['x'=4,'z'=16,'c'=2,'head'=4] {'head'}, dimensions={1} | all-to-all | bytes 262144 | tf_op jit(solution)/shard_map/all_to_all | solution.py:88
  140.0 0.6 reduce_sum.32
  (101 shorter events, 5.7 us)
Async XLA Ops:
  23.7 62.9 %all-to-all-start = ((bf16[16,64,512]{2,1,0:T(8,128)(2,1)}), bf16[16,64,512]{2,1,0:T(8,128)(2,1)}, u32[]{:S(2)}, u32[]{:S(2)}) async-start(bf16[16,64,512]{2,1,0:T(8,128)(2,1)} %copy.15), calls=%async_computation | async-start | bytes 2097152 | tf_op jit(solution)/shard_map/all_to_all | solution.py:28
  88.1 40.9 %copy-start.1 = (f32[128]{0:T(128)S(1)}, f32[128]{0:T(128)}, u32[]{:S(2)}) copy-start(f32[128]{0:T(128)} %param.16) | copy-start | bytes 1540
  128.8 11.8 %copy-start = (f32[1,4,128,128]{3,2,1,0:T(8,128)}, f32[1,4,128,128]{3,2,1,0:T(8,128)S(1)}, u32[]{:S(2)}) copy-start(f32[1,4,128,128]{3,2,1,0:T(8,128)S(1)} %get-tuple-element.49) | copy-start | bytes 786436

commit v2 on v1

v2 whole, which is shorter than its diff:
```python
import jax
import jax.numpy as jnp
from jax import lax
from jax.experimental import pallas as pl
from jax.experimental.pallas import tpu as pltpu
from jax.sharding import Mesh, PartitionSpec as P

lower_bound = 0.8
norm_eps = 1e-05

ROW = ("x", "c")
REQ = ("x", "z", "c")


HI = lax.Precision.HIGHEST


def _dot(a, b):
    return jnp.dot(a, b, precision=HI, preferred_element_type=jnp.float32)


def mixer_kernel(acc_ref, tok_ref, s0_ref, gain_ref, new_ref, mixed_ref):
    acc = acc_ref[0]
    tok = tok_ref[...].astype(jnp.float32)
    t_len = tok.shape[0] // 4
    heads = s0_ref.shape[0]
    hd = s0_ref.shape[2]
    q = tok[0:t_len]
    fl = tok[t_len:2 * t_len]
    v = tok[2 * t_len:3 * t_len]
    g = tok[3 * t_len:4 * t_len]
    a = lower_bound + (1.0 - lower_bound) * (1.0 / (1.0 + jnp.exp(-fl)))
    b = 1.0 - a
    la = jnp.log(a)
    row = lax.broadcasted_iota(jnp.int32, (t_len, t_len), 0)
    col = lax.broadcasted_iota(jnp.int32, (t_len, t_len), 1)
    causal = (col <= row).astype(jnp.float32)
    lc = _dot(causal, la)
    big_a = jnp.exp(lc)
    inv_a = jnp.exp(-lc)
    qa = q * big_a
    ba = b * inv_a
    kept = (lax.broadcasted_iota(jnp.int32, la.shape, 0) < acc).astype(jnp.float32)
    a_acc = jnp.exp(jnp.sum(kept * la, axis=0, keepdims=True))
    w = kept * a_acc * ba
    eye_r = lax.broadcasted_iota(jnp.int32, (hd, hd), 0)
    eye_c = lax.broadcasted_iota(jnp.int32, (hd, hd), 1)
    eye = (eye_r == eye_c).astype(jnp.float32)
    gain = gain_ref[...]
    silu_g = g * (1.0 / (1.0 + jnp.exp(-g)))
    for h in range(heads):
        lanes = slice(h * hd, (h + 1) * hd)
        s0 = s0_ref[h]
        v_h = v[:, lanes]
        qa_h = qa[:, lanes]
        scores = lax.dot_general(qa_h, ba[:, lanes], (((1,), (1,)), ((), ())),
                                 precision=HI, preferred_element_type=jnp.float32)
        o_h = _dot(qa_h, s0) + _dot(scores * causal, v_h)
        diag = eye * a_acc[:, lanes]
        new_ref[h] = _dot(diag, s0) + _dot(jnp.transpose(w[:, lanes]), v_h)
        meansq = jnp.mean(o_h * o_h, axis=-1, keepdims=True)
        mixed = o_h * lax.rsqrt(meansq + norm_eps) * gain * silu_g[:, lanes]
        mixed_ref[:, lanes] = mixed.astype(mixed_ref.dtype)


def mixer(acc, tok, s0, gain):
    heads, hd = s0.shape[0], s0.shape[2]
    t_len = tok.shape[0] // 4
    vmem = pl.BlockSpec(memory_space=pltpu.VMEM)
    return pl.pallas_call(
        mixer_kernel,
        out_shape=(jax.ShapeDtypeStruct(s0.shape, jnp.float32),
                   jax.ShapeDtypeStruct((t_len, heads * hd), jnp.bfloat16)),
        in_specs=[pl.BlockSpec(memory_space=pltpu.SMEM), vmem, vmem, vmem],
        out_specs=(vmem, vmem),
    )(acc, tok, s0, gain)


def route_two_stage(token_tuple, dealing):
    rows = jnp.concatenate([t[0] for t in token_tuple], axis=0)
    width = rows.shape[1]
    dest_row = jnp.broadcast_to(dealing.astype(jnp.bfloat16).reshape(1, 1), (1, width))
    payload = jnp.concatenate([rows, dest_row], axis=0)
    gathered = lax.all_gather(payload, ROW, axis=0, tiled=False)
    dest = gathered[:, -1, 0].astype(jnp.int32)
    body = gathered[:, :-1, :]
    zn = lax.axis_size("z")
    my_x = lax.axis_index("x")
    my_c = lax.axis_index("c")
    cn = lax.axis_size("c")
    target = (my_x * zn + jnp.arange(zn, dtype=jnp.int32)) * cn + my_c
    match = (target[:, None] == dest[None, :]).astype(jnp.bfloat16)
    send = jnp.einsum("zk,kre->zre", match, body, preferred_element_type=jnp.float32).astype(jnp.bfloat16)
    got = lax.all_to_all(send, "z", 0, 0, tiled=False)
    mine = jnp.sum(got.astype(jnp.float32), axis=0).astype(jnp.bfloat16)
    return mine


def per_device(
    queries,
    forget_logits,
    values,
    gate_input,
    init_states,
    norm_gain,
    out_weight,
    dealing,
    accepted,
):
    local_count = queries.shape[0]
    draft_len = queries.shape[1]
    head_local = init_states.shape[1]
    head_size = init_states.shape[3]
    token_tuple = (queries, forget_logits, values, gate_input)
    mine = route_two_stage(token_tuple, dealing)
    new_states, mixed_rows = mixer(accepted, mine, init_states[0], norm_gain.reshape(1, head_size))
    new_states = new_states[None]

    mixed_rows = mixed_rows.reshape(local_count * draft_len, head_local * head_size)
    partial_out = jnp.dot(mixed_rows, out_weight, preferred_element_type=jnp.float32)
    hn = lax.axis_size("head")
    rows = partial_out.shape[0]
    split = partial_out.reshape(rows, hn, partial_out.shape[1] // hn)
    swapped = lax.all_to_all(split, "head", 1, 1, tiled=True)
    summed = jnp.sum(swapped, axis=1)
    verified = summed.astype(jnp.bfloat16).reshape(local_count, draft_len, summed.shape[1])
    return (verified, new_states)


def solution(mesh):
    xs, zs, cs = 4, mesh.shape["req"] // 8, 2
    sub = Mesh(mesh.devices.reshape(xs, zs, cs, mesh.shape["head"]), ("x", "z", "c", "head"))
    placed = (
        P(REQ, None, "head"),
        P(REQ, None, "head"),
        P(REQ, None, "head"),
        P(REQ, None, "head"),
        P(REQ, "head", None, None),
        P(),
        P("head", None),
        P(REQ),
        P(REQ),
    )
    return jax.shard_map(
        per_device,
        mesh=sub,
        in_specs=placed,
        out_specs=(P(REQ, None, "head"), P(REQ, "head", None, None)),
        check_vma=False,
    )
```

time: 142 us -> 102 us (0.72)
  loops' own time: 21.3 us -> 0 us
  local copies, waits for them, and re-layouts: 18.4 us -> 4.66 us
  other arithmetic: 7 us -> 1.63 us
  matrix products: 6.28 us -> 1.67 us
  Pallas kernels: 0 us -> 3.1 us
  waiting for transfers between devices: 47.6 us -> 49.8 us
    another operation x1 -> x0, loops' own time: 21.3 us -> none  [per_device(): lax.scan(advance, (init_states, init_states), (query_seq, forget_seq, val...]
    dynamic_slice x32 -> x0, local copies, waits for them, and re-layouts: 9.58 us -> none  [per_device(): lax.scan(advance, (init_states, init_states), (query_seq, forget_seq, val...]
    dot_general x16 -> x0, matrix products: 5.06 us -> none  [advance(): jnp.einsum('rhk,rhkv->rhv', query_now, current, precision=lax.Precision.H...]
    select_n x16 -> x0, other arithmetic: 4.48 us -> none  [advance(): jnp.where((accepted == number)[:, None, None, None], current, chosen)]
    pallas_call x0 -> x1, Pallas kernels: none -> 3.1 us  [mixer(): pl.pallas_call(mixer_kernel, out_shape=(jax.ShapeDtypeStruct(s0.shape, jn...]
    dot_general x1 -> x0, local copies, waits for them, and re-layouts: 2.87 us -> none  [per_device(): jnp.dot(mixed_rows, out_weight, preferred_element_type=jnp.float32)]
    all_to_all x1, waiting for transfers between devices: 47.6 us -> 49.8 us  [route_two_stage(): got = lax.all_to_all(send, 'z', 0, 0, tiled=False)]
    unnamed x10 -> x6, local copies, waits for them, and re-layouts: 3.86 us -> 3.04 us
  transfers between devices with their start and end apart: 1 -> 1, of which waited for: 1 -> 1; matrix products, arithmetic and copies ran while one was open for 2% -> 0% of each run, Pallas kernels for 0% -> 0%
where the time goes in v2:
time: 102 us; the launch traced here: 101 us
  waiting for transfers between devices  49.8 us (49%)
  blocking collectives  26.3 us (26%)
  starting transfers between devices  12.3 us (12%)
  local copies, waits for them, and re-layouts  4.66 us (5%)
  Pallas kernels  3.1 us (3%)
  between operations  1.99 us (2%)
  matrix products  1.67 us (2%)
  other arithmetic  1.63 us (2%)
    all_to_all x1, waiting for transfers between devices, route_two_stage(): got = lax.all_to_all(send, 'z', 0, 0, tiled=False)  49.8 us
    all_gather x1, blocking collectives, route_two_stage(): gathered = lax.all_gather(payload, ROW, axis=0, tiled=False)  16 us
    all_to_all x1, starting transfers between devices, route_two_stage(): got = lax.all_to_all(send, 'z', 0, 0, tiled=False)  12.3 us
    all_to_all x1, blocking collectives, per_device(): swapped = lax.all_to_all(split, 'head', 1, 1, tiled=True)  10.2 us
    pallas_call x1, Pallas kernels, mixer(): pl.pallas_call(mixer_kernel, out_shape=(jax.ShapeDtypeStruct(s0.shape, jn...  3.1 us
    unnamed x6, local copies, waits for them, and re-layouts  3.04 us
  transfers between devices with their start and end apart: 1, of which 1 were waited for; matrix products, arithmetic and copies ran while one was open for 0% of the time, Pallas kernels for 0%

profile of v2, /device:TPU:6, one launch (start us, length us, event | category | flops | bytes accessed | tf_op | source)
XLA Modules:
  0.0 101.5 jit_solution(6419713119399447892)
XLA Ops:
  0.6 0.0 copy-start
  0.6 0.9 bitcast_dynamic-update-slice_fusion.3
  2.2 0.7 bitcast_dynamic-update-slice_fusion.2
  2.9 0.7 bitcast_dynamic-update-slice_fusion.1
  3.6 0.7 bitcast_dynamic-update-slice_fusion
  4.3 16.0 %all-gather.1 = bf16[8,65,512]{2,1,0:T(8,128)(2,1)S(1)} all-gather(bf16[1,65,512]{2,1,0:T(8,128)(2,1)S(1)} %bitcast.28), channel_id=2, replica_groups=mesh['x'=4,'z'=16,'c'=2,'head'=4] {'x','c'}, dimensions={0}, use_global_device_ids=true | all-gather | bytes 599040 | tf_op jit(solution)/shard_map/all_gather | solution.py:84
  20.4 0.2 fusion.1
  20.7 0.6 convolution_convert_fusion
  21.3 1.6 %copy.13 = bf16[16,64,512]{2,1,0:T(8,128)(2,1)} copy(bf16[16,64,512]{2,0,1:T(8,128)(2,1)S(1)} %convolution_convert_fusion) | data formatting | bytes 2097152 | tf_op jit(solution)/shard_map/convert_element_type | solution.py:93
  22.8 12.3 %all-to-all-start = ((bf16[16,64,512]{2,1,0:T(8,128)(2,1)}), bf16[16,64,512]{2,1,0:T(8,128)(2,1)S(1)}, u32[]{:S(2)}, u32[]{:S(2)}) async-start(bf16[16,64,512]{2,1,0:T(8,128)(2,1)} %copy.13), calls=%async_computation | async-start | bytes 2097152 | tf_op jit(solution)/shard_map/all_to_all | solution.py:94
  35.8 49.8 %all-to-all-done = bf16[16,64,512]{2,1,0:T(8,128)(2,1)S(1)} async-done(((bf16[16,64,512]{2,1,0:T(8,128)(2,1)}), bf16[16,64,512]{2,1,0:T(8,128)(2,1)S(1)}, u32[]{:S(2)}, u32[]{:S(2)}) %all-to-all-start) | async-done | bytes 1048608 | tf_op jit(solution)/shard_map/all_to_all | solution.py:94
  85.6 0.8 reduce_sum.21.tok_ref
  86.4 3.1 %shard_map.104 = (f32[4,128,128]{2,1,0:T(8,128)}, bf16[16,512]{1,0:T(8,128)(2,1)}) custom-call(s32[1]{0:T(128)S(6)} %copy.26.acc_ref, bf16[64,512]{1,0:T(8,128)(2,1)} %reduce_sum.21.tok_ref, f32[4,128,128]{2,1,0:T(8,128)} %bitcast.27, f32[1,128]{1,0:T(1,128)} %bitcast.30), custom_call_target="tpu_custom_call" | custom-call | tf_op jit(solution)/shard_map/pallas_call | solution.py:70
  89.5 0.0 copy-done
  89.5 1.1 %fusion.6 = f32[16,2048]{1,0:T(8,128)S(1)} fusion(bf16[16,512]{1,0:T(8,128)(2,1)} %get-tuple-element.4, bf16[512,2048]{1,0:T(8,128)(2,1)S(1)} %copy-done), kind=kOutput, calls=%fused_computation.16 | convolution fusion | flops 33554432 | bytes 2244608 | tf_op jit(solution)/shard_map/dot_general | solution.py:120
  90.6 10.2 %all_to_all.10 = f32[16,4,512]{2,0,1:T(8,128)S(1)} all-to-all(f32[16,4,512]{2,0,1:T(8,128)S(1)} %bitcast.26), channel_id=1, replica_groups=mesh['x'=4,'z'=16,'c'=2,'head'=4] {'head'}, dimensions={1} | all-to-all | bytes 262144 | tf_op jit(solution)/shard_map/all_to_all | solution.py:124
  100.9 0.6 reduce_sum.22
  (4 shorter events, 0.1 us)
Async XLA Ops:
  0.6 88.9 %copy-start = (bf16[512,2048]{1,0:T(8,128)(2,1)S(1)}, bf16[512,2048]{1,0:T(8,128)(2,1)}, u32[]{:S(2)}) copy-start(bf16[512,2048]{1,0:T(8,128)(2,1)} %param.15) | copy-start | bytes 6291460
  22.8 62.8 %all-to-all-start = ((bf16[16,64,512]{2,1,0:T(8,128)(2,1)}), bf16[16,64,512]{2,1,0:T(8,128)(2,1)S(1)}, u32[]{:S(2)}, u32[]{:S(2)}) async-start(bf16[16,64,512]{2,1,0:T(8,128)(2,1)} %copy.13), calls=%async_computation | async-start | bytes 2097152 | tf_op jit(solution)/shard_map/all_to_all | solution.py:94

commit v3 on v2

--- a/solution.py
+++ b/solution.py
@@ -79,21 +79,25 @@
 def route_two_stage(token_tuple, dealing):
     rows = jnp.concatenate([t[0] for t in token_tuple], axis=0)
     width = rows.shape[1]
-    dest_row = jnp.broadcast_to(dealing.astype(jnp.bfloat16).reshape(1, 1), (1, width))
+    zn = lax.axis_size("z")
+    cn = lax.axis_size("c")
+    group = lax.axis_size("x") * cn
+    dest = dealing[0]
+    dest_col = (dest // (zn * cn)) * cn + dest % cn
+    dest_row = jnp.broadcast_to((dest + 1).astype(jnp.bfloat16).reshape(1, 1), (1, width))
     payload = jnp.concatenate([rows, dest_row], axis=0)
-    gathered = lax.all_gather(payload, ROW, axis=0, tiled=False)
-    dest = gathered[:, -1, 0].astype(jnp.int32)
-    body = gathered[:, :-1, :]
-    zn = lax.axis_size("z")
+    pick = (jnp.arange(group, dtype=jnp.int32) == dest_col)[:, None, None]
+    send1 = jnp.where(pick, payload[None], jnp.zeros_like(payload)[None])
+    got1 = lax.all_to_all(send1, ROW, 0, 0, tiled=False)
+    held = got1[:, -1, 0].astype(jnp.int32) - 1
+    body = got1[:, :-1, :]
     my_x = lax.axis_index("x")
     my_c = lax.axis_index("c")
-    cn = lax.axis_size("c")
     target = (my_x * zn + jnp.arange(zn, dtype=jnp.int32)) * cn + my_c
-    match = (target[:, None] == dest[None, :]).astype(jnp.bfloat16)
+    match = (target[:, None] == held[None, :]).astype(jnp.bfloat16)
     send = jnp.einsum("zk,kre->zre", match, body, preferred_element_type=jnp.float32).astype(jnp.bfloat16)
     got = lax.all_to_all(send, "z", 0, 0, tiled=False)
-    mine = jnp.sum(got.astype(jnp.float32), axis=0).astype(jnp.bfloat16)
-    return mine
+    return jnp.sum(got.astype(jnp.float32), axis=0).astype(jnp.bfloat16)
 
 
 def per_device(

time: 102 us -> 104 us (1.020); the launches traced: 101 us -> 102 us
  blocking collectives: 26.3 us -> 10.2 us
  waiting for transfers between devices: 49.8 us -> 57.9 us
  starting transfers between devices: 12.3 us -> 20 us
    all_gather x1 -> x0, blocking collectives: 16 us -> none  [route_two_stage(): gathered = lax.all_gather(payload, ROW, axis=0, tiled=False)]
    all_to_all x0 -> x1, starting transfers between devices: none -> 9.3 us  [route_two_stage(): got1 = lax.all_to_all(send1, ROW, 0, 0, tiled=False)]
    all_to_all x0 -> x1, waiting for transfers between devices: none -> 8.93 us  [route_two_stage(): got1 = lax.all_to_all(send1, ROW, 0, 0, tiled=False)]
    all_to_all x1, starting transfers between devices: 12.3 us -> 10.7 us  [route_two_stage(): got = lax.all_to_all(send, 'z', 0, 0, tiled=False)]
  transfers between devices with their start and end apart: 1 -> 2, of which waited for: 1 -> 2; matrix products, arithmetic and copies ran while one was open for 0% -> 0% of each run, Pallas kernels for 0% -> 0%
where the time goes in v3:
time: 104 us; the launch traced here: 102 us
  waiting for transfers between devices  57.9 us (56%)
  starting transfers between devices  20 us (19%)
  blocking collectives  10.2 us (10%)
  local copies, waits for them, and re-layouts  4.52 us (4%)
  Pallas kernels  3.1 us (3%)
  other arithmetic  2.55 us (2%)
  between operations  2.17 us (2%)
  matrix products  1.69 us (2%)
    all_to_all x1, waiting for transfers between devices, route_two_stage(): got = lax.all_to_all(send, 'z', 0, 0, tiled=False)  49 us
    all_to_all x1, starting transfers between devices, route_two_stage(): got = lax.all_to_all(send, 'z', 0, 0, tiled=False)  10.7 us
    all_to_all x1, blocking collectives, per_device(): swapped = lax.all_to_all(split, 'head', 1, 1, tiled=True)  10.2 us
    all_to_all x1, starting transfers between devices, route_two_stage(): got1 = lax.all_to_all(send1, ROW, 0, 0, tiled=False)  9.3 us
    all_to_all x1, waiting for transfers between devices, route_two_stage(): got1 = lax.all_to_all(send1, ROW, 0, 0, tiled=False)  8.93 us
    pallas_call x1, Pallas kernels, mixer(): pl.pallas_call(mixer_kernel, out_shape=(jax.ShapeDtypeStruct(s0.shape, jn...  3.1 us
    unnamed x6, local copies, waits for them, and re-layouts  2.89 us
  transfers between devices with their start and end apart: 2, of which 2 were waited for; matrix products, arithmetic and copies ran while one was open for 0% of the time, Pallas kernels for 0%

profile of v3, /device:TPU:6, one launch (start us, length us, event | category | flops | bytes accessed | tf_op | source)
XLA Modules:
  0.0 102.2 jit_solution(550933932023026813)
XLA Ops:
  0.6 0.0 copy-start
  1.5 0.7 bitcast_dynamic-update-slice_fusion.3
  2.2 0.7 bitcast_dynamic-update-slice_fusion.2
  2.9 0.7 bitcast_dynamic-update-slice_fusion.1
  3.7 0.7 bitcast_dynamic-update-slice_fusion
  4.4 0.9 broadcast_select_fusion
  5.3 9.3 %all-to-all-start = ((bf16[8,65,512]{2,1,0:T(8,128)(2,1)}), bf16[8,65,512]{2,1,0:T(8,128)(2,1)S(1)}, u32[]{:S(2)}, u32[]{:S(2)}) async-start(bf16[8,65,512]{2,1,0:T(8,128)(2,1)} %broadcast_select_fusion), calls=%async_computation | async-start | bytes 1179648 | tf_op jit(solution)/shard_map/all_to_all | solution.py:91
  14.6 8.9 %all-to-all-done = bf16[8,65,512]{2,1,0:T(8,128)(2,1)S(1)} async-done(((bf16[8,65,512]{2,1,0:T(8,128)(2,1)}), bf16[8,65,512]{2,1,0:T(8,128)(2,1)S(1)}, u32[]{:S(2)}, u32[]{:S(2)}) %all-to-all-start) | async-done | bytes 532512 | tf_op jit(solution)/shard_map/all_to_all | solution.py:91
  23.6 0.2 fusion.2
  23.8 0.6 convolution_convert_fusion
  24.4 1.6 %copy.12 = bf16[16,64,512]{2,1,0:T(8,128)(2,1)} copy(bf16[16,64,512]{2,0,1:T(8,128)(2,1)S(1)} %convolution_convert_fusion) | data formatting | bytes 2097152 | tf_op jit(solution)/shard_map/convert_element_type | solution.py:98
  26.0 10.7 %all-to-all-start.1 = ((bf16[16,64,512]{2,1,0:T(8,128)(2,1)}), bf16[16,64,512]{2,1,0:T(8,128)(2,1)S(1)}, u32[]{:S(2)}, u32[]{:S(2)}) async-start(bf16[16,64,512]{2,1,0:T(8,128)(2,1)} %copy.12), calls=%async_computation.1 | async-start | bytes 2097152 | tf_op jit(solution)/shard_map/all_to_all | solution.py:99
  37.3 49.0 %all-to-all-done.1 = bf16[16,64,512]{2,1,0:T(8,128)(2,1)S(1)} async-done(((bf16[16,64,512]{2,1,0:T(8,128)(2,1)}), bf16[16,64,512]{2,1,0:T(8,128)(2,1)S(1)}, u32[]{:S(2)}, u32[]{:S(2)}) %all-to-all-start.1) | async-done | bytes 1048608 | tf_op jit(solution)/shard_map/all_to_all | solution.py:99
  86.3 0.8 reduce_sum.21.tok_ref
  87.1 3.1 %shard_map.104 = (f32[4,128,128]{2,1,0:T(8,128)}, bf16[16,512]{1,0:T(8,128)(2,1)}) custom-call(s32[1]{0:T(128)S(6)} %copy.25.acc_ref, bf16[64,512]{1,0:T(8,128)(2,1)} %reduce_sum.21.tok_ref, f32[4,128,128]{2,1,0:T(8,128)} %bitcast.31, f32[1,128]{1,0:T(1,128)} %bitcast.33), custom_call_target="tpu_custom_call" | custom-call | tf_op jit(solution)/shard_map/pallas_call | solution.py:70
  90.2 0.0 copy-done
  90.2 1.1 %fusion.7 = f32[16,2048]{1,0:T(8,128)S(1)} fusion(bf16[16,512]{1,0:T(8,128)(2,1)} %get-tuple-element.4, bf16[512,2048]{1,0:T(8,128)(2,1)S(1)} %copy-done), kind=kOutput, calls=%fused_computation.19 | convolution fusion | flops 33554432 | bytes 2244608 | tf_op jit(solution)/shard_map/dot_general | solution.py:124
  91.3 10.2 %all_to_all.15 = f32[16,4,512]{2,0,1:T(8,128)S(1)} all-to-all(f32[16,4,512]{2,0,1:T(8,128)S(1)} %bitcast.30), channel_id=1, replica_groups=mesh['x'=4,'z'=16,'c'=2,'head'=4] {'head'}, dimensions={1} | all-to-all | bytes 262144 | tf_op jit(solution)/shard_map/all_to_all | solution.py:128
  101.5 0.6 reduce_sum.22
  (5 shorter events, 0.1 us)
Async XLA Ops:
  0.6 89.6 %copy-start = (bf16[512,2048]{1,0:T(8,128)(2,1)S(1)}, bf16[512,2048]{1,0:T(8,128)(2,1)}, u32[]{:S(2)}) copy-start(bf16[512,2048]{1,0:T(8,128)(2,1)} %param.15) | copy-start | bytes 6291460
  5.3 18.2 %all-to-all-start = ((bf16[8,65,512]{2,1,0:T(8,128)(2,1)}), bf16[8,65,512]{2,1,0:T(8,128)(2,1)S(1)}, u32[]{:S(2)}, u32[]{:S(2)}) async-start(bf16[8,65,512]{2,1,0:T(8,128)(2,1)} %broadcast_select_fusion), calls=%async_computation | async-start | bytes 1179648 | tf_op jit(solution)/shard_map/all_to_all | solution.py:91
  26.0 60.3 %all-to-all-start.1 = ((bf16[16,64,512]{2,1,0:T(8,128)(2,1)}), bf16[16,64,512]{2,1,0:T(8,128)(2,1)S(1)}, u32[]{:S(2)}, u32[]{:S(2)}) async-start(bf16[16,64,512]{2,1,0:T(8,128)(2,1)} %copy.12), calls=%async_computation.1 | async-start | bytes 2097152 | tf_op jit(solution)/shard_map/all_to_all | solution.py:99

commit v4 on v2

--- a/solution.py
+++ b/solution.py
@@ -19,16 +19,37 @@
     return jnp.dot(a, b, precision=HI, preferred_element_type=jnp.float32)
 
 
-def mixer_kernel(acc_ref, tok_ref, s0_ref, gain_ref, new_ref, mixed_ref):
+def pack_kernel(dest_ref, q_ref, f_ref, v_ref, g_ref, out_ref):
+    for i, ref in enumerate((q_ref, f_ref, v_ref, g_ref)):
+        out_ref[i] = ref[0]
+    mark = jnp.broadcast_to(dest_ref[0] + 1, out_ref.shape[1:]).astype(jnp.float32)
+    out_ref[4] = mark.astype(out_ref.dtype)
+
+
+def pack(dealing, q, f, v, g):
+    vmem = pl.BlockSpec(memory_space=pltpu.VMEM)
+    return pl.pallas_call(
+        pack_kernel,
+        out_shape=jax.ShapeDtypeStruct((5,) + q.shape[1:], q.dtype),
+        in_specs=[pl.BlockSpec(memory_space=pltpu.SMEM), vmem, vmem, vmem, vmem],
+        out_specs=vmem,
+    )(dealing, q, f, v, g)
+
+
+def mixer_kernel(acc_ref, got_ref, s0_ref, gain_ref, w_hbm, new_ref, part_ref, w_vmem, mixed_scr, sem):
+    w_copy = pltpu.make_async_copy(w_hbm, w_vmem, sem)
+    w_copy.start()
     acc = acc_ref[0]
-    tok = tok_ref[...].astype(jnp.float32)
-    t_len = tok.shape[0] // 4
+    blocks = got_ref[0].astype(jnp.float32)
+    for i in range(1, got_ref.shape[0]):
+        blocks = blocks + got_ref[i].astype(jnp.float32)
     heads = s0_ref.shape[0]
     hd = s0_ref.shape[2]
-    q = tok[0:t_len]
-    fl = tok[t_len:2 * t_len]
-    v = tok[2 * t_len:3 * t_len]
-    g = tok[3 * t_len:4 * t_len]
+    q = blocks[0]
+    fl = blocks[1]
+    v = blocks[2]
+    g = blocks[3]
+    t_len = q.shape[0]
     a = lower_bound + (1.0 - lower_bound) * (1.0 / (1.0 + jnp.exp(-fl)))
     b = 1.0 - a
     la = jnp.log(a)
@@ -60,40 +81,41 @@
         new_ref[h] = _dot(diag, s0) + _dot(jnp.transpose(w[:, lanes]), v_h)
         meansq = jnp.mean(o_h * o_h, axis=-1, keepdims=True)
         mixed = o_h * lax.rsqrt(meansq + norm_eps) * gain * silu_g[:, lanes]
-        mixed_ref[:, lanes] = mixed.astype(mixed_ref.dtype)
+        mixed_scr[:, lanes] = mixed.astype(mixed_scr.dtype)
+    w_copy.wait()
+    part_ref[...] = jnp.dot(mixed_scr[...], w_vmem[...], preferred_element_type=jnp.float32)
 
 
-def mixer(acc, tok, s0, gain):
+def mixer(acc, got, s0, gain, weight):
     heads, hd = s0.shape[0], s0.shape[2]
-    t_len = tok.shape[0] // 4
+    t_len = got.shape[2]
     vmem = pl.BlockSpec(memory_space=pltpu.VMEM)
     return pl.pallas_call(
         mixer_kernel,
         out_shape=(jax.ShapeDtypeStruct(s0.shape, jnp.float32),
-                   jax.ShapeDtypeStruct((t_len, heads * hd), jnp.bfloat16)),
-        in_specs=[pl.BlockSpec(memory_space=pltpu.SMEM), vmem, vmem, vmem],
+                   jax.ShapeDtypeStruct((t_len, weight.shape[1]), jnp.float32)),
+        in_specs=[pl.BlockSpec(memory_space=pltpu.SMEM), vmem, vmem, vmem,
+                  pl.BlockSpec(memory_space=pl.ANY)],
         out_specs=(vmem, vmem),
-    )(acc, tok, s0, gain)
+        scratch_shapes=[pltpu.VMEM(weight.shape, weight.dtype),
+                        pltpu.VMEM((t_len, heads * hd), jnp.bfloat16),
+                        pltpu.SemaphoreType.DMA(())],
+    )(acc, got, s0, gain, weight)
 
 
 def route_two_stage(token_tuple, dealing):
-    rows = jnp.concatenate([t[0] for t in token_tuple], axis=0)
-    width = rows.shape[1]
-    dest_row = jnp.broadcast_to(dealing.astype(jnp.bfloat16).reshape(1, 1), (1, width))
-    payload = jnp.concatenate([rows, dest_row], axis=0)
+    payload = pack(dealing, *token_tuple)
     gathered = lax.all_gather(payload, ROW, axis=0, tiled=False)
-    dest = gathered[:, -1, 0].astype(jnp.int32)
-    body = gathered[:, :-1, :]
+    dest = gathered[:, 4, 0, 0].astype(jnp.int32) - 1
+    body = gathered[:, :4]
     zn = lax.axis_size("z")
     my_x = lax.axis_index("x")
     my_c = lax.axis_index("c")
     cn = lax.axis_size("c")
     target = (my_x * zn + jnp.arange(zn, dtype=jnp.int32)) * cn + my_c
     match = (target[:, None] == dest[None, :]).astype(jnp.bfloat16)
-    send = jnp.einsum("zk,kre->zre", match, body, preferred_element_type=jnp.float32).astype(jnp.bfloat16)
-    got = lax.all_to_all(send, "z", 0, 0, tiled=False)
-    mine = jnp.sum(got.astype(jnp.float32), axis=0).astype(jnp.bfloat16)
-    return mine
+    send = jnp.einsum("zk,kbre->zbre", match, body, preferred_element_type=jnp.float32).astype(jnp.bfloat16)
+    return lax.all_to_all(send, "z", 0, 0, tiled=False)
 
 
 def per_device(
@@ -112,12 +134,9 @@
     head_local = init_states.shape[1]
     head_size = init_states.shape[3]
     token_tuple = (queries, forget_logits, values, gate_input)
-    mine = route_two_stage(token_tuple, dealing)
-    new_states, mixed_rows = mixer(accepted, mine, init_states[0], norm_gain.reshape(1, head_size))
+    got = route_two_stage(token_tuple, dealing)
+    new_states, partial_out = mixer(accepted, got, init_states[0], norm_gain.reshape(1, head_size), out_weight)
     new_states = new_states[None]
-
-    mixed_rows = mixed_rows.reshape(local_count * draft_len, head_local * head_size)
-    partial_out = jnp.dot(mixed_rows, out_weight, preferred_element_type=jnp.float32)
     hn = lax.axis_size("head")
     rows = partial_out.shape[0]
     split = partial_out.reshape(rows, hn, partial_out.shape[1] // hn)

time: 102 us -> 101 us (level)
  Pallas kernels: 3.1 us -> 5.45 us
  local copies, waits for them, and re-layouts: 4.66 us -> 3.51 us
  matrix products: 1.67 us -> 0.57 us
    unnamed x6 -> x2, local copies, waits for them, and re-layouts: 3.04 us -> 0.99 us
    convert_element_type x1 -> x0, local copies, waits for them, and re-layouts: 1.57 us -> none  [route_two_stage(): jnp.einsum('zk,kre->zre', match, body, preferred_element_type=jnp.float32)]
    dot_general x0 -> x1, local copies, waits for them, and re-layouts: none -> 1.57 us  [route_two_stage(): jnp.einsum('zk,kbre->zbre', match, body, preferred_element_type=jnp.float32)]
    pallas_call x0 -> x1, Pallas kernels: none -> 1.41 us  [pack(): pl.pallas_call(pack_kernel, out_shape=jax.ShapeDtypeStruct((5,) + q.shape...]
    dot_general x2 -> x1, matrix products: 1.67 us -> 0.57 us  [route_two_stage(): jnp.einsum('zk,kbre->zbre', match, body, preferred_element_type=jnp.float32)]
where the time goes in v4:
time: 101 us
  waiting for transfers between devices  49.8 us (49%)
  blocking collectives  26.8 us (27%)
  starting transfers between devices  12.1 us (12%)
  Pallas kernels  5.45 us (5%)
  local copies, waits for them, and re-layouts  3.51 us (3%)
  between operations  1.97 us (2%)
    all_to_all x1, waiting for transfers between devices, route_two_stage(): return lax.all_to_all(send, 'z', 0, 0, tiled=False)  49.8 us
    all_gather x1, blocking collectives, route_two_stage(): gathered = lax.all_gather(payload, ROW, axis=0, tiled=False)  16.5 us
    all_to_all x1, starting transfers between devices, route_two_stage(): return lax.all_to_all(send, 'z', 0, 0, tiled=False)  12.1 us
    all_to_all x1, blocking collectives, per_device(): swapped = lax.all_to_all(split, 'head', 1, 1, tiled=True)  10.2 us
    pallas_call x1, Pallas kernels, mixer(): pl.pallas_call(mixer_kernel, out_shape=(jax.ShapeDtypeStruct(s0.shape, jn...  4.04 us
  transfers between devices with their start and end apart: 1, of which 1 were waited for; matrix products, arithmetic and copies ran while one was open for 0% of the time, Pallas kernels for 0%

profile of v4, /device:TPU:6, one launch (start us, length us, event | category | flops | bytes accessed | tf_op | source)
XLA Modules:
  0.0 101.1 jit_solution(13534469206221126176)
XLA Ops:
  1.3 1.4 %shard_map.104 = bf16[5,16,512]{2,1,0:T(8,128)(2,1)} custom-call(s32[1]{0:T(128)S(6)} %copy.28.dest_ref, bf16[1,16,512]{2,1,0:T(8,128)(2,1)} %q_ref.1, bf16[1,16,512]{2,1,0:T(8,128)(2,1)} %f_ref.1, bf16[1,16,512]{2,1,0:T(8,128)(2,1)} %v_ref.1, bf16[1,16,512]{2,1,0:T(8,128)(2,1)} %g_ref.1), custom_call_target="tpu_custom_call" | custom-call | tf_op jit(solution)/shard_map/pallas_call | solution.py:31
  2.7 16.5 %all-gather = bf16[40,16,512]{2,1,0:T(8,128)(2,1)S(1)} all-gather(bf16[5,16,512]{2,1,0:T(8,128)(2,1)} %shard_map.104), channel_id=2, replica_groups=mesh['x'=4,'z'=16,'c'=2,'head'=4] {'x','c'}, dimensions={0}, use_global_device_ids=true | all-gather | bytes 737280 | tf_op jit(solution)/shard_map/all_gather | solution.py:108
  19.3 0.2 fusion.3
  19.5 0.6 fusion
  20.1 1.6 %copy.26 = bf16[16,4,16,512]{3,2,1,0:T(8,128)(2,1)} copy(bf16[16,4,16,512]{3,0,2,1:T(8,128)(2,1)S(1)} %fusion) | data formatting | bytes 2097152 | tf_op jit(solution)/shard_map/zk,kbre->zbre/dot_general | solution.py:117
  21.7 12.1 %all-to-all-start = ((bf16[16,4,16,512]{3,2,1,0:T(8,128)(2,1)}), bf16[16,4,16,512]{3,2,1,0:T(8,128)(2,1)S(1)}, u32[]{:S(2)}, u32[]{:S(2)}) async-start(bf16[16,4,16,512]{3,2,1,0:T(8,128)(2,1)} %copy.26), calls=%async_computation | async-start | bytes 2097152 | tf_op jit(solution)/shard_map/all_to_all | solution.py:118
  34.4 49.8 %all-to-all-done.got_ref = bf16[16,4,16,512]{3,2,1,0:T(8,128)(2,1)S(1)} async-done(((bf16[16,4,16,512]{3,2,1,0:T(8,128)(2,1)}), bf16[16,4,16,512]{3,2,1,0:T(8,128)(2,1)S(1)}, u32[]{:S(2)}, u32[]{:S(2)}) %all-to-all-start) | async-done | bytes 1048608 | tf_op jit(solution)/shard_map/all_to_all | solution.py:118
  84.3 0.0 copy-start
  84.3 1.0 copy-done
  85.2 4.0 %shard_map.105 = (f32[4,128,128]{2,1,0:T(8,128)}, f32[16,2048]{1,0:T(8,128)}) custom-call(s32[1]{0:T(128)S(6)} %copy.29.acc_ref, bf16[16,4,16,512]{3,2,1,0:T(8,128)(2,1)} %copy-done, f32[4,128,128]{2,1,0:T(8,128)} %bitcast.19, f32[1,128]{1,0:T(1,128)} %bitcast.22, bf16[512,2048]{1,0:T(8,128)(2,1)} %w_hbm.1), custom_call_target="tpu_custom_call" | custom-call | tf_op jit(solution)/shard_map/pallas_call | solution.py:93
  89.3 0.9 copy.27
  90.2 10.2 %all_to_all.10 = f32[16,4,512]{2,0,1:T(8,128)S(1)} all-to-all(f32[16,4,512]{2,0,1:T(8,128)S(1)} %bitcast.18), channel_id=1, replica_groups=mesh['x'=4,'z'=16,'c'=2,'head'=4] {'head'}, dimensions={1} | all-to-all | bytes 262144 | tf_op jit(solution)/shard_map/all_to_all | solution.py:143
  100.4 0.6 reduce_sum.9
  (2 shorter events, 0.0 us)
Async XLA Ops:
  21.7 62.6 %all-to-all-start = ((bf16[16,4,16,512]{3,2,1,0:T(8,128)(2,1)}), bf16[16,4,16,512]{3,2,1,0:T(8,128)(2,1)S(1)}, u32[]{:S(2)}, u32[]{:S(2)}) async-start(bf16[16,4,16,512]{3,2,1,0:T(8,128)(2,1)} %copy.26), calls=%async_computation | async-start | bytes 2097152 | tf_op jit(solution)/shard_map/all_to_all | solution.py:118
  84.3 1.0 copy-start

commit v5 on v4

--- a/solution.py
+++ b/solution.py
@@ -36,9 +36,12 @@
     )(dealing, q, f, v, g)
 
 
-def mixer_kernel(acc_ref, got_ref, s0_ref, gain_ref, w_hbm, new_ref, part_ref, w_vmem, mixed_scr, sem):
-    w_copy = pltpu.make_async_copy(w_hbm, w_vmem, sem)
+def mixer_kernel(acc_ref, got_any, s0_ref, gain_ref, w_hbm, new_ref, part_ref, got_ref, w_vmem, mixed_scr, sems):
+    got_copy = pltpu.make_async_copy(got_any, got_ref, sems.at[0])
+    got_copy.start()
+    w_copy = pltpu.make_async_copy(w_hbm, w_vmem, sems.at[1])
     w_copy.start()
+    got_copy.wait()
     acc = acc_ref[0]
     blocks = got_ref[0].astype(jnp.float32)
     for i in range(1, got_ref.shape[0]):
@@ -83,38 +86,64 @@
         mixed = o_h * lax.rsqrt(meansq + norm_eps) * gain * silu_g[:, lanes]
         mixed_scr[:, lanes] = mixed.astype(mixed_scr.dtype)
     w_copy.wait()
-    part_ref[...] = jnp.dot(mixed_scr[...], w_vmem[...], preferred_element_type=jnp.float32)
+    chunk = part_ref.shape[2]
+    mixed_all = mixed_scr[...]
+    for j in range(part_ref.shape[0]):
+        part_ref[j] = jnp.dot(mixed_all, w_vmem[:, j * chunk:(j + 1) * chunk],
+                              preferred_element_type=jnp.float32)
 
 
-def mixer(acc, got, s0, gain, weight):
+def mixer(acc, got, s0, gain, weight, parts):
     heads, hd = s0.shape[0], s0.shape[2]
     t_len = got.shape[2]
     vmem = pl.BlockSpec(memory_space=pltpu.VMEM)
+    anywhere = pl.BlockSpec(memory_space=pl.ANY)
     return pl.pallas_call(
         mixer_kernel,
         out_shape=(jax.ShapeDtypeStruct(s0.shape, jnp.float32),
-                   jax.ShapeDtypeStruct((t_len, weight.shape[1]), jnp.float32)),
-        in_specs=[pl.BlockSpec(memory_space=pltpu.SMEM), vmem, vmem, vmem,
-                  pl.BlockSpec(memory_space=pl.ANY)],
+                   jax.ShapeDtypeStruct((parts, t_len, weight.shape[1] // parts), jnp.float32)),
+        in_specs=[pl.BlockSpec(memory_space=pltpu.SMEM), anywhere, vmem, vmem, anywhere],
         out_specs=(vmem, vmem),
-        scratch_shapes=[pltpu.VMEM(weight.shape, weight.dtype),
+        scratch_shapes=[pltpu.VMEM(got.shape, got.dtype),
+                        pltpu.VMEM(weight.shape, weight.dtype),
                         pltpu.VMEM((t_len, heads * hd), jnp.bfloat16),
-                        pltpu.SemaphoreType.DMA(())],
+                        pltpu.SemaphoreType.DMA((2,))],
     )(acc, got, s0, gain, weight)
+
+
+def select_kernel(idx_ref, held_ref, out_ref):
+    count = held_ref.shape[0]
+    keep = out_ref.shape[1]
+    for z in range(out_ref.shape[0]):
+        k = idx_ref[z]
+        blk = held_ref[jnp.minimum(k, count - 1), 0:keep]
+        out_ref[z] = jnp.where(k < count, blk, jnp.zeros_like(blk))
+
+
+def select(idx, held, keep):
+    vmem = pl.BlockSpec(memory_space=pltpu.VMEM)
+    return pl.pallas_call(
+        select_kernel,
+        out_shape=jax.ShapeDtypeStruct((idx.shape[0], keep) + held.shape[2:], held.dtype),
+        in_specs=[pl.BlockSpec(memory_space=pltpu.SMEM), vmem],
+        out_specs=vmem,
+    )(idx, held)
 
 
 def route_two_stage(token_tuple, dealing):
     payload = pack(dealing, *token_tuple)
     gathered = lax.all_gather(payload, ROW, axis=0, tiled=False)
     dest = gathered[:, 4, 0, 0].astype(jnp.int32) - 1
-    body = gathered[:, :4]
     zn = lax.axis_size("z")
     my_x = lax.axis_index("x")
     my_c = lax.axis_index("c")
     cn = lax.axis_size("c")
     target = (my_x * zn + jnp.arange(zn, dtype=jnp.int32)) * cn + my_c
-    match = (target[:, None] == dest[None, :]).astype(jnp.bfloat16)
-    send = jnp.einsum("zk,kbre->zbre", match, body, preferred_element_type=jnp.float32).astype(jnp.bfloat16)
+    count = dest.shape[0]
+    slots = jnp.arange(count, dtype=jnp.int32)
+    match = target[:, None] == dest[None, :]
+    idx = jnp.min(jnp.where(match, slots[None, :], count), axis=1)
+    send = select(idx, gathered, 4)
     return lax.all_to_all(send, "z", 0, 0, tiled=False)
 
 
@@ -135,13 +164,11 @@
     head_size = init_states.shape[3]
     token_tuple = (queries, forget_logits, values, gate_input)
     got = route_two_stage(token_tuple, dealing)
-    new_states, partial_out = mixer(accepted, got, init_states[0], norm_gain.reshape(1, head_size), out_weight)
+    hn = lax.axis_size("head")
+    new_states, partial_out = mixer(accepted, got, init_states[0], norm_gain.reshape(1, head_size), out_weight, hn)
     new_states = new_states[None]
-    hn = lax.axis_size("head")
-    rows = partial_out.shape[0]
-    split = partial_out.reshape(rows, hn, partial_out.shape[1] // hn)
-    swapped = lax.all_to_all(split, "head", 1, 1, tiled=True)
-    summed = jnp.sum(swapped, axis=1)
+    swapped = lax.all_to_all(partial_out, "head", 0, 0, tiled=True)
+    summed = jnp.sum(swapped, axis=0)
     verified = summed.astype(jnp.bfloat16).reshape(local_count, draft_len, summed.shape[1])
     return (verified, new_states)
 

time: 101 us -> 102 us (level)
  Pallas kernels: 5.45 us -> 8.27 us
  local copies, waits for them, and re-layouts: 3.51 us -> 0.99 us
    pallas_call x0 -> x1, Pallas kernels: none -> 2.16 us  [select(): pl.pallas_call(select_kernel, out_shape=jax.ShapeDtypeStruct((idx.shape[0...]
    dot_general x1 -> x0, local copies, waits for them, and re-layouts: 1.57 us -> none  [route_two_stage(): jnp.einsum('zk,kbre->zbre', match, body, preferred_element_type=jnp.float32)]
where the time goes in v5:
time: 102 us
  waiting for transfers between devices  49.8 us (49%)
  blocking collectives  27 us (26%)
  starting transfers between devices  12.1 us (12%)
  Pallas kernels  8.27 us (8%)
  between operations  1.96 us (2%)
  other arithmetic  1.46 us (1%)
    all_to_all x1, waiting for transfers between devices, route_two_stage(): return lax.all_to_all(send, 'z', 0, 0, tiled=False)  49.8 us
    all_gather x1, blocking collectives, route_two_stage(): gathered = lax.all_gather(payload, ROW, axis=0, tiled=False)  16.5 us
    all_to_all x1, starting transfers between devices, route_two_stage(): return lax.all_to_all(send, 'z', 0, 0, tiled=False)  12.1 us
    all_to_all x1, blocking collectives, per_device(): swapped = lax.all_to_all(partial_out, 'head', 0, 0, tiled=True)  10.5 us
    pallas_call x1, Pallas kernels, mixer(): pl.pallas_call(mixer_kernel, out_shape=(jax.ShapeDtypeStruct(s0.shape, jn...  4.69 us
    pallas_call x1, Pallas kernels, select(): pl.pallas_call(select_kernel, out_shape=jax.ShapeDtypeStruct((idx.shape[0...  2.16 us
  transfers between devices with their start and end apart: 1, of which 1 were waited for; matrix products, arithmetic and copies ran while one was open for 0% of the time, Pallas kernels for 0%

profile of v5, /device:TPU:6, one launch (start us, length us, event | category | flops | bytes accessed | tf_op | source)
XLA Modules:
  0.0 101.6 jit_solution(6578207293029487272)
XLA Ops:
  1.3 1.4 %shard_map.104 = bf16[5,16,512]{2,1,0:T(8,128)(2,1)} custom-call(s32[1]{0:T(128)S(6)} %copy.11.dest_ref, bf16[1,16,512]{2,1,0:T(8,128)(2,1)} %q_ref.1, bf16[1,16,512]{2,1,0:T(8,128)(2,1)} %f_ref.1, bf16[1,16,512]{2,1,0:T(8,128)(2,1)} %v_ref.1, bf16[1,16,512]{2,1,0:T(8,128)(2,1)} %g_ref.1), custom_call_target="tpu_custom_call" | custom-call | tf_op jit(solution)/shard_map/pallas_call | solution.py:31
  2.7 16.5 %all-gather = bf16[40,16,512]{2,1,0:T(8,128)(2,1)S(1)} all-gather(bf16[5,16,512]{2,1,0:T(8,128)(2,1)} %shard_map.104), channel_id=2, replica_groups=mesh['x'=4,'z'=16,'c'=2,'head'=4] {'x','c'}, dimensions={0}, use_global_device_ids=true | all-gather | bytes 737280 | tf_op jit(solution)/shard_map/all_gather | solution.py:135
  19.2 0.0 copy-start.1
  19.2 0.2 fusion.1
  19.5 0.6 select_reduce_fusion.idx_ref
  20.1 0.0 copy-done.1
  20.1 2.2 %shard_map.105 = bf16[16,4,16,512]{3,2,1,0:T(8,128)(2,1)} custom-call(s32[16]{0:T(128)} %select_reduce_fusion.idx_ref, bf16[8,5,16,512]{3,2,1,0:T(8,128)(2,1)} %bitcast.8), custom_call_target="tpu_custom_call" | custom-call | tf_op jit(solution)/shard_map/pallas_call | solution.py:125
  22.2 12.1 %all-to-all-start = ((bf16[16,4,16,512]{3,2,1,0:T(8,128)(2,1)}), bf16[16,4,16,512]{3,2,1,0:T(8,128)(2,1)S(1)}, u32[]{:S(2)}, u32[]{:S(2)}) async-start(bf16[16,4,16,512]{3,2,1,0:T(8,128)(2,1)} %shard_map.105), calls=%async_computation | async-start | bytes 2097152 | tf_op jit(solution)/shard_map/all_to_all | solution.py:147
  35.0 49.8 %all-to-all-done.got_any = bf16[16,4,16,512]{3,2,1,0:T(8,128)(2,1)S(1)} async-done(((bf16[16,4,16,512]{3,2,1,0:T(8,128)(2,1)}), bf16[16,4,16,512]{3,2,1,0:T(8,128)(2,1)S(1)}, u32[]{:S(2)}, u32[]{:S(2)}) %all-to-all-start) | async-done | bytes 1048608 | tf_op jit(solution)/shard_map/all_to_all | solution.py:147
  84.8 0.0 copy-start
  84.8 1.0 copy-done
  85.8 4.7 %shard_map.106 = (f32[4,128,128]{2,1,0:T(8,128)}, f32[4,16,512]{2,1,0:T(8,128)}) custom-call(s32[1]{0:T(128)S(6)} %copy.12.acc_ref, bf16[16,4,16,512]{3,2,1,0:T(8,128)(2,1)} %copy-done, f32[4,128,128]{2,1,0:T(8,128)} %bitcast.9, f32[1,128]{1,0:T(1,128)} %bitcast.11, bf16[512,2048]{1,0:T(8,128)(2,1)} %w_hbm.1), custom_call_target="tpu_custom_call" | custom-call | tf_op jit(solution)/shard_map/pallas_call | solution.py:101
  90.5 10.5 %all_to_all.10 = f32[4,16,512]{2,1,0:T(8,128)S(1)} all-to-all(f32[4,16,512]{2,1,0:T(8,128)} %get-tuple-element.4), channel_id=1, replica_groups=mesh['x'=4,'z'=16,'c'=2,'head'=4] {'head'}, dimensions={0} | all-to-all | bytes 262144 | tf_op jit(solution)/shard_map/all_to_all | solution.py:170
  101.0 0.6 reduce_sum.9
  (1 shorter events, 0.0 us)
Async XLA Ops:
  19.2 0.9 copy-start.1
  22.2 62.6 %all-to-all-start = ((bf16[16,4,16,512]{3,2,1,0:T(8,128)(2,1)}), bf16[16,4,16,512]{3,2,1,0:T(8,128)(2,1)S(1)}, u32[]{:S(2)}, u32[]{:S(2)}) async-start(bf16[16,4,16,512]{3,2,1,0:T(8,128)(2,1)} %shard_map.105), calls=%async_computation | async-start | bytes 2097152 | tf_op jit(solution)/shard_map/all_to_all | solution.py:147
  84.8 1.0 copy-start

commit v6 on v4

--- a/solution.py
+++ b/solution.py
@@ -36,13 +36,11 @@
     )(dealing, q, f, v, g)
 
 
-def mixer_kernel(acc_ref, got_ref, s0_ref, gain_ref, w_hbm, new_ref, part_ref, w_vmem, mixed_scr, sem):
+def mixer_kernel(acc_ref, tok_ref, s0_ref, gain_ref, w_hbm, new_ref, part_ref, w_vmem, mixed_scr, sem):
     w_copy = pltpu.make_async_copy(w_hbm, w_vmem, sem)
     w_copy.start()
     acc = acc_ref[0]
-    blocks = got_ref[0].astype(jnp.float32)
-    for i in range(1, got_ref.shape[0]):
-        blocks = blocks + got_ref[i].astype(jnp.float32)
+    blocks = tok_ref[...].astype(jnp.float32)
     heads = s0_ref.shape[0]
     hd = s0_ref.shape[2]
     q = blocks[0]
@@ -83,24 +81,28 @@
         mixed = o_h * lax.rsqrt(meansq + norm_eps) * gain * silu_g[:, lanes]
         mixed_scr[:, lanes] = mixed.astype(mixed_scr.dtype)
     w_copy.wait()
-    part_ref[...] = jnp.dot(mixed_scr[...], w_vmem[...], preferred_element_type=jnp.float32)
+    chunk = part_ref.shape[2]
+    mixed_all = mixed_scr[...]
+    for j in range(part_ref.shape[0]):
+        part_ref[j] = jnp.dot(mixed_all, w_vmem[:, j * chunk:(j + 1) * chunk],
+                              preferred_element_type=jnp.float32)
 
 
-def mixer(acc, got, s0, gain, weight):
+def mixer(acc, tok, s0, gain, weight, parts):
     heads, hd = s0.shape[0], s0.shape[2]
-    t_len = got.shape[2]
+    t_len = tok.shape[1]
     vmem = pl.BlockSpec(memory_space=pltpu.VMEM)
     return pl.pallas_call(
         mixer_kernel,
         out_shape=(jax.ShapeDtypeStruct(s0.shape, jnp.float32),
-                   jax.ShapeDtypeStruct((t_len, weight.shape[1]), jnp.float32)),
+                   jax.ShapeDtypeStruct((parts, t_len, weight.shape[1] // parts), jnp.float32)),
         in_specs=[pl.BlockSpec(memory_space=pltpu.SMEM), vmem, vmem, vmem,
                   pl.BlockSpec(memory_space=pl.ANY)],
         out_specs=(vmem, vmem),
         scratch_shapes=[pltpu.VMEM(weight.shape, weight.dtype),
                         pltpu.VMEM((t_len, heads * hd), jnp.bfloat16),
                         pltpu.SemaphoreType.DMA(())],
-    )(acc, got, s0, gain, weight)
+    )(acc, tok, s0, gain, weight)
 
 
 def route_two_stage(token_tuple, dealing):
@@ -113,9 +115,12 @@
     my_c = lax.axis_index("c")
     cn = lax.axis_size("c")
     target = (my_x * zn + jnp.arange(zn, dtype=jnp.int32)) * cn + my_c
-    match = (target[:, None] == dest[None, :]).astype(jnp.bfloat16)
-    send = jnp.einsum("zk,kbre->zbre", match, body, preferred_element_type=jnp.float32).astype(jnp.bfloat16)
-    return lax.all_to_all(send, "z", 0, 0, tiled=False)
+    count = dest.shape[0]
+    slots = jnp.arange(count, dtype=jnp.int32)
+    idx = jnp.min(jnp.where(target[:, None] == dest[None, :], slots[None, :], count), axis=1)
+    send = jnp.take(body, idx, axis=0, mode="fill", fill_value=0)
+    got = lax.all_to_all(send, "z", 0, 0, tiled=False)
+    return jnp.sum(got.astype(jnp.float32), axis=0).astype(jnp.bfloat16)
 
 
 def per_device(
@@ -135,13 +140,11 @@
     head_size = init_states.shape[3]
     token_tuple = (queries, forget_logits, values, gate_input)
     got = route_two_stage(token_tuple, dealing)
-    new_states, partial_out = mixer(accepted, got, init_states[0], norm_gain.reshape(1, head_size), out_weight)
+    hn = lax.axis_size("head")
+    new_states, partial_out = mixer(accepted, got, init_states[0], norm_gain.reshape(1, head_size), out_weight, hn)
     new_states = new_states[None]
-    hn = lax.axis_size("head")
-    rows = partial_out.shape[0]
-    split = partial_out.reshape(rows, hn, partial_out.shape[1] // hn)
-    swapped = lax.all_to_all(split, "head", 1, 1, tiled=True)
-    summed = jnp.sum(swapped, axis=1)
+    swapped = lax.all_to_all(partial_out, "head", 0, 0, tiled=True)
+    summed = jnp.sum(swapped, axis=0)
     verified = summed.astype(jnp.bfloat16).reshape(local_count, draft_len, summed.shape[1])
     return (verified, new_states)
 

time: 101 us -> 99.9 us (0.989)
  local copies, waits for them, and re-layouts: 3.51 us -> 0.75 us
  other arithmetic: 0.86 us -> 2.68 us
    dot_general x1 -> x0, local copies, waits for them, and re-layouts: 1.57 us -> none  [route_two_stage(): jnp.einsum('zk,kbre->zbre', match, body, preferred_element_type=jnp.float32)]
    select_n x0 -> x2, other arithmetic: none -> 1.14 us  [route_two_stage(): send = jnp.take(body, idx, axis=0, mode='fill', fill_value=0)]
where the time goes in v6:
time: 99.9 us; the launch traced here: 99.4 us
  waiting for transfers between devices  49.8 us (50%)
  blocking collectives  27 us (27%)
  starting transfers between devices  12.1 us (12%)
  Pallas kernels  5.06 us (5%)
  other arithmetic  2.68 us (3%)
  between operations  1.98 us (2%)
    all_to_all x1, waiting for transfers between devices, route_two_stage(): got = lax.all_to_all(send, 'z', 0, 0, tiled=False)  49.8 us
    all_gather x1, blocking collectives, route_two_stage(): gathered = lax.all_gather(payload, ROW, axis=0, tiled=False)  16.5 us
    all_to_all x1, starting transfers between devices, route_two_stage(): got = lax.all_to_all(send, 'z', 0, 0, tiled=False)  12.1 us
    all_to_all x1, blocking collectives, per_device(): swapped = lax.all_to_all(partial_out, 'head', 0, 0, tiled=True)  10.5 us
    pallas_call x1, Pallas kernels, mixer(): pl.pallas_call(mixer_kernel, out_shape=(jax.ShapeDtypeStruct(s0.shape, jn...  3.65 us
  transfers between devices with their start and end apart: 1, of which 1 were waited for; matrix products, arithmetic and copies ran while one was open for 0% of the time, Pallas kernels for 0%

profile of v6, /device:TPU:6, one launch (start us, length us, event | category | flops | bytes accessed | tf_op | source)
XLA Modules:
  0.0 99.4 jit_solution(17662490991866590597)
XLA Ops:
  1.3 1.4 %shard_map.104 = bf16[5,16,512]{2,1,0:T(8,128)(2,1)} custom-call(s32[1]{0:T(128)S(6)} %copy.15.dest_ref, bf16[1,16,512]{2,1,0:T(8,128)(2,1)} %q_ref.1, bf16[1,16,512]{2,1,0:T(8,128)(2,1)} %f_ref.1, bf16[1,16,512]{2,1,0:T(8,128)(2,1)} %v_ref.1, bf16[1,16,512]{2,1,0:T(8,128)(2,1)} %g_ref.1), custom_call_target="tpu_custom_call" | custom-call | tf_op jit(solution)/shard_map/pallas_call | solution.py:31
  2.7 16.5 %all-gather = bf16[40,16,512]{2,1,0:T(8,128)(2,1)S(1)} all-gather(bf16[5,16,512]{2,1,0:T(8,128)(2,1)} %shard_map.104), channel_id=2, replica_groups=mesh['x'=4,'z'=16,'c'=2,'head'=4] {'x','c'}, dimensions={0}, use_global_device_ids=true | all-gather | bytes 737280 | tf_op jit(solution)/shard_map/all_gather | solution.py:110
  19.3 0.1 copy.14
  19.4 0.1 select_reduce_fusion
  19.5 0.6 gather_fusion
  20.1 1.1 %broadcast_select_fusion = bf16[16,4,16,512]{3,2,1,0:T(8,128)(2,1)} fusion(bf16[16,4,16,512]{3,2,1,0:T(8,128)(2,1)S(1)} %gather_fusion, pred[16]{0:T(512)(128)(4,1)S(1)} %compare_and_fusion), kind=kLoop, calls=%fused_computation.1 | loop fusion | flops 524288 | bytes 2097168 | tf_op jit(solution)/shard_map/jit(_take)/select_n | solution.py:121
  21.3 12.1 %all-to-all-start = ((bf16[16,4,16,512]{3,2,1,0:T(8,128)(2,1)}), bf16[16,4,16,512]{3,2,1,0:T(8,128)(2,1)S(1)}, u32[]{:S(2)}, u32[]{:S(2)}) async-start(bf16[16,4,16,512]{3,2,1,0:T(8,128)(2,1)} %broadcast_select_fusion), calls=%async_computation | async-start | bytes 2097152 | tf_op jit(solution)/shard_map/all_to_all | solution.py:122
  34.0 49.8 %all-to-all-done = bf16[16,4,16,512]{3,2,1,0:T(8,128)(2,1)S(1)} async-done(((bf16[16,4,16,512]{3,2,1,0:T(8,128)(2,1)}), bf16[16,4,16,512]{3,2,1,0:T(8,128)(2,1)S(1)}, u32[]{:S(2)}, u32[]{:S(2)}) %all-to-all-start) | async-done | bytes 1048608 | tf_op jit(solution)/shard_map/all_to_all | solution.py:122
  83.8 0.8 reduce_sum.21.tok_ref
  84.7 3.6 %shard_map.105 = (f32[4,128,128]{2,1,0:T(8,128)}, f32[4,16,512]{2,1,0:T(8,128)}) custom-call(s32[1]{0:T(128)S(6)} %copy.16.acc_ref, bf16[4,16,512]{2,1,0:T(8,128)(2,1)} %reduce_sum.21.tok_ref, f32[4,128,128]{2,1,0:T(8,128)} %bitcast.15, f32[1,128]{1,0:T(1,128)} %bitcast.17, bf16[512,2048]{1,0:T(8,128)(2,1)} %w_hbm.1), custom_call_target="tpu_custom_call" | custom-call | tf_op jit(solution)/shard_map/pallas_call | solution.py:95
  88.3 10.5 %all_to_all.10 = f32[4,16,512]{2,1,0:T(8,128)S(1)} all-to-all(f32[4,16,512]{2,1,0:T(8,128)} %get-tuple-element.4), channel_id=1, replica_groups=mesh['x'=4,'z'=16,'c'=2,'head'=4] {'head'}, dimensions={0} | all-to-all | bytes 262144 | tf_op jit(solution)/shard_map/all_to_all | solution.py:146
  98.8 0.6 reduce_sum.22
  (7 shorter events, 0.1 us)
Async XLA Ops:
  21.3 62.6 %all-to-all-start = ((bf16[16,4,16,512]{3,2,1,0:T(8,128)(2,1)}), bf16[16,4,16,512]{3,2,1,0:T(8,128)(2,1)S(1)}, u32[]{:S(2)}, u32[]{:S(2)}) async-start(bf16[16,4,16,512]{3,2,1,0:T(8,128)(2,1)} %broadcast_select_fusion), calls=%async_computation | async-start | bytes 2097152 | tf_op jit(solution)/shard_map/all_to_all | solution.py:122

commit v7 on v6

--- a/solution.py
+++ b/solution.py
@@ -59,12 +59,9 @@
     inv_a = jnp.exp(-lc)
     qa = q * big_a
     ba = b * inv_a
-    kept = (lax.broadcasted_iota(jnp.int32, la.shape, 0) < acc).astype(jnp.float32)
-    a_acc = jnp.exp(jnp.sum(kept * la, axis=0, keepdims=True))
-    w = kept * a_acc * ba
-    eye_r = lax.broadcasted_iota(jnp.int32, (hd, hd), 0)
-    eye_c = lax.broadcasted_iota(jnp.int32, (hd, hd), 1)
-    eye = (eye_r == eye_c).astype(jnp.float32)
+    kept_t = (lax.broadcasted_iota(jnp.int32, (la.shape[1], t_len), 1) < acc).astype(jnp.float32)
+    a_col = jnp.exp(jnp.sum(kept_t * jnp.transpose(la), axis=1, keepdims=True))
+    w_t = kept_t * a_col * jnp.transpose(ba)
     gain = gain_ref[...]
     silu_g = g * (1.0 / (1.0 + jnp.exp(-g)))
     for h in range(heads):
@@ -75,8 +72,7 @@
         scores = lax.dot_general(qa_h, ba[:, lanes], (((1,), (1,)), ((), ())),
                                  precision=HI, preferred_element_type=jnp.float32)
         o_h = _dot(qa_h, s0) + _dot(scores * causal, v_h)
-        diag = eye * a_acc[:, lanes]
-        new_ref[h] = _dot(diag, s0) + _dot(jnp.transpose(w[:, lanes]), v_h)
+        new_ref[h] = a_col[lanes] * s0 + _dot(w_t[lanes], v_h)
         meansq = jnp.mean(o_h * o_h, axis=-1, keepdims=True)
         mixed = o_h * lax.rsqrt(meansq + norm_eps) * gain * silu_g[:, lanes]
         mixed_scr[:, lanes] = mixed.astype(mixed_scr.dtype)

time: 99.9 us -> 99.8 us (level)
  no operation moved by 1% of the time
where the time goes in v7:
time: 99.8 us; the launch traced here: 99.3 us
  waiting for transfers between devices  49.8 us (50%)
  blocking collectives  27 us (27%)
  starting transfers between devices  12.1 us (12%)
  Pallas kernels  5 us (5%)
  other arithmetic  2.68 us (3%)
  between operations  1.98 us (2%)
    all_to_all x1, waiting for transfers between devices, route_two_stage(): got = lax.all_to_all(send, 'z', 0, 0, tiled=False)  49.8 us
    all_gather x1, blocking collectives, route_two_stage(): gathered = lax.all_gather(payload, ROW, axis=0, tiled=False)  16.5 us
    all_to_all x1, starting transfers between devices, route_two_stage(): got = lax.all_to_all(send, 'z', 0, 0, tiled=False)  12.1 us
    all_to_all x1, blocking collectives, per_device(): swapped = lax.all_to_all(partial_out, 'head', 0, 0, tiled=True)  10.5 us
    pallas_call x1, Pallas kernels, mixer(): pl.pallas_call(mixer_kernel, out_shape=(jax.ShapeDtypeStruct(s0.shape, jn...  3.59 us
  transfers between devices with their start and end apart: 1, of which 1 were waited for; matrix products, arithmetic and copies ran while one was open for 0% of the time, Pallas kernels for 0%

profile of v7, /device:TPU:6, one launch (start us, length us, event | category | flops | bytes accessed | tf_op | source)
XLA Modules:
  0.0 99.3 jit_solution(16509653833364201784)
XLA Ops:
  1.3 1.4 %shard_map.104 = bf16[5,16,512]{2,1,0:T(8,128)(2,1)} custom-call(s32[1]{0:T(128)S(6)} %copy.15.dest_ref, bf16[1,16,512]{2,1,0:T(8,128)(2,1)} %q_ref.1, bf16[1,16,512]{2,1,0:T(8,128)(2,1)} %f_ref.1, bf16[1,16,512]{2,1,0:T(8,128)(2,1)} %v_ref.1, bf16[1,16,512]{2,1,0:T(8,128)(2,1)} %g_ref.1), custom_call_target="tpu_custom_call" | custom-call | tf_op jit(solution)/shard_map/pallas_call | solution.py:31
  2.7 16.5 %all-gather = bf16[40,16,512]{2,1,0:T(8,128)(2,1)S(1)} all-gather(bf16[5,16,512]{2,1,0:T(8,128)(2,1)} %shard_map.104), channel_id=2, replica_groups=mesh['x'=4,'z'=16,'c'=2,'head'=4] {'x','c'}, dimensions={0}, use_global_device_ids=true | all-gather | bytes 737280 | tf_op jit(solution)/shard_map/all_gather | solution.py:106
  19.3 0.1 copy.14
  19.4 0.1 select_reduce_fusion
  19.5 0.6 gather_fusion
  20.1 1.1 %broadcast_select_fusion = bf16[16,4,16,512]{3,2,1,0:T(8,128)(2,1)} fusion(bf16[16,4,16,512]{3,2,1,0:T(8,128)(2,1)S(1)} %gather_fusion, pred[16]{0:T(512)(128)(4,1)S(1)} %compare_and_fusion), kind=kLoop, calls=%fused_computation.1 | loop fusion | flops 524288 | bytes 2097168 | tf_op jit(solution)/shard_map/jit(_take)/select_n | solution.py:117
  21.3 12.1 %all-to-all-start = ((bf16[16,4,16,512]{3,2,1,0:T(8,128)(2,1)}), bf16[16,4,16,512]{3,2,1,0:T(8,128)(2,1)S(1)}, u32[]{:S(2)}, u32[]{:S(2)}) async-start(bf16[16,4,16,512]{3,2,1,0:T(8,128)(2,1)} %broadcast_select_fusion), calls=%async_computation | async-start | bytes 2097152 | tf_op jit(solution)/shard_map/all_to_all | solution.py:118
  34.0 49.8 %all-to-all-done = bf16[16,4,16,512]{3,2,1,0:T(8,128)(2,1)S(1)} async-done(((bf16[16,4,16,512]{3,2,1,0:T(8,128)(2,1)}), bf16[16,4,16,512]{3,2,1,0:T(8,128)(2,1)S(1)}, u32[]{:S(2)}, u32[]{:S(2)}) %all-to-all-start) | async-done | bytes 1048608 | tf_op jit(solution)/shard_map/all_to_all | solution.py:118
  83.8 0.8 reduce_sum.21.tok_ref
  84.7 3.6 %shard_map.105 = (f32[4,128,128]{2,1,0:T(8,128)}, f32[4,16,512]{2,1,0:T(8,128)}) custom-call(s32[1]{0:T(128)S(6)} %copy.16.acc_ref, bf16[4,16,512]{2,1,0:T(8,128)(2,1)} %reduce_sum.21.tok_ref, f32[4,128,128]{2,1,0:T(8,128)} %bitcast.15, f32[1,128]{1,0:T(1,128)} %bitcast.17, bf16[512,2048]{1,0:T(8,128)(2,1)} %w_hbm.1), custom_call_target="tpu_custom_call" | custom-call | tf_op jit(solution)/shard_map/pallas_call | solution.py:91
  88.3 10.5 %all_to_all.10 = f32[4,16,512]{2,1,0:T(8,128)S(1)} all-to-all(f32[4,16,512]{2,1,0:T(8,128)} %get-tuple-element.4), channel_id=1, replica_groups=mesh['x'=4,'z'=16,'c'=2,'head'=4] {'head'}, dimensions={0} | all-to-all | bytes 262144 | tf_op jit(solution)/shard_map/all_to_all | solution.py:142
  98.7 0.6 reduce_sum.22
  (7 shorter events, 0.1 us)
Async XLA Ops:
  21.3 62.6 %all-to-all-start = ((bf16[16,4,16,512]{3,2,1,0:T(8,128)(2,1)}), bf16[16,4,16,512]{3,2,1,0:T(8,128)(2,1)S(1)}, u32[]{:S(2)}, u32[]{:S(2)}) async-start(bf16[16,4,16,512]{3,2,1,0:T(8,128)(2,1)} %broadcast_select_fusion), calls=%async_computation | async-start | bytes 2097152 | tf_op jit(solution)/shard_map/all_to_all | solution.py:118

commit v8 on v7

--- a/solution.py
+++ b/solution.py
@@ -9,7 +9,7 @@
 norm_eps = 1e-05
 
 ROW = ("x", "c")
-REQ = ("x", "z", "c")
+REQ = ("x", "zh", "zl", "c")
 
 
 HI = lax.Precision.HIGHEST
@@ -106,7 +106,9 @@
     gathered = lax.all_gather(payload, ROW, axis=0, tiled=False)
     dest = gathered[:, 4, 0, 0].astype(jnp.int32) - 1
     body = gathered[:, :4]
-    zn = lax.axis_size("z")
+    zh_n = lax.axis_size("zh")
+    zl_n = lax.axis_size("zl")
+    zn = zh_n * zl_n
     my_x = lax.axis_index("x")
     my_c = lax.axis_index("c")
     cn = lax.axis_size("c")
@@ -115,7 +117,10 @@
     slots = jnp.arange(count, dtype=jnp.int32)
     idx = jnp.min(jnp.where(target[:, None] == dest[None, :], slots[None, :], count), axis=1)
     send = jnp.take(body, idx, axis=0, mode="fill", fill_value=0)
-    got = lax.all_to_all(send, "z", 0, 0, tiled=False)
+    send = send.reshape((zh_n, zl_n) + send.shape[1:])
+    got = lax.all_to_all(send, "zl", 1, 1, tiled=False)
+    part = jnp.sum(got.astype(jnp.float32), axis=1).astype(jnp.bfloat16)
+    got = lax.all_to_all(part, "zh", 0, 0, tiled=False)
     return jnp.sum(got.astype(jnp.float32), axis=0).astype(jnp.bfloat16)
 
 
@@ -146,8 +151,9 @@
 
 
 def solution(mesh):
-    xs, zs, cs = 4, mesh.shape["req"] // 8, 2
-    sub = Mesh(mesh.devices.reshape(xs, zs, cs, mesh.shape["head"]), ("x", "z", "c", "head"))
+    xs, cs, zl = 4, 2, 4
+    zh = mesh.shape["req"] // (xs * cs * zl)
+    sub = Mesh(mesh.devices.reshape(xs, zh, zl, cs, mesh.shape["head"]), ("x", "zh", "zl", "c", "head"))
     placed = (
         P(REQ, None, "head"),
         P(REQ, None, "head"),

time: 99.8 us -> 96.4 us (0.966)
  waiting for transfers between devices: 49.8 us -> 17.3 us
  blocking collectives: 27 us -> 55.9 us
    all_to_all x1, waiting for transfers between devices: 49.8 us -> 17.3 us  [route_two_stage(): got = lax.all_to_all(part, 'zh', 0, 0, tiled=False)]
    all_to_all x0 -> x1, blocking collectives: none -> 28.9 us  [route_two_stage(): got = lax.all_to_all(send, 'zl', 1, 1, tiled=False)]
where the time goes in v8:
time: 96.4 us; the launch traced here: 95.9 us
  blocking collectives  55.9 us (58%)
  waiting for transfers between devices  17.3 us (18%)
  starting transfers between devices  12.3 us (13%)
  Pallas kernels  5 us (5%)
  other arithmetic  2.48 us (3%)
  between operations  1.99 us (2%)
    all_to_all x1, blocking collectives, route_two_stage(): got = lax.all_to_all(send, 'zl', 1, 1, tiled=False)  28.9 us
    all_to_all x1, waiting for transfers between devices, route_two_stage(): got = lax.all_to_all(part, 'zh', 0, 0, tiled=False)  17.3 us
    all_gather x1, blocking collectives, route_two_stage(): gathered = lax.all_gather(payload, ROW, axis=0, tiled=False)  16.5 us
    all_to_all x1, starting transfers between devices, route_two_stage(): got = lax.all_to_all(part, 'zh', 0, 0, tiled=False)  12.3 us
    all_to_all x1, blocking collectives, per_device(): swapped = lax.all_to_all(partial_out, 'head', 0, 0, tiled=True)  10.5 us
    pallas_call x1, Pallas kernels, mixer(): pl.pallas_call(mixer_kernel, out_shape=(jax.ShapeDtypeStruct(s0.shape, jn...  3.59 us
  transfers between devices with their start and end apart: 1, of which 1 were waited for; matrix products, arithmetic and copies ran while one was open for 0% of the time, Pallas kernels for 0%

profile of v8, /device:TPU:6, one launch (start us, length us, event | category | flops | bytes accessed | tf_op | source)
XLA Modules:
  0.0 95.9 jit_solution(1884039311622329008)
XLA Ops:
  1.3 1.4 %shard_map.104 = bf16[5,16,512]{2,1,0:T(8,128)(2,1)} custom-call(s32[1]{0:T(128)S(6)} %copy.19.dest_ref, bf16[1,16,512]{2,1,0:T(8,128)(2,1)} %q_ref.1, bf16[1,16,512]{2,1,0:T(8,128)(2,1)} %f_ref.1, bf16[1,16,512]{2,1,0:T(8,128)(2,1)} %v_ref.1, bf16[1,16,512]{2,1,0:T(8,128)(2,1)} %g_ref.1), custom_call_target="tpu_custom_call" | custom-call | tf_op jit(solution)/shard_map/pallas_call | solution.py:31
  2.7 16.5 %all-gather = bf16[40,16,512]{2,1,0:T(8,128)(2,1)S(1)} all-gather(bf16[5,16,512]{2,1,0:T(8,128)(2,1)} %shard_map.104), channel_id=2, replica_groups=mesh['x'=4,'zh'=4,'zl'=4,'c'=2,'head'=4] {'x','c'}, dimensions={0}, use_global_device_ids=true | all-gather | bytes 737280 | tf_op jit(solution)/shard_map/all_gather | solution.py:106
  19.3 0.1 copy.18
  19.4 0.1 select_reduce_fusion
  19.5 0.1 reduce_min.14
  19.6 0.6 gather_fusion
  20.2 0.1 broadcast_select_fusion
  20.4 0.1 copy.17
  20.4 28.9 %all_to_all.15 = bf16[4,4,4,16,512]{4,3,2,0,1:T(8,128)(2,1)S(1)} all-to-all(bf16[4,4,4,16,512]{4,3,2,0,1:T(8,128)(2,1)S(1)} %copy.17), channel_id=1, replica_groups=mesh['x'=4,'zh'=4,'zl'=4,'c'=2,'head'=4] {'zl'}, dimensions={1} | all-to-all | bytes 2097152 | tf_op jit(solution)/shard_map/all_to_all | solution.py:121
  49.4 0.9 reduce_sum.33
  50.3 12.3 %all-to-all-start.1 = ((bf16[4,4,16,512]{3,2,1,0:T(8,128)(2,1)}), bf16[4,4,16,512]{3,2,1,0:T(8,128)(2,1)S(1)}, u32[]{:S(2)}, u32[]{:S(2)}) async-start(bf16[4,4,16,512]{3,2,1,0:T(8,128)(2,1)} %reduce_sum.33), calls=%async_computation.1 | async-start | bytes 524288 | tf_op jit(solution)/shard_map/all_to_all | solution.py:123
  63.3 17.3 %all-to-all-done.1 = bf16[4,4,16,512]{3,2,1,0:T(8,128)(2,1)S(1)} async-done(((bf16[4,4,16,512]{3,2,1,0:T(8,128)(2,1)}), bf16[4,4,16,512]{3,2,1,0:T(8,128)(2,1)S(1)}, u32[]{:S(2)}, u32[]{:S(2)}) %all-to-all-start.1) | async-done | bytes 262176 | tf_op jit(solution)/shard_map/all_to_all | solution.py:123
  80.6 0.7 reduce_sum.34.tok_ref
  81.2 3.6 %shard_map.105 = (f32[4,128,128]{2,1,0:T(8,128)}, f32[4,16,512]{2,1,0:T(8,128)}) custom-call(s32[1]{0:T(128)S(6)} %copy.20.acc_ref, bf16[4,16,512]{2,1,0:T(8,128)(2,1)} %reduce_sum.34.tok_ref, f32[4,128,128]{2,1,0:T(8,128)} %bitcast.17, f32[1,128]{1,0:T(1,128)} %bitcast.19, bf16[512,2048]{1,0:T(8,128)(2,1)} %w_hbm.1), custom_call_target="tpu_custom_call" | custom-call | tf_op jit(solution)/shard_map/pallas_call | solution.py:91
  84.8 10.5 %all_to_all.16 = f32[4,16,512]{2,1,0:T(8,128)S(1)} all-to-all(f32[4,16,512]{2,1,0:T(8,128)} %get-tuple-element.4), channel_id=1, replica_groups=mesh['x'=4,'zh'=4,'zl'=4,'c'=2,'head'=4] {'head'}, dimensions={0} | all-to-all | bytes 262144 | tf_op jit(solution)/shard_map/all_to_all | solution.py:147
  95.3 0.6 reduce_sum.35
  (7 shorter events, 0.1 us)
Async XLA Ops:
  50.3 30.2 %all-to-all-start.1 = ((bf16[4,4,16,512]{3,2,1,0:T(8,128)(2,1)}), bf16[4,4,16,512]{3,2,1,0:T(8,128)(2,1)S(1)}, u32[]{:S(2)}, u32[]{:S(2)}) async-start(bf16[4,4,16,512]{3,2,1,0:T(8,128)(2,1)} %reduce_sum.33), calls=%async_computation.1 | async-start | bytes 524288 | tf_op jit(solution)/shard_map/all_to_all | solution.py:123

commit v9 on v8

--- a/solution.py
+++ b/solution.py
@@ -17,23 +17,6 @@
 
 def _dot(a, b):
     return jnp.dot(a, b, precision=HI, preferred_element_type=jnp.float32)
-
-
-def pack_kernel(dest_ref, q_ref, f_ref, v_ref, g_ref, out_ref):
-    for i, ref in enumerate((q_ref, f_ref, v_ref, g_ref)):
-        out_ref[i] = ref[0]
-    mark = jnp.broadcast_to(dest_ref[0] + 1, out_ref.shape[1:]).astype(jnp.float32)
-    out_ref[4] = mark.astype(out_ref.dtype)
-
-
-def pack(dealing, q, f, v, g):
-    vmem = pl.BlockSpec(memory_space=pltpu.VMEM)
-    return pl.pallas_call(
-        pack_kernel,
-        out_shape=jax.ShapeDtypeStruct((5,) + q.shape[1:], q.dtype),
-        in_specs=[pl.BlockSpec(memory_space=pltpu.SMEM), vmem, vmem, vmem, vmem],
-        out_specs=vmem,
-    )(dealing, q, f, v, g)
 
 
 def mixer_kernel(acc_ref, tok_ref, s0_ref, gain_ref, w_hbm, new_ref, part_ref, w_vmem, mixed_scr, sem):
@@ -102,7 +85,11 @@
 
 
 def route_two_stage(token_tuple, dealing):
-    payload = pack(dealing, *token_tuple)
+    shape = (len(token_tuple) + 1,) + token_tuple[0].shape[1:]
+    block = lax.broadcasted_iota(jnp.int32, shape, 0)
+    payload = jnp.broadcast_to((dealing[0] + 1).astype(jnp.bfloat16), shape)
+    for i, t in enumerate(token_tuple):
+        payload = jnp.where(block == i, t, payload)
     gathered = lax.all_gather(payload, ROW, axis=0, tiled=False)
     dest = gathered[:, 4, 0, 0].astype(jnp.int32) - 1
     body = gathered[:, :4]

time: 96.4 us -> 95.8 us (level)
  Pallas kernels: 5 us -> 3.59 us
  other arithmetic: 2.48 us -> 3.59 us
    pallas_call x1 -> x0, Pallas kernels: 1.41 us -> none  [pack(): pl.pallas_call(pack_kernel, out_shape=jax.ShapeDtypeStruct((5,) + q.shape...]
where the time goes in v9:
time: 95.8 us; the launch traced here: 95.3 us
  blocking collectives  55.7 us (58%)
  waiting for transfers between devices  17.3 us (18%)
  starting transfers between devices  12.4 us (13%)
  other arithmetic  3.59 us (4%)
  Pallas kernels  3.59 us (4%)
  between operations  2.02 us (2%)
    all_to_all x1, blocking collectives, route_two_stage(): got = lax.all_to_all(send, 'zl', 1, 1, tiled=False)  28.9 us
    all_to_all x1, waiting for transfers between devices, route_two_stage(): got = lax.all_to_all(part, 'zh', 0, 0, tiled=False)  17.3 us
    all_gather x1, blocking collectives, route_two_stage(): gathered = lax.all_gather(payload, ROW, axis=0, tiled=False)  16.3 us
    all_to_all x1, starting transfers between devices, route_two_stage(): got = lax.all_to_all(part, 'zh', 0, 0, tiled=False)  12.4 us
    all_to_all x1, blocking collectives, per_device(): swapped = lax.all_to_all(partial_out, 'head', 0, 0, tiled=True)  10.5 us
    pallas_call x1, Pallas kernels, mixer(): pl.pallas_call(mixer_kernel, out_shape=(jax.ShapeDtypeStruct(s0.shape, jn...  3.59 us
  transfers between devices with their start and end apart: 1, of which 1 were waited for; matrix products, arithmetic and copies ran while one was open for 0% of the time, Pallas kernels for 0%

profile of v9, /device:TPU:6, one launch (start us, length us, event | category | flops | bytes accessed | tf_op | source)
XLA Modules:
  0.0 95.3 jit_solution(13239665015815671077)
XLA Ops:
  1.3 0.9 select_select_fusion
  2.2 16.3 %all_gather.4 = bf16[8,5,16,512]{3,2,1,0:T(8,128)(2,1)S(1)} all-gather(bf16[1,5,16,512]{3,2,1,0:T(8,128)(2,1)S(1)} %select_select_fusion), channel_id=1, replica_groups=mesh['x'=4,'zh'=4,'zl'=4,'c'=2,'head'=4] {'x','c'}, dimensions={0}, use_global_device_ids=true | all-gather | bytes 737280 | tf_op jit(solution)/shard_map/all_gather | solution.py:93
  18.5 0.2 fusion.1
  18.8 0.1 select_reduce_fusion
  18.8 0.1 reduce_min.14
  18.9 0.6 gather_fusion
  19.6 0.1 broadcast_select_fusion
  19.7 0.1 copy.12
  19.8 28.9 %all_to_all.15 = bf16[4,4,4,16,512]{4,3,2,0,1:T(8,128)(2,1)S(1)} all-to-all(bf16[4,4,4,16,512]{4,3,2,0,1:T(8,128)(2,1)S(1)} %copy.12), channel_id=1, replica_groups=mesh['x'=4,'zh'=4,'zl'=4,'c'=2,'head'=4] {'zl'}, dimensions={1} | all-to-all | bytes 2097152 | tf_op jit(solution)/shard_map/all_to_all | solution.py:108
  48.7 0.9 reduce_sum.33
  49.7 12.4 %all-to-all-start.1 = ((bf16[4,4,16,512]{3,2,1,0:T(8,128)(2,1)}), bf16[4,4,16,512]{3,2,1,0:T(8,128)(2,1)S(1)}, u32[]{:S(2)}, u32[]{:S(2)}) async-start(bf16[4,4,16,512]{3,2,1,0:T(8,128)(2,1)} %reduce_sum.33), calls=%async_computation.1 | async-start | bytes 524288 | tf_op jit(solution)/shard_map/all_to_all | solution.py:110
  62.7 17.3 %all-to-all-done.1 = bf16[4,4,16,512]{3,2,1,0:T(8,128)(2,1)S(1)} async-done(((bf16[4,4,16,512]{3,2,1,0:T(8,128)(2,1)}), bf16[4,4,16,512]{3,2,1,0:T(8,128)(2,1)S(1)}, u32[]{:S(2)}, u32[]{:S(2)}) %all-to-all-start.1) | async-done | bytes 262176 | tf_op jit(solution)/shard_map/all_to_all | solution.py:110
  80.0 0.7 reduce_sum.34.tok_ref
  80.6 3.6 %shard_map.104 = (f32[4,128,128]{2,1,0:T(8,128)}, f32[4,16,512]{2,1,0:T(8,128)}) custom-call(s32[1]{0:T(128)S(6)} %copy.14.acc_ref, bf16[4,16,512]{2,1,0:T(8,128)(2,1)} %reduce_sum.34.tok_ref, f32[4,128,128]{2,1,0:T(8,128)} %bitcast.17, f32[1,128]{1,0:T(1,128)} %bitcast.23, bf16[512,2048]{1,0:T(8,128)(2,1)} %w_hbm.1), custom_call_target="tpu_custom_call" | custom-call | tf_op jit(solution)/shard_map/pallas_call | solution.py:74
  84.2 10.5 %all_to_all.16 = f32[4,16,512]{2,1,0:T(8,128)S(1)} all-to-all(f32[4,16,512]{2,1,0:T(8,128)} %get-tuple-element.4), channel_id=1, replica_groups=mesh['x'=4,'zh'=4,'zl'=4,'c'=2,'head'=4] {'head'}, dimensions={0} | all-to-all | bytes 262144 | tf_op jit(solution)/shard_map/all_to_all | solution.py:134
  94.7 0.6 reduce_sum.35
  (7 shorter events, 0.1 us)
Async XLA Ops:
  49.7 30.3 %all-to-all-start.1 = ((bf16[4,4,16,512]{3,2,1,0:T(8,128)(2,1)}), bf16[4,4,16,512]{3,2,1,0:T(8,128)(2,1)S(1)}, u32[]{:S(2)}, u32[]{:S(2)}) async-start(bf16[4,4,16,512]{3,2,1,0:T(8,128)(2,1)} %reduce_sum.33), calls=%async_computation.1 | async-start | bytes 524288 | tf_op jit(solution)/shard_map/all_to_all | solution.py:110

commit v10 on v9

--- a/solution.py
+++ b/solution.py
@@ -19,10 +19,9 @@
     return jnp.dot(a, b, precision=HI, preferred_element_type=jnp.float32)
 
 
-def mixer_kernel(acc_ref, tok_ref, s0_ref, gain_ref, w_hbm, new_ref, part_ref, w_vmem, mixed_scr, sem):
+def mixer_kernel(tok_ref, s0_ref, gain_ref, w_hbm, part_ref, w_vmem, mixed_scr, sem):
     w_copy = pltpu.make_async_copy(w_hbm, w_vmem, sem)
     w_copy.start()
-    acc = acc_ref[0]
     blocks = tok_ref[...].astype(jnp.float32)
     heads = s0_ref.shape[0]
     hd = s0_ref.shape[2]
@@ -42,9 +41,6 @@
     inv_a = jnp.exp(-lc)
     qa = q * big_a
     ba = b * inv_a
-    kept_t = (lax.broadcasted_iota(jnp.int32, (la.shape[1], t_len), 1) < acc).astype(jnp.float32)
-    a_col = jnp.exp(jnp.sum(kept_t * jnp.transpose(la), axis=1, keepdims=True))
-    w_t = kept_t * a_col * jnp.transpose(ba)
     gain = gain_ref[...]
     silu_g = g * (1.0 / (1.0 + jnp.exp(-g)))
     for h in range(heads):
@@ -55,7 +51,6 @@
         scores = lax.dot_general(qa_h, ba[:, lanes], (((1,), (1,)), ((), ())),
                                  precision=HI, preferred_element_type=jnp.float32)
         o_h = _dot(qa_h, s0) + _dot(scores * causal, v_h)
-        new_ref[h] = a_col[lanes] * s0 + _dot(w_t[lanes], v_h)
         meansq = jnp.mean(o_h * o_h, axis=-1, keepdims=True)
         mixed = o_h * lax.rsqrt(meansq + norm_eps) * gain * silu_g[:, lanes]
         mixed_scr[:, lanes] = mixed.astype(mixed_scr.dtype)
@@ -67,21 +62,51 @@
                               preferred_element_type=jnp.float32)
 
 
-def mixer(acc, tok, s0, gain, weight, parts):
+def state_kernel(acc_ref, tok_ref, s0_ref, new_ref):
+    acc = acc_ref[0]
+    fl = tok_ref[1].astype(jnp.float32)
+    v = tok_ref[2].astype(jnp.float32)
+    t_len = fl.shape[0]
+    hd = s0_ref.shape[2]
+    a = lower_bound + (1.0 - lower_bound) * (1.0 / (1.0 + jnp.exp(-fl)))
+    b = 1.0 - a
+    la = jnp.log(a)
+    row = lax.broadcasted_iota(jnp.int32, (t_len, t_len), 0)
+    col = lax.broadcasted_iota(jnp.int32, (t_len, t_len), 1)
+    causal = (col <= row).astype(jnp.float32)
+    inv_a = jnp.exp(-_dot(causal, la))
+    ba = b * inv_a
+    kept_t = (lax.broadcasted_iota(jnp.int32, (la.shape[1], t_len), 1) < acc).astype(jnp.float32)
+    a_col = jnp.exp(jnp.sum(kept_t * jnp.transpose(la), axis=1, keepdims=True))
+    w_t = kept_t * a_col * jnp.transpose(ba)
+    for h in range(s0_ref.shape[0]):
+        lanes = slice(h * hd, (h + 1) * hd)
+        new_ref[h] = a_col[lanes] * s0_ref[h] + _dot(w_t[lanes], v[:, lanes])
+
+
+def new_state(acc, tok, s0):
+    vmem = pl.BlockSpec(memory_space=pltpu.VMEM)
+    return pl.pallas_call(
+        state_kernel,
+        out_shape=jax.ShapeDtypeStruct(s0.shape, jnp.float32),
+        in_specs=[pl.BlockSpec(memory_space=pltpu.SMEM), vmem, vmem],
+        out_specs=vmem,
+    )(acc, tok, s0)
+
+
+def mixer(tok, s0, gain, weight, parts):
     heads, hd = s0.shape[0], s0.shape[2]
     t_len = tok.shape[1]
     vmem = pl.BlockSpec(memory_space=pltpu.VMEM)
     return pl.pallas_call(
         mixer_kernel,
-        out_shape=(jax.ShapeDtypeStruct(s0.shape, jnp.float32),
-                   jax.ShapeDtypeStruct((parts, t_len, weight.shape[1] // parts), jnp.float32)),
-        in_specs=[pl.BlockSpec(memory_space=pltpu.SMEM), vmem, vmem, vmem,
-                  pl.BlockSpec(memory_space=pl.ANY)],
-        out_specs=(vmem, vmem),
+        out_shape=jax.ShapeDtypeStruct((parts, t_len, weight.shape[1] // parts), jnp.float32),
+        in_specs=[vmem, vmem, vmem, pl.BlockSpec(memory_space=pl.ANY)],
+        out_specs=vmem,
         scratch_shapes=[pltpu.VMEM(weight.shape, weight.dtype),
                         pltpu.VMEM((t_len, heads * hd), jnp.bfloat16),
                         pltpu.SemaphoreType.DMA(())],
-    )(acc, tok, s0, gain, weight)
+    )(tok, s0, gain, weight)
 
 
 def route_two_stage(token_tuple, dealing):
@@ -129,8 +154,8 @@
     token_tuple = (queries, forget_logits, values, gate_input)
     got = route_two_stage(token_tuple, dealing)
     hn = lax.axis_size("head")
-    new_states, partial_out = mixer(accepted, got, init_states[0], norm_gain.reshape(1, head_size), out_weight, hn)
-    new_states = new_states[None]
+    partial_out = mixer(got, init_states[0], norm_gain.reshape(1, head_size), out_weight, hn)
+    new_states = new_state(accepted, got, init_states[0])[None]
     swapped = lax.all_to_all(partial_out, "head", 0, 0, tiled=True)
     summed = jnp.sum(swapped, axis=0)
     verified = summed.astype(jnp.bfloat16).reshape(local_count, draft_len, summed.shape[1])

time: 95.8 us -> 96.4 us (level); the launches traced: 95.3 us -> 94.6 us
  blocking collectives: 55.7 us -> 75.6 us
  waiting for transfers between devices: 17.3 us -> 3 us
  starting transfers between devices: 12.4 us -> 4.48 us
  Pallas kernels: 3.59 us -> 5.9 us
    all_to_all x1, blocking collectives: 10.5 us -> 30.4 us  [route_two_stage(): got = lax.all_to_all(part, 'zh', 0, 0, tiled=False)]
    all_to_all x1, waiting for transfers between devices: 17.3 us -> 3 us  [per_device(): swapped = lax.all_to_all(partial_out, 'head', 0, 0, tiled=True)]
    all_to_all x1, starting transfers between devices: 12.4 us -> 4.48 us  [per_device(): swapped = lax.all_to_all(partial_out, 'head', 0, 0, tiled=True)]
    pallas_call x1 -> x2, Pallas kernels: 3.59 us -> 5.9 us  [the longest x1 3.57 us: mixer(): pl.pallas_call(mixer_kernel, out_shape=jax.ShapeDtypeStruct((parts, t_len...]
  transfers between devices with their start and end apart: 1 -> 1, of which waited for: 1 -> 1; matrix products, arithmetic and copies ran while one was open for 0% -> 0% of each run, Pallas kernels for 0% -> 2%
where the time goes in v10:
time: 96.4 us; the launch traced here: 94.6 us
  blocking collectives  75.6 us (78%)
  Pallas kernels  5.9 us (6%)
  starting transfers between devices  4.48 us (5%)
  waiting for transfers between devices  3 us (3%)
  other arithmetic  2.85 us (3%)
  between operations  2.03 us (2%)
    all_to_all x1, blocking collectives, route_two_stage(): got = lax.all_to_all(part, 'zh', 0, 0, tiled=False)  30.4 us
    all_to_all x1, blocking collectives, route_two_stage(): got = lax.all_to_all(send, 'zl', 1, 1, tiled=False)  28.9 us
    all_gather x1, blocking collectives, route_two_stage(): gathered = lax.all_gather(payload, ROW, axis=0, tiled=False)  16.3 us
    all_to_all x1, starting transfers between devices, per_device(): swapped = lax.all_to_all(partial_out, 'head', 0, 0, tiled=True)  4.48 us
    pallas_call x1, Pallas kernels, mixer(): pl.pallas_call(mixer_kernel, out_shape=jax.ShapeDtypeStruct((parts, t_len...  3.57 us
    all_to_all x1, waiting for transfers between devices, per_device(): swapped = lax.all_to_all(partial_out, 'head', 0, 0, tiled=True)  3 us
    pallas_call x1, Pallas kernels, new_state(): pl.pallas_call(state_kernel, out_shape=jax.ShapeDtypeStruct(s0.shape, jnp...  2.33 us
  transfers between devices with their start and end apart: 1, of which 1 were waited for; matrix products, arithmetic and copies ran while one was open for 0% of the time, Pallas kernels for 2%

profile of v10, /device:TPU:6, one launch (start us, length us, event | category | flops | bytes accessed | tf_op | source)
XLA Modules:
  0.0 94.6 jit_solution(4039249186351678558)
XLA Ops:
  1.3 0.9 select_select_fusion
  2.2 16.3 %all_gather.4 = bf16[8,5,16,512]{3,2,1,0:T(8,128)(2,1)S(1)} all-gather(bf16[1,5,16,512]{3,2,1,0:T(8,128)(2,1)S(1)} %select_select_fusion), channel_id=1, replica_groups=mesh['x'=4,'zh'=4,'zl'=4,'c'=2,'head'=4] {'x','c'}, dimensions={0}, use_global_device_ids=true | all-gather | bytes 737280 | tf_op jit(solution)/shard_map/all_gather | solution.py:118
  18.5 0.2 fusion.1
  18.8 0.1 select_reduce_fusion
  18.8 0.1 reduce_min.14
  18.9 0.6 gather_fusion
  19.6 0.1 broadcast_select_fusion
  19.7 0.1 copy.12
  19.8 28.9 %all_to_all.15 = bf16[4,4,4,16,512]{4,3,2,0,1:T(8,128)(2,1)S(1)} all-to-all(bf16[4,4,4,16,512]{4,3,2,0,1:T(8,128)(2,1)S(1)} %copy.12), channel_id=1, replica_groups=mesh['x'=4,'zh'=4,'zl'=4,'c'=2,'head'=4] {'zl'}, dimensions={1} | all-to-all | bytes 2097152 | tf_op jit(solution)/shard_map/all_to_all | solution.py:133
  48.7 0.2 reduce_sum.33
  48.9 30.4 %all_to_all.16 = bf16[4,4,16,512]{3,2,1,0:T(8,128)(2,1)S(1)} all-to-all(bf16[4,4,16,512]{3,2,1,0:T(8,128)(2,1)S(1)} %reduce_sum.33), channel_id=1, replica_groups=mesh['x'=4,'zh'=4,'zl'=4,'c'=2,'head'=4] {'zh'}, dimensions={0} | all-to-all | bytes 524288 | tf_op jit(solution)/shard_map/all_to_all | solution.py:135
  79.3 0.7 reduce_sum.34.tok_ref
  80.0 3.6 %shard_map.104 = f32[4,16,512]{2,1,0:T(8,128)} custom-call(bf16[4,16,512]{2,1,0:T(8,128)(2,1)} %reduce_sum.34.tok_ref, f32[4,128,128]{2,1,0:T(8,128)} %bitcast.17, f32[1,128]{1,0:T(1,128)} %bitcast.25, bf16[512,2048]{1,0:T(8,128)(2,1)} %w_hbm.1), custom_call_target="tpu_custom_call" | custom-call | tf_op jit(solution)/shard_map/pallas_call | solution.py:101
  83.5 4.5 %all-to-all-start.2 = ((f32[4,16,512]{2,1,0:T(8,128)}), f32[4,16,512]{2,1,0:T(8,128)S(1)}, u32[]{:S(2)}, u32[]{:S(2)}) async-start(f32[4,16,512]{2,1,0:T(8,128)} %shard_map.104), calls=%async_computation.2 | async-start | bytes 262144 | tf_op jit(solution)/shard_map/all_to_all | solution.py:159
  88.7 2.3 %shard_map.105 = f32[4,128,128]{2,1,0:T(8,128)} custom-call(s32[1]{0:T(128)S(6)} %copy.14.acc_ref, bf16[4,16,512]{2,1,0:T(8,128)(2,1)} %reduce_sum.34.tok_ref, f32[4,128,128]{2,1,0:T(8,128)} %bitcast.18), custom_call_target="tpu_custom_call" | custom-call | tf_op jit(solution)/shard_map/pallas_call | solution.py:89
  91.0 3.0 %all-to-all-done.2 = f32[4,16,512]{2,1,0:T(8,128)S(1)} async-done(((f32[4,16,512]{2,1,0:T(8,128)}), f32[4,16,512]{2,1,0:T(8,128)S(1)}, u32[]{:S(2)}, u32[]{:S(2)}) %all-to-all-start.2) | async-done | bytes 131104 | tf_op jit(solution)/shard_map/all_to_all | solution.py:159
  94.0 0.6 reduce_sum.35
  (7 shorter events, 0.1 us)
Async XLA Ops:
  83.5 10.5 %all-to-all-start.2 = ((f32[4,16,512]{2,1,0:T(8,128)}), f32[4,16,512]{2,1,0:T(8,128)S(1)}, u32[]{:S(2)}, u32[]{:S(2)}) async-start(f32[4,16,512]{2,1,0:T(8,128)} %shard_map.104), calls=%async_computation.2 | async-start | bytes 262144 | tf_op jit(solution)/shard_map/all_to_all | solution.py:159

commit v11 on v9

--- a/solution.py
+++ b/solution.py
@@ -26,10 +26,11 @@
     blocks = tok_ref[...].astype(jnp.float32)
     heads = s0_ref.shape[0]
     hd = s0_ref.shape[2]
-    q = blocks[0]
-    fl = blocks[1]
-    v = blocks[2]
-    g = blocks[3]
+    width = heads * hd
+    q = blocks[:, 0:width]
+    fl = blocks[:, width:2 * width]
+    v = blocks[:, 2 * width:3 * width]
+    g = blocks[:, 3 * width:4 * width]
     t_len = q.shape[0]
     a = lower_bound + (1.0 - lower_bound) * (1.0 / (1.0 + jnp.exp(-fl)))
     b = 1.0 - a
@@ -69,7 +70,7 @@
 
 def mixer(acc, tok, s0, gain, weight, parts):
     heads, hd = s0.shape[0], s0.shape[2]
-    t_len = tok.shape[1]
+    t_len = tok.shape[0]
     vmem = pl.BlockSpec(memory_space=pltpu.VMEM)
     return pl.pallas_call(
         mixer_kernel,
@@ -85,14 +86,18 @@
 
 
 def route_two_stage(token_tuple, dealing):
-    shape = (len(token_tuple) + 1,) + token_tuple[0].shape[1:]
-    block = lax.broadcasted_iota(jnp.int32, shape, 0)
-    payload = jnp.broadcast_to((dealing[0] + 1).astype(jnp.bfloat16), shape)
+    rows, width = token_tuple[0].shape[1:]
+    wide = width * len(token_tuple)
+    total = wide + 128
+    lane = lax.broadcasted_iota(jnp.int32, (rows, total), 1)
+    payload = jnp.broadcast_to((dealing[0] + 1).astype(jnp.bfloat16), (rows, total))
     for i, t in enumerate(token_tuple):
-        payload = jnp.where(block == i, t, payload)
+        placed = jnp.pad(t[0], ((0, 0), (i * width, total - (i + 1) * width)))
+        inside = (lane >= i * width) & (lane < (i + 1) * width)
+        payload = jnp.where(inside, placed, payload)
     gathered = lax.all_gather(payload, ROW, axis=0, tiled=False)
-    dest = gathered[:, 4, 0, 0].astype(jnp.int32) - 1
-    body = gathered[:, :4]
+    dest = gathered[:, 0, wide].astype(jnp.int32) - 1
+    body = gathered[:, :, :wide]
     zh_n = lax.axis_size("zh")
     zl_n = lax.axis_size("zl")
     zn = zh_n * zl_n

time: 95.8 us -> 95.5 us (level)
  no operation moved by 1% of the time
where the time goes in v11:
time: 95.5 us; the launch traced here: 95 us
  blocking collectives  55.5 us (58%)
  waiting for transfers between devices  17.3 us (18%)
  starting transfers between devices  12.4 us (13%)
  Pallas kernels  3.59 us (4%)
  other arithmetic  3.29 us (3%)
  between operations  2.01 us (2%)
    all_to_all x1, blocking collectives, route_two_stage(): got = lax.all_to_all(send, 'zl', 1, 1, tiled=False)  29.1 us
    all_to_all x1, waiting for transfers between devices, route_two_stage(): got = lax.all_to_all(part, 'zh', 0, 0, tiled=False)  17.3 us
    all_gather x1, blocking collectives, route_two_stage(): gathered = lax.all_gather(payload, ROW, axis=0, tiled=False)  15.9 us
    all_to_all x1, starting transfers between devices, route_two_stage(): got = lax.all_to_all(part, 'zh', 0, 0, tiled=False)  12.4 us
    all_to_all x1, blocking collectives, per_device(): swapped = lax.all_to_all(partial_out, 'head', 0, 0, tiled=True)  10.5 us
    pallas_call x1, Pallas kernels, mixer(): pl.pallas_call(mixer_kernel, out_shape=(jax.ShapeDtypeStruct(s0.shape, jn...  3.59 us
  transfers between devices with their start and end apart: 1, of which 1 were waited for; matrix products, arithmetic and copies ran while one was open for 0% of the time, Pallas kernels for 0%

profile of v11, /device:TPU:6, one launch (start us, length us, event | category | flops | bytes accessed | tf_op | source)
XLA Modules:
  0.0 95.0 jit_solution(11465835875233712357)
XLA Ops:
  1.3 0.8 select_select_fusion
  2.1 15.9 %all-gather = bf16[128,2176]{1,0:T(8,128)(2,1)S(1)} all-gather(bf16[16,2176]{1,0:T(8,128)(2,1)S(1)} %select_select_fusion), channel_id=2, replica_groups=mesh['x'=4,'zh'=4,'zl'=4,'c'=2,'head'=4] {'x','c'}, dimensions={0}, use_global_device_ids=true | all-gather | bytes 626688 | tf_op jit(solution)/shard_map/all_gather | solution.py:98
  18.1 0.1 copy.18
  18.2 0.1 select_reduce_fusion
  18.3 0.1 reduce_min.14
  18.4 0.6 gather_fusion
  19.1 0.1 broadcast_select_fusion
  19.2 0.1 copy.17
  19.3 29.1 %all_to_all.15 = bf16[4,4,16,2048]{3,2,0,1:T(8,128)(2,1)S(1)} all-to-all(bf16[4,4,16,2048]{3,2,0,1:T(8,128)(2,1)S(1)} %copy.17), channel_id=1, replica_groups=mesh['x'=4,'zh'=4,'zl'=4,'c'=2,'head'=4] {'zl'}, dimensions={1} | all-to-all | bytes 2097152 | tf_op jit(solution)/shard_map/all_to_all | solution.py:113
  48.4 0.9 reduce_sum.33
  49.3 12.4 %all-to-all-start.1 = ((bf16[4,16,2048]{2,1,0:T(8,128)(2,1)}), bf16[4,16,2048]{2,1,0:T(8,128)(2,1)S(1)}, u32[]{:S(2)}, u32[]{:S(2)}) async-start(bf16[4,16,2048]{2,1,0:T(8,128)(2,1)} %reduce_sum.33), calls=%async_computation.1 | async-start | bytes 524288 | tf_op jit(solution)/shard_map/all_to_all | solution.py:115
  62.4 17.3 %all-to-all-done.1 = bf16[4,16,2048]{2,1,0:T(8,128)(2,1)S(1)} async-done(((bf16[4,16,2048]{2,1,0:T(8,128)(2,1)}), bf16[4,16,2048]{2,1,0:T(8,128)(2,1)S(1)}, u32[]{:S(2)}, u32[]{:S(2)}) %all-to-all-start.1) | async-done | bytes 262176 | tf_op jit(solution)/shard_map/all_to_all | solution.py:115
  79.7 0.7 reduce_sum.34.tok_ref
  80.3 3.6 %shard_map.104 = (f32[4,128,128]{2,1,0:T(8,128)}, f32[4,16,512]{2,1,0:T(8,128)}) custom-call(s32[1]{0:T(128)S(6)} %copy.20.acc_ref, bf16[16,2048]{1,0:T(8,128)(2,1)} %reduce_sum.34.tok_ref, f32[4,128,128]{2,1,0:T(8,128)} %bitcast.22, f32[1,128]{1,0:T(1,128)} %bitcast.28, bf16[512,2048]{1,0:T(8,128)(2,1)} %w_hbm.1), custom_call_target="tpu_custom_call" | custom-call | tf_op jit(solution)/shard_map/pallas_call | solution.py:75
  83.9 10.5 %all_to_all.16 = f32[4,16,512]{2,1,0:T(8,128)S(1)} all-to-all(f32[4,16,512]{2,1,0:T(8,128)} %get-tuple-element.4), channel_id=1, replica_groups=mesh['x'=4,'zh'=4,'zl'=4,'c'=2,'head'=4] {'head'}, dimensions={0} | all-to-all | bytes 262144 | tf_op jit(solution)/shard_map/all_to_all | solution.py:139
  94.4 0.6 reduce_sum.35
  (9 shorter events, 0.1 us)
Async XLA Ops:
  49.3 30.3 %all-to-all-start.1 = ((bf16[4,16,2048]{2,1,0:T(8,128)(2,1)}), bf16[4,16,2048]{2,1,0:T(8,128)(2,1)S(1)}, u32[]{:S(2)}, u32[]{:S(2)}) async-start(bf16[4,16,2048]{2,1,0:T(8,128)(2,1)} %reduce_sum.33), calls=%async_computation.1 | async-start | bytes 524288 | tf_op jit(solution)/shard_map/all_to_all | solution.py:115

commit v12 on v11

--- a/solution.py
+++ b/solution.py
@@ -12,7 +12,7 @@
 REQ = ("x", "zh", "zl", "c")
 
 
-HI = lax.Precision.HIGHEST
+HI = lax.Precision.HIGH
 
 
 def _dot(a, b):

time: 95.5 us -> 95.5 us (level)
  no operation moved by 1% of the time
where the time goes in v12:
time: 95.5 us; the launch traced here: 95 us
  blocking collectives  55.5 us (58%)
  waiting for transfers between devices  17.3 us (18%)
  starting transfers between devices  12.4 us (13%)
  Pallas kernels  3.58 us (4%)
  other arithmetic  3.29 us (3%)
  between operations  2.01 us (2%)
    all_to_all x1, blocking collectives, route_two_stage(): got = lax.all_to_all(send, 'zl', 1, 1, tiled=False)  29.1 us
    all_to_all x1, waiting for transfers between devices, route_two_stage(): got = lax.all_to_all(part, 'zh', 0, 0, tiled=False)  17.3 us
    all_gather x1, blocking collectives, route_two_stage(): gathered = lax.all_gather(payload, ROW, axis=0, tiled=False)  15.9 us
    all_to_all x1, starting transfers between devices, route_two_stage(): got = lax.all_to_all(part, 'zh', 0, 0, tiled=False)  12.4 us
    all_to_all x1, blocking collectives, per_device(): swapped = lax.all_to_all(partial_out, 'head', 0, 0, tiled=True)  10.5 us
    pallas_call x1, Pallas kernels, mixer(): pl.pallas_call(mixer_kernel, out_shape=(jax.ShapeDtypeStruct(s0.shape, jn...  3.58 us
  transfers between devices with their start and end apart: 1, of which 1 were waited for; matrix products, arithmetic and copies ran while one was open for 0% of the time, Pallas kernels for 0%

profile of v12, /device:TPU:6, one launch (start us, length us, event | category | flops | bytes accessed | tf_op | source)
XLA Modules:
  0.0 95.0 jit_solution(14529261130646834631)
XLA Ops:
  1.3 0.8 select_select_fusion
  2.1 15.9 %all-gather = bf16[128,2176]{1,0:T(8,128)(2,1)S(1)} all-gather(bf16[16,2176]{1,0:T(8,128)(2,1)S(1)} %select_select_fusion), channel_id=2, replica_groups=mesh['x'=4,'zh'=4,'zl'=4,'c'=2,'head'=4] {'x','c'}, dimensions={0}, use_global_device_ids=true | all-gather | bytes 626688 | tf_op jit(solution)/shard_map/all_gather | solution.py:98
  18.1 0.1 copy.18
  18.2 0.1 select_reduce_fusion
  18.3 0.1 reduce_min.14
  18.4 0.6 gather_fusion
  19.1 0.1 broadcast_select_fusion
  19.2 0.1 copy.17
  19.3 29.1 %all_to_all.15 = bf16[4,4,16,2048]{3,2,0,1:T(8,128)(2,1)S(1)} all-to-all(bf16[4,4,16,2048]{3,2,0,1:T(8,128)(2,1)S(1)} %copy.17), channel_id=1, replica_groups=mesh['x'=4,'zh'=4,'zl'=4,'c'=2,'head'=4] {'zl'}, dimensions={1} | all-to-all | bytes 2097152 | tf_op jit(solution)/shard_map/all_to_all | solution.py:113
  48.4 0.9 reduce_sum.33
  49.3 12.4 %all-to-all-start.1 = ((bf16[4,16,2048]{2,1,0:T(8,128)(2,1)}), bf16[4,16,2048]{2,1,0:T(8,128)(2,1)S(1)}, u32[]{:S(2)}, u32[]{:S(2)}) async-start(bf16[4,16,2048]{2,1,0:T(8,128)(2,1)} %reduce_sum.33), calls=%async_computation.1 | async-start | bytes 524288 | tf_op jit(solution)/shard_map/all_to_all | solution.py:115
  62.4 17.3 %all-to-all-done.1 = bf16[4,16,2048]{2,1,0:T(8,128)(2,1)S(1)} async-done(((bf16[4,16,2048]{2,1,0:T(8,128)(2,1)}), bf16[4,16,2048]{2,1,0:T(8,128)(2,1)S(1)}, u32[]{:S(2)}, u32[]{:S(2)}) %all-to-all-start.1) | async-done | bytes 262176 | tf_op jit(solution)/shard_map/all_to_all | solution.py:115
  79.7 0.7 reduce_sum.34.tok_ref
  80.3 3.6 %shard_map.104 = (f32[4,128,128]{2,1,0:T(8,128)}, f32[4,16,512]{2,1,0:T(8,128)}) custom-call(s32[1]{0:T(128)S(6)} %copy.20.acc_ref, bf16[16,2048]{1,0:T(8,128)(2,1)} %reduce_sum.34.tok_ref, f32[4,128,128]{2,1,0:T(8,128)} %bitcast.22, f32[1,128]{1,0:T(1,128)} %bitcast.28, bf16[512,2048]{1,0:T(8,128)(2,1)} %w_hbm.1), custom_call_target="tpu_custom_call" | custom-call | tf_op jit(solution)/shard_map/pallas_call | solution.py:75
  83.9 10.5 %all_to_all.16 = f32[4,16,512]{2,1,0:T(8,128)S(1)} all-to-all(f32[4,16,512]{2,1,0:T(8,128)} %get-tuple-element.4), channel_id=1, replica_groups=mesh['x'=4,'zh'=4,'zl'=4,'c'=2,'head'=4] {'head'}, dimensions={0} | all-to-all | bytes 262144 | tf_op jit(solution)/shard_map/all_to_all | solution.py:139
  94.4 0.6 reduce_sum.35
  (9 shorter events, 0.1 us)
Async XLA Ops:
  49.3 30.3 %all-to-all-start.1 = ((bf16[4,16,2048]{2,1,0:T(8,128)(2,1)}), bf16[4,16,2048]{2,1,0:T(8,128)(2,1)S(1)}, u32[]{:S(2)}, u32[]{:S(2)}) async-start(bf16[4,16,2048]{2,1,0:T(8,128)(2,1)} %reduce_sum.33), calls=%async_computation.1 | async-start | bytes 524288 | tf_op jit(solution)/shard_map/all_to_all | solution.py:115

commit v13 on v11

--- a/solution.py
+++ b/solution.py
@@ -20,8 +20,13 @@
 
 
 def mixer_kernel(acc_ref, tok_ref, s0_ref, gain_ref, w_hbm, new_ref, part_ref, w_vmem, mixed_scr, sem):
-    w_copy = pltpu.make_async_copy(w_hbm, w_vmem, sem)
-    w_copy.start()
+    pieces = sem.shape[0]
+    step = w_hbm.shape[0] // pieces
+    w_copies = []
+    for j in range(pieces):
+        rows = pl.ds(j * step, step)
+        w_copies.append(pltpu.make_async_copy(w_hbm.at[rows], w_vmem.at[rows], sem.at[j]))
+        w_copies[-1].start()
     acc = acc_ref[0]
     blocks = tok_ref[...].astype(jnp.float32)
     heads = s0_ref.shape[0]
@@ -60,7 +65,8 @@
         meansq = jnp.mean(o_h * o_h, axis=-1, keepdims=True)
         mixed = o_h * lax.rsqrt(meansq + norm_eps) * gain * silu_g[:, lanes]
         mixed_scr[:, lanes] = mixed.astype(mixed_scr.dtype)
-    w_copy.wait()
+    for w_copy in w_copies:
+        w_copy.wait()
     chunk = part_ref.shape[2]
     mixed_all = mixed_scr[...]
     for j in range(part_ref.shape[0]):
@@ -81,7 +87,7 @@
         out_specs=(vmem, vmem),
         scratch_shapes=[pltpu.VMEM(weight.shape, weight.dtype),
                         pltpu.VMEM((t_len, heads * hd), jnp.bfloat16),
-                        pltpu.SemaphoreType.DMA(())],
+                        pltpu.SemaphoreType.DMA((4,))],
     )(acc, tok, s0, gain, weight)
 
 

time: 95.5 us -> 95.5 us (level)
  no operation moved by 1% of the time
where the time goes in v13:
time: 95.5 us; the launch traced here: 95 us
  blocking collectives  55.5 us (58%)
  waiting for transfers between devices  17.3 us (18%)
  starting transfers between devices  12.4 us (13%)
  Pallas kernels  3.57 us (4%)
  other arithmetic  3.29 us (3%)
  between operations  2.01 us (2%)
    all_to_all x1, blocking collectives, route_two_stage(): got = lax.all_to_all(send, 'zl', 1, 1, tiled=False)  29.1 us
    all_to_all x1, waiting for transfers between devices, route_two_stage(): got = lax.all_to_all(part, 'zh', 0, 0, tiled=False)  17.3 us
    all_gather x1, blocking collectives, route_two_stage(): gathered = lax.all_gather(payload, ROW, axis=0, tiled=False)  15.9 us
    all_to_all x1, starting transfers between devices, route_two_stage(): got = lax.all_to_all(part, 'zh', 0, 0, tiled=False)  12.4 us
    all_to_all x1, blocking collectives, per_device(): swapped = lax.all_to_all(partial_out, 'head', 0, 0, tiled=True)  10.5 us
    pallas_call x1, Pallas kernels, mixer(): pl.pallas_call(mixer_kernel, out_shape=(jax.ShapeDtypeStruct(s0.shape, jn...  3.57 us
  transfers between devices with their start and end apart: 1, of which 1 were waited for; matrix products, arithmetic and copies ran while one was open for 0% of the time, Pallas kernels for 0%

profile of v13, /device:TPU:6, one launch (start us, length us, event | category | flops | bytes accessed | tf_op | source)
XLA Modules:
  0.0 95.0 jit_solution(2061467209948360341)
XLA Ops:
  1.3 0.8 select_select_fusion
  2.1 15.9 %all-gather = bf16[128,2176]{1,0:T(8,128)(2,1)S(1)} all-gather(bf16[16,2176]{1,0:T(8,128)(2,1)S(1)} %select_select_fusion), channel_id=2, replica_groups=mesh['x'=4,'zh'=4,'zl'=4,'c'=2,'head'=4] {'x','c'}, dimensions={0}, use_global_device_ids=true | all-gather | bytes 626688 | tf_op jit(solution)/shard_map/all_gather | solution.py:104
  18.1 0.1 copy.18
  18.2 0.1 select_reduce_fusion
  18.3 0.1 reduce_min.14
  18.4 0.6 gather_fusion
  19.1 0.1 broadcast_select_fusion
  19.2 0.1 copy.17
  19.3 29.1 %all_to_all.15 = bf16[4,4,16,2048]{3,2,0,1:T(8,128)(2,1)S(1)} all-to-all(bf16[4,4,16,2048]{3,2,0,1:T(8,128)(2,1)S(1)} %copy.17), channel_id=1, replica_groups=mesh['x'=4,'zh'=4,'zl'=4,'c'=2,'head'=4] {'zl'}, dimensions={1} | all-to-all | bytes 2097152 | tf_op jit(solution)/shard_map/all_to_all | solution.py:119
  48.4 0.9 reduce_sum.33
  49.3 12.4 %all-to-all-start.1 = ((bf16[4,16,2048]{2,1,0:T(8,128)(2,1)}), bf16[4,16,2048]{2,1,0:T(8,128)(2,1)S(1)}, u32[]{:S(2)}, u32[]{:S(2)}) async-start(bf16[4,16,2048]{2,1,0:T(8,128)(2,1)} %reduce_sum.33), calls=%async_computation.1 | async-start | bytes 524288 | tf_op jit(solution)/shard_map/all_to_all | solution.py:121
  62.4 17.3 %all-to-all-done.1 = bf16[4,16,2048]{2,1,0:T(8,128)(2,1)S(1)} async-done(((bf16[4,16,2048]{2,1,0:T(8,128)(2,1)}), bf16[4,16,2048]{2,1,0:T(8,128)(2,1)S(1)}, u32[]{:S(2)}, u32[]{:S(2)}) %all-to-all-start.1) | async-done | bytes 262176 | tf_op jit(solution)/shard_map/all_to_all | solution.py:121
  79.7 0.7 reduce_sum.34.tok_ref
  80.3 3.6 %shard_map.104 = (f32[4,128,128]{2,1,0:T(8,128)}, f32[4,16,512]{2,1,0:T(8,128)}) custom-call(s32[1]{0:T(128)S(6)} %copy.20.acc_ref, bf16[16,2048]{1,0:T(8,128)(2,1)} %reduce_sum.34.tok_ref, f32[4,128,128]{2,1,0:T(8,128)} %bitcast.22, f32[1,128]{1,0:T(1,128)} %bitcast.28, bf16[512,2048]{1,0:T(8,128)(2,1)} %w_hbm.1), custom_call_target="tpu_custom_call" | custom-call | tf_op jit(solution)/shard_map/pallas_call | solution.py:81
  83.9 10.5 %all_to_all.16 = f32[4,16,512]{2,1,0:T(8,128)S(1)} all-to-all(f32[4,16,512]{2,1,0:T(8,128)} %get-tuple-element.4), channel_id=1, replica_groups=mesh['x'=4,'zh'=4,'zl'=4,'c'=2,'head'=4] {'head'}, dimensions={0} | all-to-all | bytes 262144 | tf_op jit(solution)/shard_map/all_to_all | solution.py:145
  94.4 0.6 reduce_sum.35
  (9 shorter events, 0.1 us)
Async XLA Ops:
  49.3 30.3 %all-to-all-start.1 = ((bf16[4,16,2048]{2,1,0:T(8,128)(2,1)}), bf16[4,16,2048]{2,1,0:T(8,128)(2,1)S(1)}, u32[]{:S(2)}, u32[]{:S(2)}) async-start(bf16[4,16,2048]{2,1,0:T(8,128)(2,1)} %reduce_sum.33), calls=%async_computation.1 | async-start | bytes 524288 | tf_op jit(solution)/shard_map/all_to_all | solution.py:121

commit v14 on v13

--- a/solution.py
+++ b/solution.py
@@ -19,7 +19,8 @@
     return jnp.dot(a, b, precision=HI, preferred_element_type=jnp.float32)
 
 
-def mixer_kernel(acc_ref, tok_ref, s0_ref, gain_ref, w_hbm, new_ref, part_ref, w_vmem, mixed_scr, sem):
+def mixer_kernel(acc_ref, tok_ref, s0_hbm, gain_ref, w_hbm, new_hbm, part_ref,
+                 w_vmem, mixed_scr, s0_ref, new_ref, sem, s0_sem, new_sem):
     pieces = sem.shape[0]
     step = w_hbm.shape[0] // pieces
     w_copies = []
@@ -27,6 +28,10 @@
         rows = pl.ds(j * step, step)
         w_copies.append(pltpu.make_async_copy(w_hbm.at[rows], w_vmem.at[rows], sem.at[j]))
         w_copies[-1].start()
+    s0_copies = [pltpu.make_async_copy(s0_hbm.at[h], s0_ref.at[h], s0_sem.at[h])
+                 for h in range(s0_ref.shape[0])]
+    for copy in s0_copies:
+        copy.start()
     acc = acc_ref[0]
     blocks = tok_ref[...].astype(jnp.float32)
     heads = s0_ref.shape[0]
@@ -53,8 +58,10 @@
     w_t = kept_t * a_col * jnp.transpose(ba)
     gain = gain_ref[...]
     silu_g = g * (1.0 / (1.0 + jnp.exp(-g)))
+    new_copies = []
     for h in range(heads):
         lanes = slice(h * hd, (h + 1) * hd)
+        s0_copies[h].wait()
         s0 = s0_ref[h]
         v_h = v[:, lanes]
         qa_h = qa[:, lanes]
@@ -62,6 +69,8 @@
                                  precision=HI, preferred_element_type=jnp.float32)
         o_h = _dot(qa_h, s0) + _dot(scores * causal, v_h)
         new_ref[h] = a_col[lanes] * s0 + _dot(w_t[lanes], v_h)
+        new_copies.append(pltpu.make_async_copy(new_ref.at[h], new_hbm.at[h], new_sem.at[h]))
+        new_copies[-1].start()
         meansq = jnp.mean(o_h * o_h, axis=-1, keepdims=True)
         mixed = o_h * lax.rsqrt(meansq + norm_eps) * gain * silu_g[:, lanes]
         mixed_scr[:, lanes] = mixed.astype(mixed_scr.dtype)
@@ -72,22 +81,28 @@
     for j in range(part_ref.shape[0]):
         part_ref[j] = jnp.dot(mixed_all, w_vmem[:, j * chunk:(j + 1) * chunk],
                               preferred_element_type=jnp.float32)
+    for copy in new_copies:
+        copy.wait()
 
 
 def mixer(acc, tok, s0, gain, weight, parts):
     heads, hd = s0.shape[0], s0.shape[2]
     t_len = tok.shape[0]
     vmem = pl.BlockSpec(memory_space=pltpu.VMEM)
+    anywhere = pl.BlockSpec(memory_space=pl.ANY)
     return pl.pallas_call(
         mixer_kernel,
         out_shape=(jax.ShapeDtypeStruct(s0.shape, jnp.float32),
                    jax.ShapeDtypeStruct((parts, t_len, weight.shape[1] // parts), jnp.float32)),
-        in_specs=[pl.BlockSpec(memory_space=pltpu.SMEM), vmem, vmem, vmem,
-                  pl.BlockSpec(memory_space=pl.ANY)],
-        out_specs=(vmem, vmem),
+        in_specs=[pl.BlockSpec(memory_space=pltpu.SMEM), vmem, anywhere, vmem, anywhere],
+        out_specs=(anywhere, vmem),
         scratch_shapes=[pltpu.VMEM(weight.shape, weight.dtype),
                         pltpu.VMEM((t_len, heads * hd), jnp.bfloat16),
-                        pltpu.SemaphoreType.DMA((4,))],
+                        pltpu.VMEM(s0.shape, jnp.float32),
+                        pltpu.VMEM(s0.shape, jnp.float32),
+                        pltpu.SemaphoreType.DMA((4,)),
+                        pltpu.SemaphoreType.DMA((heads,)),
+                        pltpu.SemaphoreType.DMA((heads,))],
     )(acc, tok, s0, gain, weight)
 
 

time: 95.5 us -> 96.8 us (1.014)
  Pallas kernels: 3.57 us -> 4.83 us
    pallas_call x1, Pallas kernels: 3.57 us -> 4.83 us  [mixer(): pl.pallas_call(mixer_kernel, out_shape=(jax.ShapeDtypeStruct(s0.shape, jn...]
where the time goes in v14:
time: 96.8 us; the launch traced here: 96.2 us
  blocking collectives  55.5 us (57%)
  waiting for transfers between devices  17.3 us (18%)
  starting transfers between devices  12.4 us (13%)
  Pallas kernels  4.83 us (5%)
  other arithmetic  3.29 us (3%)
  between operations  2.01 us (2%)
    all_to_all x1, blocking collectives, route_two_stage(): got = lax.all_to_all(send, 'zl', 1, 1, tiled=False)  29.1 us
    all_to_all x1, waiting for transfers between devices, route_two_stage(): got = lax.all_to_all(part, 'zh', 0, 0, tiled=False)  17.3 us
    all_gather x1, blocking collectives, route_two_stage(): gathered = lax.all_gather(payload, ROW, axis=0, tiled=False)  15.9 us
    all_to_all x1, starting transfers between devices, route_two_stage(): got = lax.all_to_all(part, 'zh', 0, 0, tiled=False)  12.4 us
    all_to_all x1, blocking collectives, per_device(): swapped = lax.all_to_all(partial_out, 'head', 0, 0, tiled=True)  10.5 us
    pallas_call x1, Pallas kernels, mixer(): pl.pallas_call(mixer_kernel, out_shape=(jax.ShapeDtypeStruct(s0.shape, jn...  4.83 us
  transfers between devices with their start and end apart: 1, of which 1 were waited for; matrix products, arithmetic and copies ran while one was open for 0% of the time, Pallas kernels for 0%

profile of v14, /device:TPU:6, one launch (start us, length us, event | category | flops | bytes accessed | tf_op | source)
XLA Modules:
  0.0 96.2 jit_solution(6411478036022659429)
XLA Ops:
  1.3 0.8 select_select_fusion
  2.1 15.9 %all-gather = bf16[128,2176]{1,0:T(8,128)(2,1)S(1)} all-gather(bf16[16,2176]{1,0:T(8,128)(2,1)S(1)} %select_select_fusion), channel_id=2, replica_groups=mesh['x'=4,'zh'=4,'zl'=4,'c'=2,'head'=4] {'x','c'}, dimensions={0}, use_global_device_ids=true | all-gather | bytes 626688 | tf_op jit(solution)/shard_map/all_gather | solution.py:119
  18.1 0.1 copy.18
  18.2 0.1 select_reduce_fusion
  18.3 0.1 reduce_min.14
  18.4 0.6 gather_fusion
  19.1 0.1 broadcast_select_fusion
  19.2 0.1 copy.17
  19.3 29.1 %all_to_all.15 = bf16[4,4,16,2048]{3,2,0,1:T(8,128)(2,1)S(1)} all-to-all(bf16[4,4,16,2048]{3,2,0,1:T(8,128)(2,1)S(1)} %copy.17), channel_id=1, replica_groups=mesh['x'=4,'zh'=4,'zl'=4,'c'=2,'head'=4] {'zl'}, dimensions={1} | all-to-all | bytes 2097152 | tf_op jit(solution)/shard_map/all_to_all | solution.py:134
  48.4 0.9 reduce_sum.33
  49.3 12.4 %all-to-all-start.1 = ((bf16[4,16,2048]{2,1,0:T(8,128)(2,1)}), bf16[4,16,2048]{2,1,0:T(8,128)(2,1)S(1)}, u32[]{:S(2)}, u32[]{:S(2)}) async-start(bf16[4,16,2048]{2,1,0:T(8,128)(2,1)} %reduce_sum.33), calls=%async_computation.1 | async-start | bytes 524288 | tf_op jit(solution)/shard_map/all_to_all | solution.py:136
  62.4 17.3 %all-to-all-done.1 = bf16[4,16,2048]{2,1,0:T(8,128)(2,1)S(1)} async-done(((bf16[4,16,2048]{2,1,0:T(8,128)(2,1)}), bf16[4,16,2048]{2,1,0:T(8,128)(2,1)S(1)}, u32[]{:S(2)}, u32[]{:S(2)}) %all-to-all-start.1) | async-done | bytes 262176 | tf_op jit(solution)/shard_map/all_to_all | solution.py:136
  79.7 0.7 reduce_sum.34.tok_ref
  80.3 4.8 %shard_map.104 = (f32[4,128,128]{2,1,0:T(8,128)}, f32[4,16,512]{2,1,0:T(8,128)}) custom-call(s32[1]{0:T(128)S(6)} %copy.20.acc_ref, bf16[16,2048]{1,0:T(8,128)(2,1)} %reduce_sum.34.tok_ref, f32[4,128,128]{2,1,0:T(8,128)} %bitcast.22, f32[1,128]{1,0:T(1,128)} %bitcast.28, bf16[512,2048]{1,0:T(8,128)(2,1)} %w_hbm.1), custom_call_target="tpu_custom_call" | custom-call | tf_op jit(solution)/shard_map/pallas_call | solution.py:93
  85.2 10.5 %all_to_all.16 = f32[4,16,512]{2,1,0:T(8,128)S(1)} all-to-all(f32[4,16,512]{2,1,0:T(8,128)} %get-tuple-element.4), channel_id=1, replica_groups=mesh['x'=4,'zh'=4,'zl'=4,'c'=2,'head'=4] {'head'}, dimensions={0} | all-to-all | bytes 262144 | tf_op jit(solution)/shard_map/all_to_all | solution.py:160
  95.6 0.6 reduce_sum.35
  (9 shorter events, 0.1 us)
Async XLA Ops:
  49.3 30.3 %all-to-all-start.1 = ((bf16[4,16,2048]{2,1,0:T(8,128)(2,1)}), bf16[4,16,2048]{2,1,0:T(8,128)(2,1)S(1)}, u32[]{:S(2)}, u32[]{:S(2)}) async-start(bf16[4,16,2048]{2,1,0:T(8,128)(2,1)} %reduce_sum.33), calls=%async_computation.1 | async-start | bytes 524288 | tf_op jit(solution)/shard_map/all_to_all | solution.py:136

commit v15 on v13

--- a/solution.py
+++ b/solution.py
@@ -101,7 +101,13 @@
         placed = jnp.pad(t[0], ((0, 0), (i * width, total - (i + 1) * width)))
         inside = (lane >= i * width) & (lane < (i + 1) * width)
         payload = jnp.where(inside, placed, payload)
-    gathered = lax.all_gather(payload, ROW, axis=0, tiled=False)
+    zn_all = lax.axis_size("zh") * lax.axis_size("zl")
+    cn_all = lax.axis_size("c")
+    dest_col = (dealing[0] // (zn_all * cn_all)) * cn_all + dealing[0] % cn_all
+    group = lax.axis_size("x") * cn_all
+    pick = (jnp.arange(group, dtype=jnp.int32) == dest_col)[:, None, None]
+    send1 = jnp.where(pick, payload[None], jnp.zeros_like(payload)[None])
+    gathered = lax.all_to_all(send1, ROW, 0, 0, tiled=False)
     dest = gathered[:, 0, wide].astype(jnp.int32) - 1
     body = gathered[:, :, :wide]
     zh_n = lax.axis_size("zh")

time: 95.5 us -> 96.9 us (1.015)
  the two profiles are of different devices: /device:TPU:6 before, /device:TPU:64 now
where the time goes in v15:
time: 96.9 us; the launch traced here: 96.4 us
  blocking collectives  40 us (41%)
  waiting for transfers between devices  30.3 us (31%)
  starting transfers between devices  15.2 us (16%)
  other arithmetic  4.44 us (5%)
  Pallas kernels  3.57 us (4%)
  between operations  2.07 us (2%)
    all_to_all x1, blocking collectives, route_two_stage(): got = lax.all_to_all(send, 'zl', 1, 1, tiled=False)  29.6 us
    all_to_all x1, waiting for transfers between devices, route_two_stage(): got = lax.all_to_all(part, 'zh', 0, 0, tiled=False)  19.7 us
    all_to_all x1, starting transfers between devices, route_two_stage(): got = lax.all_to_all(part, 'zh', 0, 0, tiled=False)  10.9 us
    all_to_all x1, waiting for transfers between devices, route_two_stage(): gathered = lax.all_to_all(send1, ROW, 0, 0, tiled=False)  10.7 us
    all_to_all x1, blocking collectives, per_device(): swapped = lax.all_to_all(partial_out, 'head', 0, 0, tiled=True)  10.5 us
    all_to_all x1, starting transfers between devices, route_two_stage(): gathered = lax.all_to_all(send1, ROW, 0, 0, tiled=False)  4.3 us
    pallas_call x1, Pallas kernels, mixer(): pl.pallas_call(mixer_kernel, out_shape=(jax.ShapeDtypeStruct(s0.shape, jn...  3.57 us
  transfers between devices with their start and end apart: 2, of which 2 were waited for; matrix products, arithmetic and copies ran while one was open for 0% of the time, Pallas kernels for 0%

profile of v15, /device:TPU:64, one launch (start us, length us, event | category | flops | bytes accessed | tf_op | source)
XLA Modules:
  0.0 96.4 jit_solution(16942042240528255944)
XLA Ops:
  1.4 0.8 select_select_fusion
  2.2 0.9 broadcast_select_fusion.1
  3.1 4.3 %all-to-all-start = ((bf16[8,16,2176]{2,1,0:T(8,128)(2,1)}), bf16[8,16,2176]{2,1,0:T(8,128)(2,1)S(1)}, u32[]{:S(2)}, u32[]{:S(2)}) async-start(bf16[8,16,2176]{2,1,0:T(8,128)(2,1)} %broadcast_select_fusion.1), calls=%async_computation | async-start | bytes 1114112 | tf_op jit(solution)/shard_map/all_to_all | solution.py:110
  7.4 10.7 %all-to-all-done = bf16[8,16,2176]{2,1,0:T(8,128)(2,1)S(1)} async-done(((bf16[8,16,2176]{2,1,0:T(8,128)(2,1)}), bf16[8,16,2176]{2,1,0:T(8,128)(2,1)S(1)}, u32[]{:S(2)}, u32[]{:S(2)}) %all-to-all-start) | async-done | bytes 557088 | tf_op jit(solution)/shard_map/all_to_all | solution.py:110
  18.1 0.2 fusion.4
  18.3 0.1 select_reduce_fusion
  18.4 0.1 reduce_min.14
  18.6 0.6 gather_fusion
  19.2 0.1 broadcast_select_fusion
  19.3 0.1 copy.12
  19.4 29.6 %all_to_all.20 = bf16[4,4,16,2048]{3,2,0,1:T(8,128)(2,1)S(1)} all-to-all(bf16[4,4,16,2048]{3,2,0,1:T(8,128)(2,1)S(1)} %copy.12), channel_id=1, replica_groups=mesh['x'=4,'zh'=4,'zl'=4,'c'=2,'head'=4] {'zl'}, dimensions={1} | all-to-all | bytes 2097152 | tf_op jit(solution)/shard_map/all_to_all | solution.py:125
  49.0 0.9 reduce_sum.33
  49.9 10.9 %all-to-all-start.2 = ((bf16[4,16,2048]{2,1,0:T(8,128)(2,1)}), bf16[4,16,2048]{2,1,0:T(8,128)(2,1)S(1)}, u32[]{:S(2)}, u32[]{:S(2)}) async-start(bf16[4,16,2048]{2,1,0:T(8,128)(2,1)} %reduce_sum.33), calls=%async_computation.2 | async-start | bytes 524288 | tf_op jit(solution)/shard_map/all_to_all | solution.py:127
  61.4 19.7 %all-to-all-done.2 = bf16[4,16,2048]{2,1,0:T(8,128)(2,1)S(1)} async-done(((bf16[4,16,2048]{2,1,0:T(8,128)(2,1)}), bf16[4,16,2048]{2,1,0:T(8,128)(2,1)S(1)}, u32[]{:S(2)}, u32[]{:S(2)}) %all-to-all-start.2) | async-done | bytes 262176 | tf_op jit(solution)/shard_map/all_to_all | solution.py:127
  81.1 0.7 reduce_sum.34.tok_ref
  81.8 3.6 %shard_map.104 = (f32[4,128,128]{2,1,0:T(8,128)}, f32[4,16,512]{2,1,0:T(8,128)}) custom-call(s32[1]{0:T(128)S(6)} %copy.14.acc_ref, bf16[16,2048]{1,0:T(8,128)(2,1)} %reduce_sum.34.tok_ref, f32[4,128,128]{2,1,0:T(8,128)} %bitcast.22, f32[1,128]{1,0:T(1,128)} %bitcast.28, bf16[512,2048]{1,0:T(8,128)(2,1)} %w_hbm.1), custom_call_target="tpu_custom_call" | custom-call | tf_op jit(solution)/shard_map/pallas_call | solution.py:81
  85.3 10.5 %all_to_all.21 = f32[4,16,512]{2,1,0:T(8,128)S(1)} all-to-all(f32[4,16,512]{2,1,0:T(8,128)} %get-tuple-element.4), channel_id=1, replica_groups=mesh['x'=4,'zh'=4,'zl'=4,'c'=2,'head'=4] {'head'}, dimensions={0} | all-to-all | bytes 262144 | tf_op jit(solution)/shard_map/all_to_all | solution.py:151
  95.8 0.6 reduce_sum.35
  (8 shorter events, 0.1 us)
Async XLA Ops:
  3.1 15.0 %all-to-all-start = ((bf16[8,16,2176]{2,1,0:T(8,128)(2,1)}), bf16[8,16,2176]{2,1,0:T(8,128)(2,1)S(1)}, u32[]{:S(2)}, u32[]{:S(2)}) async-start(bf16[8,16,2176]{2,1,0:T(8,128)(2,1)} %broadcast_select_fusion.1), calls=%async_computation | async-start | bytes 1114112 | tf_op jit(solution)/shard_map/all_to_all | solution.py:110
  49.9 31.2 %all-to-all-start.2 = ((bf16[4,16,2048]{2,1,0:T(8,128)(2,1)}), bf16[4,16,2048]{2,1,0:T(8,128)(2,1)S(1)}, u32[]{:S(2)}, u32[]{:S(2)}) async-start(bf16[4,16,2048]{2,1,0:T(8,128)(2,1)} %reduce_sum.33), calls=%async_computation.2 | async-start | bytes 524288 | tf_op jit(solution)/shard_map/all_to_all | solution.py:127

commit v16 on v13

--- a/solution.py
+++ b/solution.py
@@ -8,7 +8,7 @@
 lower_bound = 0.8
 norm_eps = 1e-05
 
-ROW = ("x", "c")
+ROW = ("zl", "c")
 REQ = ("x", "zh", "zl", "c")
 
 
@@ -104,20 +104,22 @@
     gathered = lax.all_gather(payload, ROW, axis=0, tiled=False)
     dest = gathered[:, 0, wide].astype(jnp.int32) - 1
     body = gathered[:, :, :wide]
+    xn = lax.axis_size("x")
     zh_n = lax.axis_size("zh")
     zl_n = lax.axis_size("zl")
-    zn = zh_n * zl_n
-    my_x = lax.axis_index("x")
+    cn = lax.axis_size("c")
+    my_zl = lax.axis_index("zl")
     my_c = lax.axis_index("c")
-    cn = lax.axis_size("c")
-    target = (my_x * zn + jnp.arange(zn, dtype=jnp.int32)) * cn + my_c
+    xs = jnp.arange(xn, dtype=jnp.int32)[:, None]
+    zhs = jnp.arange(zh_n, dtype=jnp.int32)[None, :]
+    target = (((xs * zh_n + zhs) * zl_n + my_zl) * cn + my_c).reshape(-1)
     count = dest.shape[0]
     slots = jnp.arange(count, dtype=jnp.int32)
     idx = jnp.min(jnp.where(target[:, None] == dest[None, :], slots[None, :], count), axis=1)
     send = jnp.take(body, idx, axis=0, mode="fill", fill_value=0)
-    send = send.reshape((zh_n, zl_n) + send.shape[1:])
-    got = lax.all_to_all(send, "zl", 1, 1, tiled=False)
-    part = jnp.sum(got.astype(jnp.float32), axis=1).astype(jnp.bfloat16)
+    send = send.reshape((xn, zh_n) + send.shape[1:])
+    got = lax.all_to_all(send, "x", 0, 0, tiled=False)
+    part = jnp.sum(got.astype(jnp.float32), axis=0).astype(jnp.bfloat16)
     got = lax.all_to_all(part, "zh", 0, 0, tiled=False)
     return jnp.sum(got.astype(jnp.float32), axis=0).astype(jnp.bfloat16)
 

time: 95.5 us -> 87.9 us (0.920)
  the two profiles are of different devices: /device:TPU:6 before, /device:TPU:64 now
where the time goes in v16:
time: 87.9 us; the launch traced here: 87.4 us
  blocking collectives  46.5 us (53%)
  waiting for transfers between devices  20.2 us (23%)
  starting transfers between devices  10.8 us (12%)
  Pallas kernels  3.57 us (4%)
  other arithmetic  3.36 us (4%)
  between operations  2.01 us (2%)
  local copies, waits for them, and re-layouts  0.93 us (1%)
    all_to_all x1, waiting for transfers between devices, route_two_stage(): got = lax.all_to_all(part, 'zh', 0, 0, tiled=False)  20.2 us
    all_to_all x1, blocking collectives, route_two_stage(): got = lax.all_to_all(send, 'x', 0, 0, tiled=False)  18.3 us
    all_gather x1, blocking collectives, route_two_stage(): gathered = lax.all_gather(payload, ROW, axis=0, tiled=False)  17.7 us
    all_to_all x1, starting transfers between devices, route_two_stage(): got = lax.all_to_all(part, 'zh', 0, 0, tiled=False)  10.8 us
    all_to_all x1, blocking collectives, per_device(): swapped = lax.all_to_all(partial_out, 'head', 0, 0, tiled=True)  10.5 us
    pallas_call x1, Pallas kernels, mixer(): pl.pallas_call(mixer_kernel, out_shape=(jax.ShapeDtypeStruct(s0.shape, jn...  3.57 us
  transfers between devices with their start and end apart: 1, of which 1 were waited for; matrix products, arithmetic and copies ran while one was open for 0% of the time, Pallas kernels for 0%

profile of v16, /device:TPU:64, one launch (start us, length us, event | category | flops | bytes accessed | tf_op | source)
XLA Modules:
  0.0 87.4 jit_solution(15163321089065347939)
XLA Ops:
  1.3 0.8 select_select_fusion
  2.1 17.7 %all-gather = bf16[128,2176]{1,0:T(8,128)(2,1)S(1)} all-gather(bf16[16,2176]{1,0:T(8,128)(2,1)S(1)} %select_select_fusion), channel_id=2, replica_groups=mesh['x'=4,'zh'=4,'zl'=4,'c'=2,'head'=4] {'zl','c'}, dimensions={0}, use_global_device_ids=true | all-gather | bytes 626688 | tf_op jit(solution)/shard_map/all_gather | solution.py:104
  19.9 0.1 copy.13
  20.0 0.1 multiply_add_fusion
  20.1 0.1 reshape.81
  20.2 0.1 select_reduce_fusion
  20.3 0.1 reduce_min.14
  20.4 0.6 gather_fusion
  21.0 0.1 broadcast_select_fusion
  21.2 18.3 %all_to_all.15 = bf16[4,4,16,2048]{3,2,1,0:T(8,128)(2,1)S(1)} all-to-all(bf16[4,4,16,2048]{3,2,1,0:T(8,128)(2,1)S(1)} %broadcast_select_fusion), channel_id=1, replica_groups=mesh['x'=4,'zh'=4,'zl'=4,'c'=2,'head'=4] {'x'}, dimensions={0} | all-to-all | bytes 2097152 | tf_op jit(solution)/shard_map/all_to_all | solution.py:121
  39.5 0.9 %reduce_sum.33 = bf16[4,16,2048]{2,1,0:T(8,128)(2,1)} reduce(bf16[4,4,16,2048]{3,2,1,0:T(8,128)(2,1)S(1)} %all_to_all.15, bf16[]{:T(256)} %constant.46.clone.1), dimensions={0}, to_apply=%region_1.2 | reduce | flops 393216 | bytes 1310722 | tf_op jit(solution)/shard_map/reduce_sum | solution.py:122
  40.4 10.8 %all-to-all-start.1 = ((bf16[4,16,2048]{2,1,0:T(8,128)(2,1)}), bf16[4,16,2048]{2,1,0:T(8,128)(2,1)S(1)}, u32[]{:S(2)}, u32[]{:S(2)}) async-start(bf16[4,16,2048]{2,1,0:T(8,128)(2,1)} %reduce_sum.33), calls=%async_computation.1 | async-start | bytes 524288 | tf_op jit(solution)/shard_map/all_to_all | solution.py:123
  51.9 20.2 %all-to-all-done.1 = bf16[4,16,2048]{2,1,0:T(8,128)(2,1)S(1)} async-done(((bf16[4,16,2048]{2,1,0:T(8,128)(2,1)}), bf16[4,16,2048]{2,1,0:T(8,128)(2,1)S(1)}, u32[]{:S(2)}, u32[]{:S(2)}) %all-to-all-start.1) | async-done | bytes 262176 | tf_op jit(solution)/shard_map/all_to_all | solution.py:123
  72.1 0.7 reduce_sum.34.tok_ref
  72.8 3.6 %shard_map.104 = (f32[4,128,128]{2,1,0:T(8,128)}, f32[4,16,512]{2,1,0:T(8,128)}) custom-call(s32[1]{0:T(128)S(6)} %copy.15.acc_ref, bf16[16,2048]{1,0:T(8,128)(2,1)} %reduce_sum.34.tok_ref, f32[4,128,128]{2,1,0:T(8,128)} %bitcast.22, f32[1,128]{1,0:T(1,128)} %bitcast.28, bf16[512,2048]{1,0:T(8,128)(2,1)} %w_hbm.1), custom_call_target="tpu_custom_call" | custom-call | tf_op jit(solution)/shard_map/pallas_call | solution.py:81
  76.3 10.5 %all_to_all.16 = f32[4,16,512]{2,1,0:T(8,128)S(1)} all-to-all(f32[4,16,512]{2,1,0:T(8,128)} %get-tuple-element.4), channel_id=1, replica_groups=mesh['x'=4,'zh'=4,'zl'=4,'c'=2,'head'=4] {'head'}, dimensions={0} | all-to-all | bytes 262144 | tf_op jit(solution)/shard_map/all_to_all | solution.py:147
  86.8 0.6 reduce_sum.35
  (9 shorter events, 0.1 us)
Async XLA Ops:
  40.4 31.7 %all-to-all-start.1 = ((bf16[4,16,2048]{2,1,0:T(8,128)(2,1)}), bf16[4,16,2048]{2,1,0:T(8,128)(2,1)S(1)}, u32[]{:S(2)}, u32[]{:S(2)}) async-start(bf16[4,16,2048]{2,1,0:T(8,128)(2,1)} %reduce_sum.33), calls=%async_computation.1 | async-start | bytes 524288 | tf_op jit(solution)/shard_map/all_to_all | solution.py:123

commit v17 on v16

--- a/solution.py
+++ b/solution.py
@@ -8,7 +8,7 @@
 lower_bound = 0.8
 norm_eps = 1e-05
 
-ROW = ("zl", "c")
+ROW = ("zh", "c")
 REQ = ("x", "zh", "zl", "c")
 
 
@@ -108,19 +108,19 @@
     zh_n = lax.axis_size("zh")
     zl_n = lax.axis_size("zl")
     cn = lax.axis_size("c")
-    my_zl = lax.axis_index("zl")
+    my_zh = lax.axis_index("zh")
     my_c = lax.axis_index("c")
     xs = jnp.arange(xn, dtype=jnp.int32)[:, None]
-    zhs = jnp.arange(zh_n, dtype=jnp.int32)[None, :]
-    target = (((xs * zh_n + zhs) * zl_n + my_zl) * cn + my_c).reshape(-1)
+    zls = jnp.arange(zl_n, dtype=jnp.int32)[None, :]
+    target = (((xs * zh_n + my_zh) * zl_n + zls) * cn + my_c).reshape(-1)
     count = dest.shape[0]
     slots = jnp.arange(count, dtype=jnp.int32)
     idx = jnp.min(jnp.where(target[:, None] == dest[None, :], slots[None, :], count), axis=1)
     send = jnp.take(body, idx, axis=0, mode="fill", fill_value=0)
-    send = send.reshape((xn, zh_n) + send.shape[1:])
+    send = send.reshape((xn, zl_n) + send.shape[1:])
     got = lax.all_to_all(send, "x", 0, 0, tiled=False)
     part = jnp.sum(got.astype(jnp.float32), axis=0).astype(jnp.bfloat16)
-    got = lax.all_to_all(part, "zh", 0, 0, tiled=False)
+    got = lax.all_to_all(part, "zl", 0, 0, tiled=False)
     return jnp.sum(got.astype(jnp.float32), axis=0).astype(jnp.bfloat16)
 
 

time: 87.9 us -> 79.5 us (0.904)
  the two profiles are of different devices: /device:TPU:64 before, /device:TPU:6 now
where the time goes in v17:
time: 79.5 us; the launch traced here: 78.4 us
  blocking collectives  57.2 us (72%)
  waiting for transfers between devices  7.84 us (10%)
  Pallas kernels  3.57 us (4%)
  starting transfers between devices  3.41 us (4%)
  other arithmetic  3.37 us (4%)
  between operations  2 us (3%)
  local copies, waits for them, and re-layouts  0.93 us (1%)
    all_gather x1, blocking collectives, route_two_stage(): gathered = lax.all_gather(payload, ROW, axis=0, tiled=False)  28.7 us
    all_to_all x1, blocking collectives, route_two_stage(): got = lax.all_to_all(send, 'x', 0, 0, tiled=False)  18.1 us
    all_to_all x1, blocking collectives, per_device(): swapped = lax.all_to_all(partial_out, 'head', 0, 0, tiled=True)  10.5 us
    all_to_all x1, waiting for transfers between devices, route_two_stage(): got = lax.all_to_all(part, 'zl', 0, 0, tiled=False)  7.84 us
    pallas_call x1, Pallas kernels, mixer(): pl.pallas_call(mixer_kernel, out_shape=(jax.ShapeDtypeStruct(s0.shape, jn...  3.57 us
    all_to_all x1, starting transfers between devices, route_two_stage(): got = lax.all_to_all(part, 'zl', 0, 0, tiled=False)  3.41 us
  transfers between devices with their start and end apart: 1, of which 1 were waited for; matrix products, arithmetic and copies ran while one was open for 0% of the time, Pallas kernels for 0%

profile of v17, /device:TPU:6, one launch (start us, length us, event | category | flops | bytes accessed | tf_op | source)
XLA Modules:
  0.0 78.4 jit_solution(12012733471669869969)
XLA Ops:
  1.3 0.8 %select_select_fusion = bf16[16,2176]{1,0:T(8,128)(2,1)S(1)} fusion(bf16[16,512]{1,0:T(8,128)(2,1)} %bitcast.23, bf16[16,512]{1,0:T(8,128)(2,1)} %bitcast.24, bf16[16,512]{1,0:T(8,128)(2,1)} %bitcast.25, bf16[16,512]{1,0:T(8,128)(2,1)} %bitcast.26, pred[2176]{0:T(1024)(128)(4,1)S(1)} %get-tuple-element.6, pred[2176]{0:T(1024)(128)(4,1)S(1)} %get-tuple-element.9, ...), kind=kLoop, calls=%fused_computation.2 | loop fusion | flops 139264 | bytes 143874 | tf_op jit(solution)/shard_map/jit(_where)/select_n | solution.py:103
  2.1 28.7 %all-gather = bf16[128,2176]{1,0:T(8,128)(2,1)S(1)} all-gather(bf16[16,2176]{1,0:T(8,128)(2,1)S(1)} %select_select_fusion), channel_id=2, replica_groups=mesh['x'=4,'zh'=4,'zl'=4,'c'=2,'head'=4] {'zh','c'}, dimensions={0}, use_global_device_ids=true | all-gather | bytes 626688 | tf_op jit(solution)/shard_map/all_gather | solution.py:104
  30.9 0.1 copy.13
  31.0 0.1 multiply_add_fusion
  31.1 0.1 add.83
  31.2 0.1 select_reduce_fusion
  31.3 0.1 reduce_min.14
  31.4 0.6 gather_fusion
  32.0 0.1 broadcast_select_fusion
  32.1 18.1 %all_to_all.15 = bf16[4,4,16,2048]{3,2,1,0:T(8,128)(2,1)S(1)} all-to-all(bf16[4,4,16,2048]{3,2,1,0:T(8,128)(2,1)S(1)} %broadcast_select_fusion), channel_id=1, replica_groups=mesh['x'=4,'zh'=4,'zl'=4,'c'=2,'head'=4] {'x'}, dimensions={0} | all-to-all | bytes 2097152 | tf_op jit(solution)/shard_map/all_to_all | solution.py:121
  50.2 0.9 %reduce_sum.33 = bf16[4,16,2048]{2,1,0:T(8,128)(2,1)} reduce(bf16[4,4,16,2048]{3,2,1,0:T(8,128)(2,1)S(1)} %all_to_all.15, bf16[]{:T(256)} %constant.46.clone.1), dimensions={0}, to_apply=%region_1.2 | reduce | flops 393216 | bytes 1310722 | tf_op jit(solution)/shard_map/reduce_sum | solution.py:122
  51.2 3.4 %all-to-all-start.1 = ((bf16[4,16,2048]{2,1,0:T(8,128)(2,1)}), bf16[4,16,2048]{2,1,0:T(8,128)(2,1)S(1)}, u32[]{:S(2)}, u32[]{:S(2)}) async-start(bf16[4,16,2048]{2,1,0:T(8,128)(2,1)} %reduce_sum.33), calls=%async_computation.1 | async-start | bytes 524288 | tf_op jit(solution)/shard_map/all_to_all | solution.py:123
  55.2 7.8 %all-to-all-done.1 = bf16[4,16,2048]{2,1,0:T(8,128)(2,1)S(1)} async-done(((bf16[4,16,2048]{2,1,0:T(8,128)(2,1)}), bf16[4,16,2048]{2,1,0:T(8,128)(2,1)S(1)}, u32[]{:S(2)}, u32[]{:S(2)}) %all-to-all-start.1) | async-done | bytes 262176 | tf_op jit(solution)/shard_map/all_to_all | solution.py:123
  63.1 0.7 reduce_sum.34.tok_ref
  63.7 3.6 %shard_map.104 = (f32[4,128,128]{2,1,0:T(8,128)}, f32[4,16,512]{2,1,0:T(8,128)}) custom-call(s32[1]{0:T(128)S(6)} %copy.15.acc_ref, bf16[16,2048]{1,0:T(8,128)(2,1)} %reduce_sum.34.tok_ref, f32[4,128,128]{2,1,0:T(8,128)} %bitcast.22, f32[1,128]{1,0:T(1,128)} %bitcast.28, bf16[512,2048]{1,0:T(8,128)(2,1)} %w_hbm.1), custom_call_target="tpu_custom_call" | custom-call | tf_op jit(solution)/shard_map/pallas_call | solution.py:81
  67.3 10.5 %all_to_all.16 = f32[4,16,512]{2,1,0:T(8,128)S(1)} all-to-all(f32[4,16,512]{2,1,0:T(8,128)} %get-tuple-element.4), channel_id=1, replica_groups=mesh['x'=4,'zh'=4,'zl'=4,'c'=2,'head'=4] {'head'}, dimensions={0} | all-to-all | bytes 262144 | tf_op jit(solution)/shard_map/all_to_all | solution.py:147
  77.8 0.6 reduce_sum.35
  (9 shorter events, 0.1 us)
Async XLA Ops:
  51.2 11.9 %all-to-all-start.1 = ((bf16[4,16,2048]{2,1,0:T(8,128)(2,1)}), bf16[4,16,2048]{2,1,0:T(8,128)(2,1)S(1)}, u32[]{:S(2)}, u32[]{:S(2)}) async-start(bf16[4,16,2048]{2,1,0:T(8,128)(2,1)} %reduce_sum.33), calls=%async_computation.1 | async-start | bytes 524288 | tf_op jit(solution)/shard_map/all_to_all | solution.py:123

commit v18 on v17

--- a/solution.py
+++ b/solution.py
@@ -101,7 +101,9 @@
         placed = jnp.pad(t[0], ((0, 0), (i * width, total - (i + 1) * width)))
         inside = (lane >= i * width) & (lane < (i + 1) * width)
         payload = jnp.where(inside, placed, payload)
-    gathered = lax.all_gather(payload, ROW, axis=0, tiled=False)
+    far = lax.all_gather(payload, "zh", axis=0, tiled=False)
+    near = lax.ppermute(far, "c", [(0, 1), (1, 0)])
+    gathered = jnp.concatenate([far, near], axis=0)
     dest = gathered[:, 0, wide].astype(jnp.int32) - 1
     body = gathered[:, :, :wide]
     xn = lax.axis_size("x")

time: 79.5 us -> 81.5 us (1.025)
  starting transfers between devices: 3.41 us -> 5.32 us
  blocking collectives: 57.2 us -> 56.2 us
  waiting for transfers between devices: 7.84 us -> 8.84 us
    ppermute x0 -> x1, starting transfers between devices: none -> 1.91 us  [route_two_stage(): near = lax.ppermute(far, 'c', [(0, 1), (1, 0)])]
    ppermute x0 -> x1, waiting for transfers between devices: none -> 1.34 us  [route_two_stage(): near = lax.ppermute(far, 'c', [(0, 1), (1, 0)])]
    all_gather x1, blocking collectives: 28.7 us -> 27.8 us  [route_two_stage(): far = lax.all_gather(payload, 'zh', axis=0, tiled=False)]
  transfers between devices with their start and end apart: 1 -> 2, of which waited for: 1 -> 2; matrix products, arithmetic and copies ran while one was open for 0% -> 0% of each run, Pallas kernels for 0% -> 0%
where the time goes in v18:
time: 81.5 us; the launch traced here: 80.4 us
  blocking collectives  56.2 us (69%)
  waiting for transfers between devices  8.84 us (11%)
  starting transfers between devices  5.32 us (7%)
  other arithmetic  3.64 us (4%)
  Pallas kernels  3.57 us (4%)
  between operations  2.02 us (2%)
    all_gather x1, blocking collectives, route_two_stage(): far = lax.all_gather(payload, 'zh', axis=0, tiled=False)  27.8 us
    all_to_all x1, blocking collectives, route_two_stage(): got = lax.all_to_all(send, 'x', 0, 0, tiled=False)  17.9 us
    all_to_all x1, blocking collectives, per_device(): swapped = lax.all_to_all(partial_out, 'head', 0, 0, tiled=True)  10.5 us
    all_to_all x1, waiting for transfers between devices, route_two_stage(): got = lax.all_to_all(part, 'zl', 0, 0, tiled=False)  7.5 us
    pallas_call x1, Pallas kernels, mixer(): pl.pallas_call(mixer_kernel, out_shape=(jax.ShapeDtypeStruct(s0.shape, jn...  3.57 us
    all_to_all x1, starting transfers between devices, route_two_stage(): got = lax.all_to_all(part, 'zl', 0, 0, tiled=False)  3.41 us
    ppermute x1, starting transfers between devices, route_two_stage(): near = lax.ppermute(far, 'c', [(0, 1), (1, 0)])  1.91 us
  transfers between devices with their start and end apart: 2, of which 2 were waited for; matrix products, arithmetic and copies ran while one was open for 0% of the time, Pallas kernels for 0%

profile of v18, /device:TPU:6, one launch (start us, length us, event | category | flops | bytes accessed | tf_op | source)
XLA Modules:
  0.0 80.4 jit_solution(8202777052244010815)
XLA Ops:
  1.3 0.8 %select_select_fusion = bf16[16,2176]{1,0:T(8,128)(2,1)S(1)} fusion(bf16[16,512]{1,0:T(8,128)(2,1)} %bitcast.22, bf16[16,512]{1,0:T(8,128)(2,1)} %bitcast.23, bf16[16,512]{1,0:T(8,128)(2,1)} %bitcast.24, bf16[16,512]{1,0:T(8,128)(2,1)} %bitcast.25, pred[2176]{0:T(1024)(128)(4,1)S(1)} %get-tuple-element.6, pred[2176]{0:T(1024)(128)(4,1)S(1)} %get-tuple-element.9, ...), kind=kLoop, calls=%fused_computation.3 | loop fusion | flops 139264 | bytes 143874 | tf_op jit(solution)/shard_map/jit(_where)/select_n | solution.py:103
  2.1 27.8 %all-gather = bf16[64,2176]{1,0:T(8,128)(2,1)S(1)} all-gather(bf16[16,2176]{1,0:T(8,128)(2,1)S(1)} %select_select_fusion), channel_id=2, replica_groups=mesh['x'=4,'zh'=4,'zl'=4,'c'=2,'head'=4] {'zh'}, dimensions={0}, use_global_device_ids=true | all-gather | bytes 348160 | tf_op jit(solution)/shard_map/all_gather | solution.py:104
  30.0 1.9 %collective-permute-start = (bf16[4,16,2176]{2,1,0:T(8,128)(2,1)S(1)}, bf16[4,16,2176]{2,1,0:T(8,128)(2,1)S(1)}, u32[]{:S(2)}, u32[]{:S(2)}) collective-permute-start(bf16[4,16,2176]{2,1,0:T(8,128)(2,1)S(1)} %bitcast.18), channel_id=1, source_target_pairs={{0,4},{4,0},{1,5},{5,1},{2,6},{6,2},{3,7},{7,3},{8,12},{12,8},{9,1... | collective-permute-start | bytes 835592 | tf_op jit(solution)/shard_map/ppermute | solution.py:105
  31.9 0.1 multiply_add_fusion
  32.0 0.1 add.83
  32.1 1.3 %collective-permute-done = bf16[4,16,2176]{2,1,0:T(8,128)(2,1)S(1)} collective-permute-done((bf16[4,16,2176]{2,1,0:T(8,128)(2,1)S(1)}, bf16[4,16,2176]{2,1,0:T(8,128)(2,1)S(1)}, u32[]{:S(2)}, u32[]{:S(2)}) %collective-permute-start) | collective-permute-done | bytes 278560 | tf_op jit(solution)/shard_map/ppermute | solution.py:105
  33.4 0.2 fusion.4
  33.6 0.1 select_reduce_fusion
  33.7 0.1 reduce_min.14
  33.9 0.6 gather_fusion
  34.5 0.1 broadcast_select_fusion
  34.7 17.9 %all_to_all.15 = bf16[4,4,16,2048]{3,2,1,0:T(8,128)(2,1)S(1)} all-to-all(bf16[4,4,16,2048]{3,2,1,0:T(8,128)(2,1)S(1)} %broadcast_select_fusion), channel_id=1, replica_groups=mesh['x'=4,'zh'=4,'zl'=4,'c'=2,'head'=4] {'x'}, dimensions={0} | all-to-all | bytes 2097152 | tf_op jit(solution)/shard_map/all_to_all | solution.py:123
  52.6 0.9 %reduce_sum.33 = bf16[4,16,2048]{2,1,0:T(8,128)(2,1)} reduce(bf16[4,4,16,2048]{3,2,1,0:T(8,128)(2,1)S(1)} %all_to_all.15, bf16[]{:T(256)} %constant.46.clone.1), dimensions={0}, to_apply=%region_1.2 | reduce | flops 393216 | bytes 1310722 | tf_op jit(solution)/shard_map/reduce_sum | solution.py:124
  53.5 3.4 %all-to-all-start.1 = ((bf16[4,16,2048]{2,1,0:T(8,128)(2,1)}), bf16[4,16,2048]{2,1,0:T(8,128)(2,1)S(1)}, u32[]{:S(2)}, u32[]{:S(2)}) async-start(bf16[4,16,2048]{2,1,0:T(8,128)(2,1)} %reduce_sum.33), calls=%async_computation.1 | async-start | bytes 524288 | tf_op jit(solution)/shard_map/all_to_all | solution.py:125
  57.6 7.5 %all-to-all-done.1 = bf16[4,16,2048]{2,1,0:T(8,128)(2,1)S(1)} async-done(((bf16[4,16,2048]{2,1,0:T(8,128)(2,1)}), bf16[4,16,2048]{2,1,0:T(8,128)(2,1)S(1)}, u32[]{:S(2)}, u32[]{:S(2)}) %all-to-all-start.1) | async-done | bytes 262176 | tf_op jit(solution)/shard_map/all_to_all | solution.py:125
  65.1 0.7 reduce_sum.34.tok_ref
  65.7 3.6 %shard_map.104 = (f32[4,128,128]{2,1,0:T(8,128)}, f32[4,16,512]{2,1,0:T(8,128)}) custom-call(s32[1]{0:T(128)S(6)} %copy.14.acc_ref, bf16[16,2048]{1,0:T(8,128)(2,1)} %reduce_sum.34.tok_ref, f32[4,128,128]{2,1,0:T(8,128)} %bitcast.21, f32[1,128]{1,0:T(1,128)} %bitcast.27, bf16[512,2048]{1,0:T(8,128)(2,1)} %w_hbm.1), custom_call_target="tpu_custom_call" | custom-call | tf_op jit(solution)/shard_map/pallas_call | solution.py:81
  69.3 10.5 %all_to_all.16 = f32[4,16,512]{2,1,0:T(8,128)S(1)} all-to-all(f32[4,16,512]{2,1,0:T(8,128)} %get-tuple-element.4), channel_id=1, replica_groups=mesh['x'=4,'zh'=4,'zl'=4,'c'=2,'head'=4] {'head'}, dimensions={0} | all-to-all | bytes 262144 | tf_op jit(solution)/shard_map/all_to_all | solution.py:149
  79.7 0.6 reduce_sum.35
  (7 shorter events, 0.1 us)
Async XLA Ops:
  30.0 3.4 %collective-permute-start = (bf16[4,16,2176]{2,1,0:T(8,128)(2,1)S(1)}, bf16[4,16,2176]{2,1,0:T(8,128)(2,1)S(1)}, u32[]{:S(2)}, u32[]{:S(2)}) collective-permute-start(bf16[4,16,2176]{2,1,0:T(8,128)(2,1)S(1)} %bitcast.18), channel_id=1, source_target_pairs={{0,4},{4,0},{1,5},{5,1},{2,6},{6,2},{3,7},{7,3},{8,12},{12,8},{9,1... | collective-permute-start | bytes 835592 | tf_op jit(solution)/shard_map/ppermute | solution.py:105
  53.5 11.6 %all-to-all-start.1 = ((bf16[4,16,2048]{2,1,0:T(8,128)(2,1)}), bf16[4,16,2048]{2,1,0:T(8,128)(2,1)S(1)}, u32[]{:S(2)}, u32[]{:S(2)}) async-start(bf16[4,16,2048]{2,1,0:T(8,128)(2,1)} %reduce_sum.33), calls=%async_computation.1 | async-start | bytes 524288 | tf_op jit(solution)/shard_map/all_to_all | solution.py:125

commit v19 on v17

--- a/solution.py
+++ b/solution.py
@@ -8,7 +8,7 @@
 lower_bound = 0.8
 norm_eps = 1e-05
 
-ROW = ("zh", "c")
+ROW = ("c", "zh")
 REQ = ("x", "zh", "zl", "c")
 
 

time: 79.5 us -> 99.7 us (1.25)
  blocking collectives: 57.2 us -> 76.4 us
  starting transfers between devices: 3.41 us -> 4.7 us
    all_gather x1, blocking collectives: 28.7 us -> 48.4 us  [route_two_stage(): gathered = lax.all_gather(payload, ROW, axis=0, tiled=False)]
    all_to_all x1, starting transfers between devices: 3.41 us -> 4.7 us  [route_two_stage(): got = lax.all_to_all(part, 'zl', 0, 0, tiled=False)]
where the time goes in v19:
time: 99.7 us; the launch traced here: 98.6 us
  blocking collectives  76.4 us (77%)
  waiting for transfers between devices  7.65 us (8%)
  starting transfers between devices  4.7 us (5%)
  Pallas kernels  3.57 us (4%)
  other arithmetic  3.37 us (3%)
  between operations  2 us (2%)
    all_gather x1, blocking collectives, route_two_stage(): gathered = lax.all_gather(payload, ROW, axis=0, tiled=False)  48.4 us
    all_to_all x1, blocking collectives, route_two_stage(): got = lax.all_to_all(send, 'x', 0, 0, tiled=False)  17.5 us
    all_to_all x1, blocking collectives, per_device(): swapped = lax.all_to_all(partial_out, 'head', 0, 0, tiled=True)  10.5 us
    all_to_all x1, waiting for transfers between devices, route_two_stage(): got = lax.all_to_all(part, 'zl', 0, 0, tiled=False)  7.65 us
    all_to_all x1, starting transfers between devices, route_two_stage(): got = lax.all_to_all(part, 'zl', 0, 0, tiled=False)  4.7 us
    pallas_call x1, Pallas kernels, mixer(): pl.pallas_call(mixer_kernel, out_shape=(jax.ShapeDtypeStruct(s0.shape, jn...  3.57 us
  transfers between devices with their start and end apart: 1, of which 1 were waited for; matrix products, arithmetic and copies ran while one was open for 0% of the time, Pallas kernels for 0%

profile of v19, /device:TPU:6, one launch (start us, length us, event | category | flops | bytes accessed | tf_op | source)
XLA Modules:
  0.0 98.6 jit_solution(17672024776709325250)
XLA Ops:
  1.3 0.8 select_select_fusion
  2.1 48.4 %all-gather = bf16[128,2176]{1,0:T(8,128)(2,1)S(1)} all-gather(bf16[16,2176]{1,0:T(8,128)(2,1)S(1)} %select_select_fusion), channel_id=2, replica_groups=mesh['x'=4,'zh'=4,'zl'=4,'c'=2,'head'=4] {'c','zh'}, dimensions={0}, use_global_device_ids=true | all-gather | bytes 626688 | tf_op jit(solution)/shard_map/all_gather | solution.py:104
  50.6 0.1 copy.13
  50.7 0.1 multiply_add_fusion
  50.8 0.1 add.83
  50.9 0.1 select_reduce_fusion
  51.0 0.1 reduce_min.14
  51.1 0.6 gather_fusion
  51.7 0.1 broadcast_select_fusion
  51.9 17.5 %all_to_all.15 = bf16[4,4,16,2048]{3,2,1,0:T(8,128)(2,1)S(1)} all-to-all(bf16[4,4,16,2048]{3,2,1,0:T(8,128)(2,1)S(1)} %broadcast_select_fusion), channel_id=1, replica_groups=mesh['x'=4,'zh'=4,'zl'=4,'c'=2,'head'=4] {'x'}, dimensions={0} | all-to-all | bytes 2097152 | tf_op jit(solution)/shard_map/all_to_all | solution.py:121
  69.4 0.9 reduce_sum.33
  70.3 4.7 %all-to-all-start.1 = ((bf16[4,16,2048]{2,1,0:T(8,128)(2,1)}), bf16[4,16,2048]{2,1,0:T(8,128)(2,1)S(1)}, u32[]{:S(2)}, u32[]{:S(2)}) async-start(bf16[4,16,2048]{2,1,0:T(8,128)(2,1)} %reduce_sum.33), calls=%async_computation.1 | async-start | bytes 524288 | tf_op jit(solution)/shard_map/all_to_all | solution.py:123
  75.7 7.7 %all-to-all-done.1 = bf16[4,16,2048]{2,1,0:T(8,128)(2,1)S(1)} async-done(((bf16[4,16,2048]{2,1,0:T(8,128)(2,1)}), bf16[4,16,2048]{2,1,0:T(8,128)(2,1)S(1)}, u32[]{:S(2)}, u32[]{:S(2)}) %all-to-all-start.1) | async-done | bytes 262176 | tf_op jit(solution)/shard_map/all_to_all | solution.py:123
  83.3 0.7 reduce_sum.34.tok_ref
  84.0 3.6 %shard_map.104 = (f32[4,128,128]{2,1,0:T(8,128)}, f32[4,16,512]{2,1,0:T(8,128)}) custom-call(s32[1]{0:T(128)S(6)} %copy.15.acc_ref, bf16[16,2048]{1,0:T(8,128)(2,1)} %reduce_sum.34.tok_ref, f32[4,128,128]{2,1,0:T(8,128)} %bitcast.22, f32[1,128]{1,0:T(1,128)} %bitcast.28, bf16[512,2048]{1,0:T(8,128)(2,1)} %w_hbm.1), custom_call_target="tpu_custom_call" | custom-call | tf_op jit(solution)/shard_map/pallas_call | solution.py:81
  87.5 10.5 %all_to_all.16 = f32[4,16,512]{2,1,0:T(8,128)S(1)} all-to-all(f32[4,16,512]{2,1,0:T(8,128)} %get-tuple-element.4), channel_id=1, replica_groups=mesh['x'=4,'zh'=4,'zl'=4,'c'=2,'head'=4] {'head'}, dimensions={0} | all-to-all | bytes 262144 | tf_op jit(solution)/shard_map/all_to_all | solution.py:147
  98.0 0.6 reduce_sum.35
  (9 shorter events, 0.1 us)
Async XLA Ops:
  70.3 13.0 %all-to-all-start.1 = ((bf16[4,16,2048]{2,1,0:T(8,128)(2,1)}), bf16[4,16,2048]{2,1,0:T(8,128)(2,1)S(1)}, u32[]{:S(2)}, u32[]{:S(2)}) async-start(bf16[4,16,2048]{2,1,0:T(8,128)(2,1)} %reduce_sum.33), calls=%async_computation.1 | async-start | bytes 524288 | tf_op jit(solution)/shard_map/all_to_all | solution.py:123
